TPU v7x, 256 devices: a whole 4x4x8 slice. The times are simulated.
256 devices in a mesh: rot: 8 (over x_hi, y), space: 32 (over x_lo, z, core).
Axes of the slice: x: 4 (x_hi: 2, x_lo: 2; x = x_hi * 2 + x_lo), y: 4, z: 8, core: 2. Of those that a mesh axis runs over, the one named last changes fastest.
Arguments:
- raster: bfloat16 [4, 512, 2, 256], P(None, 'space'), may hold values from -6 to 6
- coarse_features: bfloat16 [8, 64, 512, 2, 256], P('rot', None, 'space'), may hold values from -6 to 6
- lift_weight: bfloat16 [8, 9, 64, 4], P('rot'), may hold values from -1 to 1
- lift_bias: float32 [64], replicated, may hold values from -3 to 3
- group_weight: bfloat16 [8, 9, 64, 64], P('rot'), may hold values from -0.09375 to 0.09375
- group_bias: float32 [64], replicated, may hold values from -3 to 3
Outputs:
- features: bfloat16 [8, 64, 512, 2, 256], P('rot', None, 'space')
All inputs are finite; a program needn't handle non-finite values.
Results may differ from a plain program's by a relative error of at most 0.0045.
Values may be sent and summed in bfloat16 or wider, within the bound.
No kernel may reach another device: no remote copies, remote signals or barrier semaphores. Data moves between devices by JAX's collectives and lax.ppermute only.
A program may use at most 192 MiB of HBM per device.

v0:
```python
import jax
import jax.numpy as jnp
from jax import lax
from jax.experimental import pallas as pl
from jax.experimental.pallas import tpu as pltpu
from jax.sharding import PartitionSpec as P


def padded_rows(array, axis, dim, width):
    size, length = lax.axis_size(axis), array.shape[dim]
    up = [(i, i + 1) for i in range(size - 1)]
    down = [(j, i) for i, j in up]
    last = lax.slice_in_dim(array, length - width, length, axis=dim)
    leading = lax.slice_in_dim(array, 0, width, axis=dim)
    before = lax.ppermute(last, axis, up)
    after = lax.ppermute(leading, axis, down)
    return jnp.concatenate([before, array, after], axis=dim)


def conv_rows_valid(images, kernel):
    return lax.conv_general_dilated(
        images,
        kernel,
        (1, 1),
        ((0, 0), (1, 1)),
        dimension_numbers=("CHNW", "HWOI", "CHNW"),
        preferred_element_type=jnp.float32,
    )


def bank_kernel(pairs_ref, bank_ref):
    count, _, channels, lanes = pairs_ref.shape
    for g in range(count):
        for p in range(bank_ref.shape[2] // lanes):
            bank_ref[:, g * channels : (g + 1) * channels, p * lanes : (p + 1) * lanes] = pairs_ref[
                (g - 2 * p) % count
            ]


def circulant_bank(filters):
    count, taps, channels, _ = filters.shape
    pairs = jnp.concatenate([filters, jnp.roll(filters, 1, axis=0)], axis=-1)
    return pl.pallas_call(
        bank_kernel,
        out_shape=jax.ShapeDtypeStruct((taps, count * channels, count * channels), filters.dtype),
    )(pairs)


def mixing_kernel(bank_ref, bias_ref, x_ref, o_ref):
    row, tile = pl.program_id(0), pl.program_id(1)
    count, channels, cols = x_ref.shape[0], x_ref.shape[3], x_ref.shape[4]
    planes = [
        jnp.concatenate([x_ref[h, row + dy, tile] for h in range(count)], axis=0) for dy in range(3)
    ]
    sums = []
    for dx in range(3):
        total = None
        for dy in range(3):
            term = jnp.dot(bank_ref[3 * dy + dx], planes[dy], preferred_element_type=jnp.float32)
            total = term if total is None else total + term
        sums.append(total)
    column = lax.broadcasted_iota(jnp.int32, sums[0].shape, 1)
    left = jnp.where(column == 0, 0.0, pltpu.roll(sums[0], 1, 1))
    right = jnp.where(column == cols - 1, 0.0, pltpu.roll(sums[2], cols - 1, 1))
    mixed = sums[1] + left + right + bias_ref[...]
    mixed = jnp.maximum(mixed, 0.0).astype(o_ref.dtype)
    for g in range(count):
        o_ref[g, 0, 0] = mixed[g * channels : (g + 1) * channels]


def group_mix(bank, bias, windows):
    count, rows_in, tiles, channels, cols = windows.shape
    rows_out = rows_in - 2
    full = count * channels
    return pl.pallas_call(
        mixing_kernel,
        grid=(rows_out, tiles),
        in_specs=[
            pl.BlockSpec((9, full, full), lambda r, t: (0, 0, 0)),
            pl.BlockSpec((full, 1), lambda r, t: (0, 0)),
            pl.BlockSpec(windows.shape, lambda r, t: (0, 0, 0, 0, 0)),
        ],
        out_specs=pl.BlockSpec((count, 1, 1, channels, cols), lambda r, t: (0, r, t, 0, 0)),
        out_shape=jax.ShapeDtypeStruct((count, rows_out, tiles, channels, cols), jnp.bfloat16),
        compiler_params=pltpu.CompilerParams(vmem_limit_bytes=48 * 1024 * 1024),
    )(bank, bias, windows)


def shards(raster, coarse_features, lift_weight, lift_bias, group_weight, group_bias):
    n = lax.axis_size("rot")
    channels = lift_weight.shape[2]
    rows = raster.shape[1]
    chunk = rows // n

    raster_padded = padded_rows(raster, "space", 1, 1)
    lift_kernel = lift_weight[0].reshape(3, 3, channels, -1)
    lifted = conv_rows_valid(raster_padded, lift_kernel)
    lifted = lifted + lift_bias[:, None, None, None] + coarse_features[0].astype(jnp.float32)
    hidden = jnp.maximum(lifted, 0.0).astype(jnp.bfloat16)

    hidden_ext = jnp.transpose(padded_rows(hidden, "space", 1, 1), (1, 2, 0, 3))
    split = (n, chunk) + hidden_ext.shape[1:]
    top = lax.slice_in_dim(hidden_ext, 0, rows, axis=0).reshape(split)
    bottom = lax.slice_in_dim(hidden_ext, 2, rows + 2, axis=0).reshape(split)
    windows = jnp.concatenate([top, lax.slice_in_dim(bottom, chunk - 2, chunk, axis=1)], axis=1)
    gathered = lax.all_to_all(windows, "rot", 0, 0)

    spread = jnp.broadcast_to(group_weight, (n,) + group_weight.shape[1:])
    filters = lax.all_to_all(spread, "rot", 0, 0)
    bias = jnp.tile(group_bias, n)[:, None]
    mixed = group_mix(circulant_bank(filters), bias, gathered)

    returned = lax.all_to_all(mixed, "rot", 0, 0)
    result = jnp.transpose(returned, (3, 0, 1, 2, 4)).reshape((channels, rows) + returned.shape[2:3] + returned.shape[4:])
    return result[None]


def solution(mesh):
    return jax.shard_map(
        shards,
        mesh=mesh,
        in_specs=(
            P(None, "space", None, None),
            P("rot", None, "space", None, None),
            P("rot", None, None, None),
            P(),
            P("rot", None, None, None),
            P(),
        ),
        out_specs=P("rot", None, "space", None, None),
        check_vma=False,
    )
```

profile of v0, /device:TPU:96, one launch (start us, length us, event | category | flops | bytes accessed | tf_op | source)
XLA Modules:
  0.0 128.1 jit_solution(11532245771894654123)
XLA Ops:
  0.0 0.0 copy-start
  0.0 0.0 copy-start.1
  0.0 0.8 fusion.8
  0.8 0.2 copy.31
  1.0 1.9 %collective-permute-start = (bf16[4,1,2,256]{0,2,3,1:T(2,128)(2,1)S(1)}, bf16[4,1,2,256]{0,2,3,1:T(2,128)(2,1)S(1)}, u32[]{:S(2)}, u32[]{:S(2)}) collective-permute-start(bf16[4,1,2,256]{0,2,3,1:T(2,128)(2,1)S(1)} %copy.31), channel_id=1, source_target_pairs={{0,1},{1,2},{2,3},{3,4},{4,5},{5,6},{6,7},{7,8},{8,9},{9,10},{10,1... | collective-permute-start | bytes 12296 | tf_op jit(solution)/shard_map/ppermute | solution.py:15
  2.9 0.2 copy.32
  3.1 0.0 copy-start.4
  3.1 3.6 %collective-permute-start.1 = (bf16[4,1,2,256]{0,2,3,1:T(2,128)(2,1)S(1)}, bf16[4,1,2,256]{0,2,3,1:T(2,128)(2,1)S(1)}, u32[]{:S(2)}, u32[]{:S(2)}) collective-permute-start(bf16[4,1,2,256]{0,2,3,1:T(2,128)(2,1)S(1)} %copy.32), channel_id=1, source_target_pairs={{1,0},{2,1},{3,2},{4,3},{5,4},{6,5},{7,6},{8,7},{9,8},{10,9},{11,1... | collective-permute-start | bytes 12296 | tf_op jit(solution)/shard_map/ppermute | solution.py:16
  6.8 5.2 %copy.33 = bf16[4,16,2,256]{0,2,3,1:T(2,128)(2,1)} copy(bf16[4,16,2,256]{3,2,1,0:T(2,128)(2,1)} %param.6) | data formatting | bytes 131072 | tf_op args[0]
  12.0 0.0 copy-done.1
  12.0 4.0 %copy.34 = bf16[1,64,16,2,256]{1,3,4,2,0:T(2,128)(2,1)} copy(bf16[1,64,16,2,256]{4,3,2,1,0:T(2,128)(2,1)S(1)} %copy-done.1) | data formatting | bytes 2097152 | tf_op args[1]
  15.9 0.0 collective-permute-done
  15.9 0.0 collective-permute-done.1
  15.9 0.0 copy-done
  15.9 0.0 copy-done.4
  15.9 0.0 copy-start.2
  16.0 10.8 %fusion.1 = bf16[64,16,2,256]{0,2,3,1:T(2,128)(2,1)S(1)} fusion(bf16[3,3,64,4]{2,3,1,0:T(4,128)(2,1)S(1)} %bitcast.13, bf16[4,1,2,256]{0,2,3,1:T(2,128)(2,1)S(1)} %collective-permute-done.1, bf16[4,16,2,256]{0,2,3,1:T(2,128)(2,1)} %copy.33, bf16[4,1,2,256]{0,2,3,1:T(2,128)(2,1)S(1)} %collective-permute-done, bf16[1,64,16,2,256]{1,3,4,2,0:T(2,128)(2,1)} %copy.34, ...), kind=kOutput, calls=%fused_computation.2 | convolution fusion | flops 40493056 | bytes 2175744 | tf_op jit(solution)/shard_map/conv_general_dilated | solution.py:21
  26.7 0.9 fusion.7
  27.6 3.4 %collective-permute-start.2 = (bf16[64,1,2,256]{0,2,3,1:T(2,128)(2,1)}, bf16[64,1,2,256]{0,2,3,1:T(2,128)(2,1)S(1)}, u32[]{:S(2)}, u32[]{:S(2)}) collective-permute-start(bf16[64,1,2,256]{0,2,3,1:T(2,128)(2,1)} %get-tuple-element.7), channel_id=1, source_target_pairs={{0,1},{1,2},{2,3},{3,4},{4,5},{5,6},{6,7},{7,8},{8,9},{9,10},{10,1... | collective-permute-start | bytes 196616 | tf_op jit(solution)/shard_map/ppermute | solution.py:15
  31.0 2.1 %collective-permute-start.3 = (bf16[64,1,2,256]{0,2,3,1:T(2,128)(2,1)}, bf16[64,1,2,256]{0,2,3,1:T(2,128)(2,1)S(1)}, u32[]{:S(2)}, u32[]{:S(2)}) collective-permute-start(bf16[64,1,2,256]{0,2,3,1:T(2,128)(2,1)} %get-tuple-element.8), channel_id=1, source_target_pairs={{1,0},{2,1},{3,2},{4,3},{5,4},{6,5},{7,6},{8,7},{9,8},{10,9},{11,1... | collective-permute-start | bytes 196616 | tf_op jit(solution)/shard_map/ppermute | solution.py:16
  33.2 0.0 copy-done.2
  33.2 0.3 broadcast_in_dim.9
  33.5 1.6 %reshape.13 = bf16[8,2,18432]{2,1,0:T(2,128)(2,1)} reshape(bf16[8,9,64,64]{3,2,1,0:T(8,128)(2,1)S(1)} %broadcast_in_dim.9) | data formatting | bytes 1179648
  35.1 6.9 %all-to-all-start = ((bf16[8,2,18432]{2,1,0:T(2,128)(2,1)}), bf16[8,2,18432]{2,1,0:T(2,128)(2,1)}, u32[]{:S(2)}, u32[]{:S(2)}) async-start(bf16[8,2,18432]{2,1,0:T(2,128)(2,1)} %reshape.13), calls=%async_computation | async-start | bytes 1179648 | tf_op jit(solution)/shard_map/all_to_all | solution.py:109
  42.0 0.0 collective-permute-done.2
  42.0 0.0 collective-permute-done.3
  42.1 4.2 %maximum_bitcast_fusion = bf16[18,2,64,256]{2,1,3,0:T(2,128)(2,1)S(1)} fusion(bf16[64,1,2,256]{0,2,3,1:T(2,128)(2,1)S(1)} %collective-permute-done.3, bf16[64,16,2,256]{0,2,3,1:T(2,128)(2,1)S(1)} %fusion.1, bf16[64,1,2,256]{0,2,3,1:T(2,128)(2,1)S(1)} %collective-permute-done.2), kind=kLoop, calls=%fused_computation.7 | loop fusion | flops 1179648 | bytes 2359296 | tf_op jit(solution)/shard_map/transpose | solution.py:101
  46.2 3.8 %fusion.6 = (bf16[16,2,64,256]{2,1,3,0:T(2,128)(2,1)}, bf16[16,2,64,256]{2,1,3,0:T(2,128)(2,1)S(1)}) fusion(bf16[18,2,64,256]{2,1,3,0:T(2,128)(2,1)S(1)} %maximum_bitcast_fusion), kind=kLoop, calls=%fused_computation.11 | loop fusion | bytes 4194304 | tf_op jit(solution)/shard_map/slice | solution.py:103
  50.0 4.5 %copy.35 = bf16[16,2,64,256]{3,2,1,0:T(8,128)(2,1)S(1)} copy(bf16[16,2,64,256]{2,1,3,0:T(2,128)(2,1)} %get-tuple-element.5) | data formatting | bytes 2097152 | tf_op jit(solution)/shard_map/slice | solution.py:103
  54.6 3.4 %copy.36 = bf16[16,2,64,256]{3,2,1,0:T(8,128)(2,1)} copy(bf16[16,2,64,256]{2,1,3,0:T(2,128)(2,1)S(1)} %get-tuple-element.6) | data formatting | bytes 2097152 | tf_op jit(solution)/shard_map/slice | solution.py:104
  57.9 2.8 %pad_maximum_fusion.2 = bf16[8,4,2,64,256]{4,3,2,1,0:T(8,128)(2,1)} fusion(bf16[8,2,2,64,256]{4,3,2,1,0:T(8,128)(2,1)} %bitcast.15, bf16[8,2,2,64,256]{4,3,2,1,0:T(8,128)(2,1)S(1)} %bitcast.14), kind=kLoop, calls=%fused_computation.8 | loop fusion | flops 1048576 | bytes 4194304 | tf_op jit(solution)/shard_map/concatenate | solution.py:105
  60.7 0.0 copy-start.3
  60.7 0.0 all-to-all-done
  60.7 7.3 %all-to-all-start.1 = ((bf16[8,4,2,64,256]{4,3,2,1,0:T(8,128)(2,1)}), bf16[8,4,2,64,256]{4,3,2,1,0:T(8,128)(2,1)S(1)}, u32[]{:S(2)}, u32[]{:S(2)}) async-start(bf16[8,4,2,64,256]{4,3,2,1,0:T(8,128)(2,1)} %pad_maximum_fusion.2), calls=%async_computation.1 | async-start | bytes 4194304 | tf_op jit(solution)/shard_map/all_to_all | solution.py:106
  68.1 0.0 copy-done.3
  68.1 0.2 broadcast_in_dim_tile.4.bias_ref
  68.3 2.5 %reshape.14 = bf16[8,9,64,64]{3,2,1,0:T(8,128)(2,1)S(1)} reshape(bf16[8,2,18432]{2,1,0:T(2,128)(2,1)} %all-to-all-done) | data formatting | bytes 1179648
  70.8 0.1 slice.35
  70.9 1.7 %maximum_maximum_fusion.pairs_ref = bf16[8,9,64,128]{3,2,1,0:T(8,128)(2,1)} fusion(bf16[7,9,64,64]{3,2,1,0:T(8,128)(2,1)S(1)} %slice.35, bf16[1,9,64,64]{3,2,1,0:T(8,128)(2,1)S(1)} %slice.34, bf16[8,9,64,64]{3,2,1,0:T(8,128)(2,1)S(1)} %reshape.14), kind=kLoop, calls=%fused_computation.9 | loop fusion | flops 3538944 | bytes 2359296 | tf_op jit(solution)/shard_map/concatenate | solution.py:42
  72.5 4.2 %shard_map.64.bank_ref = bf16[9,512,512]{2,1,0:T(8,128)(2,1)} custom-call(bf16[8,9,64,128]{3,2,1,0:T(8,128)(2,1)} %maximum_maximum_fusion.pairs_ref), custom_call_target="tpu_custom_call" | custom-call | tf_op jit(solution)/shard_map/pallas_call | solution.py:43
  76.7 18.4 %all-to-all-done.1.x_ref = bf16[8,4,2,64,256]{4,3,2,1,0:T(8,128)(2,1)S(1)} async-done(((bf16[8,4,2,64,256]{4,3,2,1,0:T(8,128)(2,1)}), bf16[8,4,2,64,256]{4,3,2,1,0:T(8,128)(2,1)S(1)}, u32[]{:S(2)}, u32[]{:S(2)}) %all-to-all-start.1) | async-done | bytes 2097184 | tf_op jit(solution)/shard_map/all_to_all | solution.py:106
  95.1 8.3 %shard_map.65 = bf16[8,2,2,64,256]{4,3,2,1,0:T(8,128)(2,1)S(1)} custom-call(bf16[9,512,512]{2,1,0:T(8,128)(2,1)} %shard_map.64.bank_ref, f32[512,1]{1,0:T(8,128)S(1)} %broadcast_in_dim_tile.4.bias_ref, bf16[8,4,2,64,256]{4,3,2,1,0:T(8,128)(2,1)S(1)} %all-to-all-done.1.x_ref), custom_call_target="tpu_custom_call" | custom-call | tf_op jit(solution)/shard_map/pallas_call | solution.py:75
  103.4 22.7 %all_to_all.15 = bf16[8,2,2,64,256]{4,3,2,1,0:T(8,128)(2,1)S(1)} all-to-all(bf16[8,2,2,64,256]{4,3,2,1,0:T(8,128)(2,1)S(1)} %shard_map.65), channel_id=1, replica_groups=mesh['rot'=8,'space'=32] {'rot'}, dimensions={0} | all-to-all | bytes 2097152 | tf_op jit(solution)/shard_map/all_to_all | solution.py:113
  126.1 2.1 %copy.38 = bf16[1,64,16,2,256]{4,3,2,1,0:T(2,128)(2,1)} copy(bf16[1,64,16,2,256]{4,1,3,2,0:T(8,128)(2,1)S(1)} %bitcast.16) | data formatting | bytes 2097152 | tf_op jit(solution)/shard_map/broadcast_in_dim;reshape | solution.py:115
  (2 shorter events, 0.0 us)
Async XLA Ops:
  0.0 15.9 %copy-start = (bf16[1,9,64,4]{2,3,1,0:T(4,128)(2,1)S(1)}, bf16[1,9,64,4]{2,3,1,0:T(4,128)(2,1)}, u32[]{:S(2)}) copy-start(bf16[1,9,64,4]{2,3,1,0:T(4,128)(2,1)} %param.8) | copy-start | bytes 13828
  0.0 12.0 %copy-start.1 = (bf16[1,64,16,2,256]{4,3,2,1,0:T(2,128)(2,1)S(1)}, bf16[1,64,16,2,256]{4,3,2,1,0:T(2,128)(2,1)}, u32[]{:S(2)}) copy-start(bf16[1,64,16,2,256]{4,3,2,1,0:T(2,128)(2,1)} %param.7) | copy-start | bytes 3145732
  1.0 14.9 %collective-permute-start = (bf16[4,1,2,256]{0,2,3,1:T(2,128)(2,1)S(1)}, bf16[4,1,2,256]{0,2,3,1:T(2,128)(2,1)S(1)}, u32[]{:S(2)}, u32[]{:S(2)}) collective-permute-start(bf16[4,1,2,256]{0,2,3,1:T(2,128)(2,1)S(1)} %copy.31), channel_id=1, source_target_pairs={{0,1},{1,2},{2,3},{3,4},{4,5},{5,6},{6,7},{7,8},{8,9},{9,10},{10,1... | collective-permute-start | bytes 12296 | tf_op jit(solution)/shard_map/ppermute | solution.py:15
  3.1 12.8 %copy-start.4 = (f32[64]{0:T(128)S(1)}, f32[64]{0:T(128)}, u32[]{:S(2)}) copy-start(f32[64]{0:T(128)} %param.9) | copy-start | bytes 772
  3.1 12.8 %collective-permute-start.1 = (bf16[4,1,2,256]{0,2,3,1:T(2,128)(2,1)S(1)}, bf16[4,1,2,256]{0,2,3,1:T(2,128)(2,1)S(1)}, u32[]{:S(2)}, u32[]{:S(2)}) collective-permute-start(bf16[4,1,2,256]{0,2,3,1:T(2,128)(2,1)S(1)} %copy.32), channel_id=1, source_target_pairs={{1,0},{2,1},{3,2},{4,3},{5,4},{6,5},{7,6},{8,7},{9,8},{10,9},{11,1... | collective-permute-start | bytes 12296 | tf_op jit(solution)/shard_map/ppermute | solution.py:16
  15.9 17.2 %copy-start.2 = (bf16[1,9,64,64]{3,2,1,0:T(8,128)(2,1)S(1)}, bf16[1,9,64,64]{3,2,1,0:T(8,128)(2,1)}, u32[]{:S(2)}) copy-start(bf16[1,9,64,64]{3,2,1,0:T(8,128)(2,1)} %param.10) | copy-start | bytes 221188
  27.6 14.4 %collective-permute-start.2 = (bf16[64,1,2,256]{0,2,3,1:T(2,128)(2,1)}, bf16[64,1,2,256]{0,2,3,1:T(2,128)(2,1)S(1)}, u32[]{:S(2)}, u32[]{:S(2)}) collective-permute-start(bf16[64,1,2,256]{0,2,3,1:T(2,128)(2,1)} %get-tuple-element.7), channel_id=1, source_target_pairs={{0,1},{1,2},{2,3},{3,4},{4,5},{5,6},{6,7},{7,8},{8,9},{9,10},{10,1... | collective-permute-start | bytes 196616 | tf_op jit(solution)/shard_map/ppermute | solution.py:15
  31.0 11.0 %collective-permute-start.3 = (bf16[64,1,2,256]{0,2,3,1:T(2,128)(2,1)}, bf16[64,1,2,256]{0,2,3,1:T(2,128)(2,1)S(1)}, u32[]{:S(2)}, u32[]{:S(2)}) collective-permute-start(bf16[64,1,2,256]{0,2,3,1:T(2,128)(2,1)} %get-tuple-element.8), channel_id=1, source_target_pairs={{1,0},{2,1},{3,2},{4,3},{5,4},{6,5},{7,6},{8,7},{9,8},{10,9},{11,1... | collective-permute-start | bytes 196616 | tf_op jit(solution)/shard_map/ppermute | solution.py:16
  35.1 25.6 %all-to-all-start = ((bf16[8,2,18432]{2,1,0:T(2,128)(2,1)}), bf16[8,2,18432]{2,1,0:T(2,128)(2,1)}, u32[]{:S(2)}, u32[]{:S(2)}) async-start(bf16[8,2,18432]{2,1,0:T(2,128)(2,1)} %reshape.13), calls=%async_computation | async-start | bytes 1179648 | tf_op jit(solution)/shard_map/all_to_all | solution.py:109
  60.7 7.3 %copy-start.3 = (f32[64]{0:T(128)S(1)}, f32[64]{0:T(128)}, u32[]{:S(2)}) copy-start(f32[64]{0:T(128)} %param.11) | copy-start | bytes 772
  60.7 34.4 %all-to-all-start.1 = ((bf16[8,4,2,64,256]{4,3,2,1,0:T(8,128)(2,1)}), bf16[8,4,2,64,256]{4,3,2,1,0:T(8,128)(2,1)S(1)}, u32[]{:S(2)}, u32[]{:S(2)}) async-start(bf16[8,4,2,64,256]{4,3,2,1,0:T(8,128)(2,1)} %pad_maximum_fusion.2), calls=%async_computation.1 | async-start | bytes 4194304 | tf_op jit(solution)/shard_map/all_to_all | solution.py:106
where the time goes:
time: 129 us; the launch traced here: 128 us
  local copies, waits for them, and re-layouts  29.6 us (23%)
  starting transfers between devices  25.4 us (20%)
  blocking collectives  22.7 us (18%)
  waiting for transfers between devices  18.4 us (14%)
  Pallas kernels  12.5 us (10%)
  matrix products  10.8 us (8%)
  other arithmetic  8.61 us (7%)
    all_to_all x1, blocking collectives, shards(): returned = lax.all_to_all(mixed, 'rot', 0, 0)  22.7 us
    all_to_all x1, waiting for transfers between devices, shards(): gathered = lax.all_to_all(windows, 'rot', 0, 0)  18.4 us
    unnamed x14, local copies, waits for them, and re-layouts  13.3 us
    conv_general_dilated x1, matrix products, conv_rows_valid(): lax.conv_general_dilated(images, kernel, (1, 1), ((0, 0), (1, 1)), dimens...  10.8 us
    slice x2, local copies, waits for them, and re-layouts, shards(): top = lax.slice_in_dim(hidden_ext, 0, rows, axis=0).reshape(split)  8.33 us
    pallas_call x1, Pallas kernels, group_mix(): pl.pallas_call(mixing_kernel, grid=(rows_out, tiles), in_specs=[pl.BlockS...  8.27 us
    all_to_all x1, starting transfers between devices, shards(): gathered = lax.all_to_all(windows, 'rot', 0, 0)  7.33 us
    all_to_all x1, starting transfers between devices, shards(): filters = lax.all_to_all(spread, 'rot', 0, 0)  6.93 us
  transfers between devices with their start and end apart: 6, of which 1 were waited for; matrix products, arithmetic and copies ran while one was open for 27% of the time, Pallas kernels for 3%

commit v1 on v0

--- a/solution.py
+++ b/solution.py
@@ -15,17 +15,6 @@
     before = lax.ppermute(last, axis, up)
     after = lax.ppermute(leading, axis, down)
     return jnp.concatenate([before, array, after], axis=dim)
-
-
-def conv_rows_valid(images, kernel):
-    return lax.conv_general_dilated(
-        images,
-        kernel,
-        (1, 1),
-        ((0, 0), (1, 1)),
-        dimension_numbers=("CHNW", "HWOI", "CHNW"),
-        preferred_element_type=jnp.float32,
-    )
 
 
 def bank_kernel(pairs_ref, bank_ref):
@@ -92,13 +81,18 @@
     rows = raster.shape[1]
     chunk = rows // n
 
-    raster_padded = padded_rows(raster, "space", 1, 1)
-    lift_kernel = lift_weight[0].reshape(3, 3, channels, -1)
-    lifted = conv_rows_valid(raster_padded, lift_kernel)
-    lifted = lifted + lift_bias[:, None, None, None] + coarse_features[0].astype(jnp.float32)
+    raster_padded = jnp.pad(padded_rows(raster, "space", 1, 1), ((0, 0), (0, 0), (0, 0), (1, 1)))
+    cols = raster.shape[3]
+    taps = jnp.stack(
+        [raster_padded[:, dy : dy + rows, :, dx : dx + cols] for dy in range(3) for dx in range(3)], 0
+    ).reshape((-1,) + raster.shape[1:])
+    lift_matrix = jnp.transpose(lift_weight[0], (1, 0, 2)).reshape(channels, -1)
+    lifted = jnp.einsum("ok,krtw->rtow", lift_matrix, taps, preferred_element_type=jnp.float32)
+    coarse = jnp.transpose(coarse_features[0], (1, 2, 0, 3)).astype(jnp.float32)
+    lifted = lifted + lift_bias[None, None, :, None] + coarse
     hidden = jnp.maximum(lifted, 0.0).astype(jnp.bfloat16)
 
-    hidden_ext = jnp.transpose(padded_rows(hidden, "space", 1, 1), (1, 2, 0, 3))
+    hidden_ext = padded_rows(hidden, "space", 0, 1)
     split = (n, chunk) + hidden_ext.shape[1:]
     top = lax.slice_in_dim(hidden_ext, 0, rows, axis=0).reshape(split)
     bottom = lax.slice_in_dim(hidden_ext, 2, rows + 2, axis=0).reshape(split)

time: 129 us -> 101 us (0.78)
  local copies, waits for them, and re-layouts: 29.6 us -> 12.3 us
  matrix products: 10.8 us -> 2.28 us
  other arithmetic: 8.61 us -> 3.55 us
  waiting for transfers between devices: 18.4 us -> 21.7 us
    slice x4 -> x0, local copies, waits for them, and re-layouts: 11.9 us -> none  [the longest x2 8.33 us: shards(): top = lax.slice_in_dim(hidden_ext, 0, rows, axis=0).reshape(split)]
    conv_general_dilated x1 -> x0, matrix products: 10.8 us -> none  [conv_rows_valid(): lax.conv_general_dilated(images, kernel, (1, 1), ((0, 0), (1, 1)), dimens...]
    unnamed x14 -> x13, local copies, waits for them, and re-layouts: 13.3 us -> 5.8 us
    transpose x1 -> x0, other arithmetic: 4.17 us -> none  [shards(): hidden_ext = jnp.transpose(padded_rows(hidden, 'space', 1, 1), (1, 2, 0, 3))]
    ppermute x2, waiting for transfers between devices: 0.01 us -> 3.43 us  [padded_rows(): after = lax.ppermute(leading, axis, down)]
    another operation x0 -> x11, local copies, waits for them, and re-layouts: none -> 2.89 us  [shards(): jnp.stack([raster_padded[:, dy:dy + rows, :, dx:dx + cols] for dy in rang...]
    dot_general x0 -> x1, matrix products: none -> 2.28 us  [shards(): jnp.einsum('ok,krtw->rtow', lift_matrix, taps, preferred_element_type=jnp...]
    slice x3 -> x2, local copies, waits for them, and re-layouts: 1.86 us -> 0.03 us  [padded_rows(): last = lax.slice_in_dim(array, length - width, length, axis=dim)]
  transfers between devices with their start and end apart: 6 -> 6, of which waited for: 1 -> 2; matrix products, arithmetic and copies ran while one was open for 27% -> 14% of each run, Pallas kernels for 3% -> 4%
where the time goes in v1:
time: 101 us
  starting transfers between devices  25.3 us (25%)
  blocking collectives  22.8 us (23%)
  waiting for transfers between devices  21.7 us (21%)
  Pallas kernels  12.5 us (12%)
  local copies, waits for them, and re-layouts  12.3 us (12%)
  other arithmetic  3.55 us (4%)
  matrix products  2.28 us (2%)
    all_to_all x1, blocking collectives, shards(): returned = lax.all_to_all(mixed, 'rot', 0, 0)  22.8 us
    all_to_all x1, waiting for transfers between devices, shards(): gathered = lax.all_to_all(windows, 'rot', 0, 0)  18.3 us
    pallas_call x1, Pallas kernels, group_mix(): pl.pallas_call(mixing_kernel, grid=(rows_out, tiles), in_specs=[pl.BlockS...  8.27 us
    all_to_all x1, starting transfers between devices, shards(): gathered = lax.all_to_all(windows, 'rot', 0, 0)  7.2 us
    all_to_all x1, starting transfers between devices, shards(): filters = lax.all_to_all(spread, 'rot', 0, 0)  6.93 us
    ppermute x2, starting transfers between devices, padded_rows(): after = lax.ppermute(leading, axis, down)  6.07 us
    unnamed x13, local copies, waits for them, and re-layouts  5.8 us
    ppermute x2, starting transfers between devices, padded_rows(): before = lax.ppermute(last, axis, up)  5.05 us
  transfers between devices with their start and end apart: 6, of which 2 were waited for; matrix products, arithmetic and copies ran while one was open for 14% of the time, Pallas kernels for 4%

profile of v1, /device:TPU:96, one launch (start us, length us, event | category | flops | bytes accessed | tf_op | source)
XLA Modules:
  0.0 100.6 jit_solution(10821980876112287043)
XLA Ops:
  0.0 0.0 copy-start
  0.0 0.9 copy.136
  0.9 1.9 %collective-permute-start = (bf16[4,1,2,256]{3,1,2,0:T(2,128)(2,1)S(1)}, bf16[4,1,2,256]{3,1,2,0:T(2,128)(2,1)S(1)}, u32[]{:S(2)}, u32[]{:S(2)}) collective-permute-start(bf16[4,1,2,256]{3,1,2,0:T(2,128)(2,1)S(1)} %get-tuple-element.17), channel_id=1, source_target_pairs={{0,1},{1,2},{2,3},{3,4},{4,5},{5,6},{6,7},{7,8},{8,9},{9,10},{10,1... | collective-permute-start | bytes 12296 | tf_op jit(solution)/shard_map/ppermute | solution.py:15
  2.8 3.6 %collective-permute-start.1 = (bf16[4,1,2,256]{3,1,2,0:T(2,128)(2,1)S(1)}, bf16[4,1,2,256]{3,1,2,0:T(2,128)(2,1)S(1)}, u32[]{:S(2)}, u32[]{:S(2)}) collective-permute-start(bf16[4,1,2,256]{3,1,2,0:T(2,128)(2,1)S(1)} %get-tuple-element.18), channel_id=1, source_target_pairs={{1,0},{2,1},{3,2},{4,3},{5,4},{6,5},{7,6},{8,7},{9,8},{10,9},{11,1... | collective-permute-start | bytes 12296 | tf_op jit(solution)/shard_map/ppermute | solution.py:16
  6.5 0.0 copy-start.2
  6.5 1.2 %broadcast_in_dim.9 = bf16[8,9,64,64]{3,2,1,0:T(8,128)(2,1)S(1)} broadcast(bf16[9,64,64]{2,1,0:T(8,128)(2,1)} %bitcast.52), dimensions={1,2,3} | broadcast | bytes 663552 | tf_op jit(solution)/shard_map/broadcast_in_dim | solution.py:102
  7.7 1.6 %reshape.17 = bf16[8,2,18432]{2,1,0:T(2,128)(2,1)} reshape(bf16[8,9,64,64]{3,2,1,0:T(8,128)(2,1)S(1)} %broadcast_in_dim.9) | data formatting | bytes 1179648
  9.3 6.9 %all-to-all-start = ((bf16[8,2,18432]{2,1,0:T(2,128)(2,1)}), bf16[8,2,18432]{2,1,0:T(2,128)(2,1)S(1)}, u32[]{:S(2)}, u32[]{:S(2)}) async-start(bf16[8,2,18432]{2,1,0:T(2,128)(2,1)} %reshape.17), calls=%async_computation | async-start | bytes 1179648 | tf_op jit(solution)/shard_map/all_to_all | solution.py:103
  16.3 0.0 copy-done.2
  16.3 0.1 copy.146
  16.4 0.0 collective-permute-done
  16.4 0.0 collective-permute-done.1
  16.4 0.1 fusion.8
  16.6 0.1 slice_bitcast_fusion
  16.7 0.0 copy-start.4
  16.7 0.1 copy.142
  16.8 0.1 copy.144
  16.9 0.1 copy.145
  17.1 0.1 copy.147
  17.2 0.1 copy.148
  17.3 0.1 copy.150
  17.4 0.1 copy.143
  17.5 0.1 copy.149
  17.7 1.8 %stack.39 = bf16[9,4,16,2,256]{4,0,1,3,2:T(8,128)(2,1)S(1)} concatenate(bf16[1,4,16,2,256]{4,0,1,3,2:T(2,128)(2,1)S(1)} %copy.142, bf16[1,4,16,2,256]{4,0,1,3,2:T(2,128)(2,1)S(1)} %copy.143, bf16[1,4,16,2,256]{4,0,1,3,2:T(2,128)(2,1)S(1)} %copy.144, bf16[1,4,16,2,256]{4,0,1,3,2:T(2,128)(2,1)S(1)} %copy.145, bf16[1,4,16,2,256]{4,0,1,3,2:T(2,128)(2,1)S(1)} %copy.146, ...), dimensions={0} | concatenate | bytes 1179648 | tf_op jit(solution)/shard_map/stack | solution.py:86
  19.5 0.0 copy-done
  19.5 0.0 copy-done.4
  19.5 2.3 %fusion.2 = bf16[16,2,64,256]{3,2,1,0:T(8,128)(2,1)S(1)} fusion(bf16[9,4,16,2,256]{4,0,1,3,2:T(8,128)(2,1)S(1)} %stack.39, bf16[1,64,16,2,256]{4,3,2,1,0:T(2,128)(2,1)} %param.7, f32[64]{0:T(128)S(1)} %copy-done.4, bf16[64,9,4,1,1]{0,2,1,4,3:T(4,128)(2,1)S(1)} %bitcast.47), kind=kOutput, calls=%fused_computation.4 | convolution fusion | flops 40370176 | bytes 2691840 | tf_op jit(solution)/shard_map/ok,krtw->rtow/dot_general | solution.py:90
  21.8 3.1 %collective-permute-start.2 = (bf16[1,2,64,256]{3,2,1,0:T(8,128)(2,1)S(1)}, bf16[1,2,64,256]{3,2,1,0:T(8,128)(2,1)S(1)}, u32[]{:S(2)}, u32[]{:S(2)}) collective-permute-start(bf16[1,2,64,256]{3,2,1,0:T(8,128)(2,1)S(1)} %get-tuple-element.7), channel_id=1, source_target_pairs={{0,1},{1,2},{2,3},{3,4},{4,5},{5,6},{6,7},{7,8},{8,9},{9,10},{10,1... | collective-permute-start | bytes 196616 | tf_op jit(solution)/shard_map/ppermute | solution.py:15
  25.0 2.4 %collective-permute-start.3 = (bf16[1,2,64,256]{3,2,1,0:T(8,128)(2,1)S(1)}, bf16[1,2,64,256]{3,2,1,0:T(8,128)(2,1)S(1)}, u32[]{:S(2)}, u32[]{:S(2)}) collective-permute-start(bf16[1,2,64,256]{3,2,1,0:T(8,128)(2,1)S(1)} %get-tuple-element.8), channel_id=1, source_target_pairs={{1,0},{2,1},{3,2},{4,3},{5,4},{6,5},{7,6},{8,7},{9,8},{10,9},{11,1... | collective-permute-start | bytes 196616 | tf_op jit(solution)/shard_map/ppermute | solution.py:16
  27.4 0.0 collective-permute-done.2
  27.4 3.4 %collective-permute-done.3 = bf16[1,2,64,256]{3,2,1,0:T(8,128)(2,1)S(1)} collective-permute-done((bf16[1,2,64,256]{3,2,1,0:T(8,128)(2,1)S(1)}, bf16[1,2,64,256]{3,2,1,0:T(8,128)(2,1)S(1)}, u32[]{:S(2)}, u32[]{:S(2)}) %collective-permute-start.3) | collective-permute-done | bytes 65568 | tf_op jit(solution)/shard_map/ppermute | solution.py:16
  30.8 0.1 pad_maximum_fusion.2
  31.0 1.5 %pad_maximum_fusion = bf16[8,4,2,64,256]{4,3,2,1,0:T(8,128)(2,1)} fusion(bf16[8,2,2,64,256]{4,3,2,1,0:T(8,128)(2,1)S(1)} %bitcast.49, bf16[8,2,2,64,256]{4,3,2,1,0:T(8,128)(2,1)S(1)} %bitcast.48), kind=kLoop, calls=%fused_computation | loop fusion | flops 1048576 | bytes 4194304 | tf_op jit(solution)/shard_map/concatenate | solution.py:99
  32.5 0.0 copy-start.3
  32.5 0.0 all-to-all-done
  32.5 0.0 copy-start.1
  32.5 0.8 copy-done.1
  33.3 7.2 %all-to-all-start.1 = ((bf16[8,4,2,64,256]{4,3,2,1,0:T(8,128)(2,1)}), bf16[8,4,2,64,256]{4,3,2,1,0:T(8,128)(2,1)S(1)}, u32[]{:S(2)}, u32[]{:S(2)}) async-start(bf16[8,4,2,64,256]{4,3,2,1,0:T(8,128)(2,1)} %pad_maximum_fusion), calls=%async_computation.1 | async-start | bytes 4194304 | tf_op jit(solution)/shard_map/all_to_all | solution.py:100
  40.5 0.0 copy-done.3
  40.6 0.2 broadcast_in_dim_tile.4.bias_ref
  40.8 2.5 %reshape.18 = bf16[8,9,64,64]{3,2,1,0:T(8,128)(2,1)S(1)} reshape(bf16[8,2,18432]{2,1,0:T(2,128)(2,1)} %copy-done.1) | data formatting | bytes 1179648
  43.2 0.1 slice.75
  43.3 1.7 %maximum_maximum_fusion.pairs_ref = bf16[8,9,64,128]{3,2,1,0:T(8,128)(2,1)} fusion(bf16[7,9,64,64]{3,2,1,0:T(8,128)(2,1)S(1)} %slice.75, bf16[1,9,64,64]{3,2,1,0:T(8,128)(2,1)S(1)} %slice.74, bf16[8,9,64,64]{3,2,1,0:T(8,128)(2,1)S(1)} %reshape.18), kind=kLoop, calls=%fused_computation.6 | loop fusion | flops 3538944 | bytes 2359296 | tf_op jit(solution)/shard_map/concatenate | solution.py:31
  45.0 4.2 %shard_map.64.bank_ref = bf16[9,512,512]{2,1,0:T(8,128)(2,1)} custom-call(bf16[8,9,64,128]{3,2,1,0:T(8,128)(2,1)} %maximum_maximum_fusion.pairs_ref), custom_call_target="tpu_custom_call" | custom-call | tf_op jit(solution)/shard_map/pallas_call | solution.py:32
  49.2 18.3 %all-to-all-done.1.x_ref = bf16[8,4,2,64,256]{4,3,2,1,0:T(8,128)(2,1)S(1)} async-done(((bf16[8,4,2,64,256]{4,3,2,1,0:T(8,128)(2,1)}), bf16[8,4,2,64,256]{4,3,2,1,0:T(8,128)(2,1)S(1)}, u32[]{:S(2)}, u32[]{:S(2)}) %all-to-all-start.1) | async-done | bytes 2097184 | tf_op jit(solution)/shard_map/all_to_all | solution.py:100
  67.5 8.3 %shard_map.65 = bf16[8,2,2,64,256]{4,3,2,1,0:T(8,128)(2,1)S(1)} custom-call(bf16[9,512,512]{2,1,0:T(8,128)(2,1)} %shard_map.64.bank_ref, f32[512,1]{1,0:T(8,128)S(1)} %broadcast_in_dim_tile.4.bias_ref, bf16[8,4,2,64,256]{4,3,2,1,0:T(8,128)(2,1)S(1)} %all-to-all-done.1.x_ref), custom_call_target="tpu_custom_call" | custom-call | tf_op jit(solution)/shard_map/pallas_call | solution.py:64
  75.8 22.8 %all_to_all.15 = bf16[8,2,2,64,256]{4,3,2,1,0:T(8,128)(2,1)S(1)} all-to-all(bf16[8,2,2,64,256]{4,3,2,1,0:T(8,128)(2,1)S(1)} %shard_map.65), channel_id=1, replica_groups=mesh['rot'=8,'space'=32] {'rot'}, dimensions={0} | all-to-all | bytes 2097152 | tf_op jit(solution)/shard_map/all_to_all | solution.py:107
  98.5 2.1 %copy.154 = bf16[1,64,16,2,256]{4,3,2,1,0:T(2,128)(2,1)} copy(bf16[1,64,16,2,256]{4,1,3,2,0:T(8,128)(2,1)S(1)} %bitcast.50) | data formatting | bytes 2097152 | tf_op jit(solution)/shard_map/broadcast_in_dim;reshape | solution.py:109
  (5 shorter events, 0.1 us)
Async XLA Ops:
  0.0 19.5 %copy-start = (bf16[1,9,64,4]{2,3,1,0:T(4,128)(2,1)S(1)}, bf16[1,9,64,4]{2,3,1,0:T(4,128)(2,1)}, u32[]{:S(2)}) copy-start(bf16[1,9,64,4]{2,3,1,0:T(4,128)(2,1)} %param.8) | copy-start | bytes 13828
  0.9 15.5 %collective-permute-start = (bf16[4,1,2,256]{3,1,2,0:T(2,128)(2,1)S(1)}, bf16[4,1,2,256]{3,1,2,0:T(2,128)(2,1)S(1)}, u32[]{:S(2)}, u32[]{:S(2)}) collective-permute-start(bf16[4,1,2,256]{3,1,2,0:T(2,128)(2,1)S(1)} %get-tuple-element.17), channel_id=1, source_target_pairs={{0,1},{1,2},{2,3},{3,4},{4,5},{5,6},{6,7},{7,8},{8,9},{9,10},{10,1... | collective-permute-start | bytes 12296 | tf_op jit(solution)/shard_map/ppermute | solution.py:15
  2.8 13.6 %collective-permute-start.1 = (bf16[4,1,2,256]{3,1,2,0:T(2,128)(2,1)S(1)}, bf16[4,1,2,256]{3,1,2,0:T(2,128)(2,1)S(1)}, u32[]{:S(2)}, u32[]{:S(2)}) collective-permute-start(bf16[4,1,2,256]{3,1,2,0:T(2,128)(2,1)S(1)} %get-tuple-element.18), channel_id=1, source_target_pairs={{1,0},{2,1},{3,2},{4,3},{5,4},{6,5},{7,6},{8,7},{9,8},{10,9},{11,1... | collective-permute-start | bytes 12296 | tf_op jit(solution)/shard_map/ppermute | solution.py:16
  6.5 9.8 %copy-start.2 = (bf16[4,16,2,256]{3,2,1,0:T(2,128)(2,1)S(1)}, bf16[4,16,2,256]{3,2,1,0:T(2,128)(2,1)}, u32[]{:S(2)}) copy-start(bf16[4,16,2,256]{3,2,1,0:T(2,128)(2,1)} %param.6) | copy-start | bytes 196612
  9.3 23.2 %all-to-all-start = ((bf16[8,2,18432]{2,1,0:T(2,128)(2,1)}), bf16[8,2,18432]{2,1,0:T(2,128)(2,1)S(1)}, u32[]{:S(2)}, u32[]{:S(2)}) async-start(bf16[8,2,18432]{2,1,0:T(2,128)(2,1)} %reshape.17), calls=%async_computation | async-start | bytes 1179648 | tf_op jit(solution)/shard_map/all_to_all | solution.py:103
  16.7 2.8 %copy-start.4 = (f32[64]{0:T(128)S(1)}, f32[64]{0:T(128)}, u32[]{:S(2)}) copy-start(f32[64]{0:T(128)} %param.9) | copy-start | bytes 772
  21.8 5.6 %collective-permute-start.2 = (bf16[1,2,64,256]{3,2,1,0:T(8,128)(2,1)S(1)}, bf16[1,2,64,256]{3,2,1,0:T(8,128)(2,1)S(1)}, u32[]{:S(2)}, u32[]{:S(2)}) collective-permute-start(bf16[1,2,64,256]{3,2,1,0:T(8,128)(2,1)S(1)} %get-tuple-element.7), channel_id=1, source_target_pairs={{0,1},{1,2},{2,3},{3,4},{4,5},{5,6},{6,7},{7,8},{8,9},{9,10},{10,1... | collective-permute-start | bytes 196616 | tf_op jit(solution)/shard_map/ppermute | solution.py:15
  25.0 5.9 %collective-permute-start.3 = (bf16[1,2,64,256]{3,2,1,0:T(8,128)(2,1)S(1)}, bf16[1,2,64,256]{3,2,1,0:T(8,128)(2,1)S(1)}, u32[]{:S(2)}, u32[]{:S(2)}) collective-permute-start(bf16[1,2,64,256]{3,2,1,0:T(8,128)(2,1)S(1)} %get-tuple-element.8), channel_id=1, source_target_pairs={{1,0},{2,1},{3,2},{4,3},{5,4},{6,5},{7,6},{8,7},{9,8},{10,9},{11,1... | collective-permute-start | bytes 196616 | tf_op jit(solution)/shard_map/ppermute | solution.py:16
  32.5 8.0 %copy-start.3 = (f32[64]{0:T(128)S(1)}, f32[64]{0:T(128)}, u32[]{:S(2)}) copy-start(f32[64]{0:T(128)} %param.11) | copy-start | bytes 772
  32.5 0.8 copy-start.1
  33.3 34.1 %all-to-all-start.1 = ((bf16[8,4,2,64,256]{4,3,2,1,0:T(8,128)(2,1)}), bf16[8,4,2,64,256]{4,3,2,1,0:T(8,128)(2,1)S(1)}, u32[]{:S(2)}, u32[]{:S(2)}) async-start(bf16[8,4,2,64,256]{4,3,2,1,0:T(8,128)(2,1)} %pad_maximum_fusion), calls=%async_computation.1 | async-start | bytes 4194304 | tf_op jit(solution)/shard_map/all_to_all | solution.py:100

commit v2 on v1

--- a/solution.py
+++ b/solution.py
@@ -36,11 +36,9 @@
 
 
 def mixing_kernel(bank_ref, bias_ref, x_ref, o_ref):
-    row, tile = pl.program_id(0), pl.program_id(1)
-    count, channels, cols = x_ref.shape[0], x_ref.shape[3], x_ref.shape[4]
-    planes = [
-        jnp.concatenate([x_ref[h, row + dy, tile] for h in range(count)], axis=0) for dy in range(3)
-    ]
+    row = pl.program_id(0)
+    count, channels, cols = x_ref.shape[0], x_ref.shape[2], x_ref.shape[3]
+    planes = [jnp.concatenate([x_ref[h, row + dy] for h in range(count)], axis=0) for dy in range(3)]
     sums = []
     for dx in range(3):
         total = None
@@ -54,23 +52,23 @@
     mixed = sums[1] + left + right + bias_ref[...]
     mixed = jnp.maximum(mixed, 0.0).astype(o_ref.dtype)
     for g in range(count):
-        o_ref[g, 0, 0] = mixed[g * channels : (g + 1) * channels]
+        o_ref[g, 0] = mixed[g * channels : (g + 1) * channels]
 
 
 def group_mix(bank, bias, windows):
-    count, rows_in, tiles, channels, cols = windows.shape
+    count, rows_in, channels, cols = windows.shape
     rows_out = rows_in - 2
     full = count * channels
     return pl.pallas_call(
         mixing_kernel,
-        grid=(rows_out, tiles),
+        grid=(rows_out,),
         in_specs=[
-            pl.BlockSpec((9, full, full), lambda r, t: (0, 0, 0)),
-            pl.BlockSpec((full, 1), lambda r, t: (0, 0)),
-            pl.BlockSpec(windows.shape, lambda r, t: (0, 0, 0, 0, 0)),
+            pl.BlockSpec((9, full, full), lambda r: (0, 0, 0)),
+            pl.BlockSpec((full, 1), lambda r: (0, 0)),
+            pl.BlockSpec(windows.shape, lambda r: (0, 0, 0, 0)),
         ],
-        out_specs=pl.BlockSpec((count, 1, 1, channels, cols), lambda r, t: (0, r, t, 0, 0)),
-        out_shape=jax.ShapeDtypeStruct((count, rows_out, tiles, channels, cols), jnp.bfloat16),
+        out_specs=pl.BlockSpec((count, 1, channels, cols), lambda r: (0, r, 0, 0)),
+        out_shape=jax.ShapeDtypeStruct((count, rows_out, channels, cols), jnp.bfloat16),
         compiler_params=pltpu.CompilerParams(vmem_limit_bytes=48 * 1024 * 1024),
     )(bank, bias, windows)
 
@@ -81,22 +79,28 @@
     rows = raster.shape[1]
     chunk = rows // n
 
-    raster_padded = jnp.pad(padded_rows(raster, "space", 1, 1), ((0, 0), (0, 0), (0, 0), (1, 1)))
-    cols = raster.shape[3]
+    tiles, cols = raster.shape[2], raster.shape[3]
+    quarters = n // tiles
+    span = rows // quarters
+    space = lax.axis_index("space")
+
+    raster_padded = jnp.pad(padded_rows(raster, "space", 1, 2), ((0, 0), (0, 0), (0, 0), (1, 1)))
     taps = jnp.stack(
-        [raster_padded[:, dy : dy + rows, :, dx : dx + cols] for dy in range(3) for dx in range(3)], 0
-    ).reshape((-1,) + raster.shape[1:])
+        [raster_padded[:, dy : dy + rows + 2, :, dx : dx + cols] for dy in range(3) for dx in range(3)], 0
+    ).reshape((-1, rows + 2) + raster.shape[2:])
     lift_matrix = jnp.transpose(lift_weight[0], (1, 0, 2)).reshape(channels, -1)
     lifted = jnp.einsum("ok,krtw->rtow", lift_matrix, taps, preferred_element_type=jnp.float32)
-    coarse = jnp.transpose(coarse_features[0], (1, 2, 0, 3)).astype(jnp.float32)
-    lifted = lifted + lift_bias[None, None, :, None] + coarse
-    hidden = jnp.maximum(lifted, 0.0).astype(jnp.bfloat16)
+    coarse = jnp.transpose(padded_rows(coarse_features[0], "space", 1, 1), (1, 2, 0, 3))
+    lifted = lifted + lift_bias[None, None, :, None] + coarse.astype(jnp.float32)
+    line = lax.broadcasted_iota(jnp.int32, (rows + 2, 1, 1, 1), 0)
+    inside = ((line > 0) | (space > 0)) & ((line < rows + 1) | (space < lax.axis_size("space") - 1))
+    hidden_ext = jnp.where(inside, jnp.maximum(lifted, 0.0), 0.0).astype(jnp.bfloat16)
 
-    hidden_ext = padded_rows(hidden, "space", 0, 1)
-    split = (n, chunk) + hidden_ext.shape[1:]
+    split = (quarters, span) + hidden_ext.shape[1:]
     top = lax.slice_in_dim(hidden_ext, 0, rows, axis=0).reshape(split)
     bottom = lax.slice_in_dim(hidden_ext, 2, rows + 2, axis=0).reshape(split)
-    windows = jnp.concatenate([top, lax.slice_in_dim(bottom, chunk - 2, chunk, axis=1)], axis=1)
+    windows = jnp.concatenate([top, lax.slice_in_dim(bottom, span - 2, span, axis=1)], axis=1)
+    windows = jnp.transpose(windows, (2, 0, 1, 3, 4)).reshape((n, span + 2) + hidden_ext.shape[2:])
     gathered = lax.all_to_all(windows, "rot", 0, 0)
 
     spread = jnp.broadcast_to(group_weight, (n,) + group_weight.shape[1:])
@@ -105,7 +109,8 @@
     mixed = group_mix(circulant_bank(filters), bias, gathered)
 
     returned = lax.all_to_all(mixed, "rot", 0, 0)
-    result = jnp.transpose(returned, (3, 0, 1, 2, 4)).reshape((channels, rows) + returned.shape[2:3] + returned.shape[4:])
+    returned = returned.reshape((tiles, quarters) + returned.shape[1:])
+    result = jnp.transpose(returned, (3, 1, 2, 0, 4)).reshape((channels, rows, tiles, cols))
     return result[None]
 
 

time: 101 us -> 102 us (level)
  local copies, waits for them, and re-layouts: 12.3 us -> 23.4 us
  waiting for transfers between devices: 21.7 us -> 12.8 us
  other arithmetic: 3.55 us -> 2.5 us
    another operation x12 -> x11, local copies, waits for them, and re-layouts: 4.94 us -> 11.6 us  [shards(): jnp.stack([raster_padded[:, dy:dy + rows + 2, :, dx:dx + cols] for dy in...]
    all_to_all x1, waiting for transfers between devices: 18.3 us -> 12.8 us  [shards(): gathered = lax.all_to_all(windows, 'rot', 0, 0)]
    ppermute x2, waiting for transfers between devices: 3.43 us -> 0.01 us  [padded_rows(): after = lax.ppermute(leading, axis, down)]
    transpose x0 -> x1, local copies, waits for them, and re-layouts: none -> 2.05 us  [shards(): jnp.transpose(returned, (3, 1, 2, 0, 4))]
    concatenate x3 -> x1, other arithmetic: 1.83 us -> 0.14 us  [shards(): jnp.concatenate([top, lax.slice_in_dim(bottom, span - 2, span, axis=1)],...]
    concatenate x0 -> x2, local copies, waits for them, and re-layouts: none -> 1.32 us  [the longest x1 1.31 us: shards(): jnp.concatenate([top, lax.slice_in_dim(bottom, span - 2, span, axis=1)],...]
    unnamed x13 -> x17, local copies, waits for them, and re-layouts: 5.8 us -> 6.81 us
  transfers between devices with their start and end apart: 6 -> 6, of which waited for: 2 -> 1; matrix products, arithmetic and copies ran while one was open for 14% -> 24% of each run, Pallas kernels for 4% -> 4%
where the time goes in v2:
time: 102 us; the launch traced here: 101 us
  starting transfers between devices  25.3 us (25%)
  local copies, waits for them, and re-layouts  23.4 us (23%)
  blocking collectives  22.7 us (22%)
  waiting for transfers between devices  12.8 us (13%)
  Pallas kernels  12.5 us (12%)
  other arithmetic  2.5 us (2%)
  matrix products  1.54 us (2%)
    all_to_all x1, blocking collectives, shards(): returned = lax.all_to_all(mixed, 'rot', 0, 0)  22.7 us
    all_to_all x1, waiting for transfers between devices, shards(): gathered = lax.all_to_all(windows, 'rot', 0, 0)  12.8 us
    another operation x11, local copies, waits for them, and re-layouts, shards(): jnp.stack([raster_padded[:, dy:dy + rows + 2, :, dx:dx + cols] for dy in...  11.6 us
    pallas_call x1, Pallas kernels, group_mix(): pl.pallas_call(mixing_kernel, grid=(rows_out,), in_specs=[pl.BlockSpec((9...  8.25 us
    all_to_all x1, starting transfers between devices, shards(): gathered = lax.all_to_all(windows, 'rot', 0, 0)  7.21 us
    all_to_all x1, starting transfers between devices, shards(): filters = lax.all_to_all(spread, 'rot', 0, 0)  6.93 us
    unnamed x17, local copies, waits for them, and re-layouts  6.81 us
    ppermute x2, starting transfers between devices, padded_rows(): after = lax.ppermute(leading, axis, down)  5.79 us
  transfers between devices with their start and end apart: 6, of which 1 were waited for; matrix products, arithmetic and copies ran while one was open for 24% of the time, Pallas kernels for 4%

profile of v2, /device:TPU:96, one launch (start us, length us, event | category | flops | bytes accessed | tf_op | source)
XLA Modules:
  0.0 100.8 jit_solution(8326607055114744801)
XLA Ops:
  0.0 0.0 copy-start
  0.0 0.8 fusion.9
  0.8 1.9 %collective-permute-start = (bf16[4,2,2,256]{3,2,1,0:T(2,128)(2,1)S(1)}, bf16[4,2,2,256]{3,2,1,0:T(2,128)(2,1)S(1)}, u32[]{:S(2)}, u32[]{:S(2)}) collective-permute-start(bf16[4,2,2,256]{3,2,1,0:T(2,128)(2,1)S(1)} %get-tuple-element.19), channel_id=1, source_target_pairs={{0,1},{1,2},{2,3},{3,4},{4,5},{5,6},{6,7},{7,8},{8,9},{9,10},{10,1... | collective-permute-start | bytes 24584 | tf_op jit(solution)/shard_map/ppermute | solution.py:15
  2.7 3.6 %collective-permute-start.1 = (bf16[4,2,2,256]{3,2,1,0:T(2,128)(2,1)S(1)}, bf16[4,2,2,256]{3,2,1,0:T(2,128)(2,1)S(1)}, u32[]{:S(2)}, u32[]{:S(2)}) collective-permute-start(bf16[4,2,2,256]{3,2,1,0:T(2,128)(2,1)S(1)} %get-tuple-element.18), channel_id=1, source_target_pairs={{1,0},{2,1},{3,2},{4,3},{5,4},{6,5},{7,6},{8,7},{9,8},{10,9},{11,1... | collective-permute-start | bytes 24584 | tf_op jit(solution)/shard_map/ppermute | solution.py:16
  6.4 1.8 %copy.184 = bf16[1,64,16,2,256]{4,1,3,2,0:T(8,128)(2,1)S(1)} copy(bf16[1,64,16,2,256]{4,3,2,1,0:T(2,128)(2,1)} %param.7) | data formatting | bytes 2097152 | tf_op args[1]
  8.2 3.4 %collective-permute-start.2 = (bf16[64,1,2,256]{3,0,2,1:T(8,128)(2,1)S(1)}, bf16[64,1,2,256]{3,0,2,1:T(8,128)(2,1)}, u32[]{:S(2)}, u32[]{:S(2)}) collective-permute-start(bf16[64,1,2,256]{3,0,2,1:T(8,128)(2,1)S(1)} %get-tuple-element.7), channel_id=1, source_target_pairs={{0,1},{1,2},{2,3},{3,4},{4,5},{5,6},{6,7},{7,8},{8,9},{9,10},{10,1... | collective-permute-start | bytes 196616 | tf_op jit(solution)/shard_map/ppermute | solution.py:15
  11.6 2.1 %collective-permute-start.3 = (bf16[64,1,2,256]{3,0,2,1:T(8,128)(2,1)S(1)}, bf16[64,1,2,256]{3,0,2,1:T(8,128)(2,1)}, u32[]{:S(2)}, u32[]{:S(2)}) collective-permute-start(bf16[64,1,2,256]{3,0,2,1:T(8,128)(2,1)S(1)} %get-tuple-element.8), channel_id=1, source_target_pairs={{1,0},{2,1},{3,2},{4,3},{5,4},{6,5},{7,6},{8,7},{9,8},{10,9},{11,1... | collective-permute-start | bytes 196616 | tf_op jit(solution)/shard_map/ppermute | solution.py:16
  13.8 0.0 copy-done.3
  13.8 0.3 broadcast_in_dim.19
  14.1 0.0 copy-start.2
  14.1 1.6 %reshape.37 = bf16[8,2,18432]{2,1,0:T(2,128)(2,1)} reshape(bf16[8,9,64,64]{3,2,1,0:T(8,128)(2,1)S(1)} %broadcast_in_dim.19) | data formatting | bytes 1179648
  15.7 6.9 %all-to-all-start = ((bf16[8,2,18432]{2,1,0:T(2,128)(2,1)}), bf16[8,2,18432]{2,1,0:T(2,128)(2,1)S(1)}, u32[]{:S(2)}, u32[]{:S(2)}) async-start(bf16[8,2,18432]{2,1,0:T(2,128)(2,1)} %reshape.37), calls=%async_computation | async-start | bytes 1179648 | tf_op jit(solution)/shard_map/all_to_all | solution.py:107
  22.6 0.6 or_and_fusion
  23.2 0.0 collective-permute-done
  23.2 0.0 copy-done.2
  23.2 0.1 constant_dynamic-update-slice_fusion.1
  23.3 0.0 collective-permute-done.1
  23.3 0.5 slice_bitcast_fusion.1
  23.9 0.1 copy.158
  24.0 0.1 copy.160
  24.1 0.1 copy.161
  24.2 0.1 copy.162
  24.4 0.8 copy.163
  25.1 0.8 copy.164
  25.9 0.8 copy.166
  26.7 0.1 maximum_bitcast_fusion.1
  26.8 0.8 copy.159
  27.6 0.8 copy.165
  28.4 6.7 %stack.39 = bf16[9,4,18,2,256]{4,0,1,3,2:T(8,128)(2,1)S(1)} concatenate(bf16[1,4,18,2,256]{4,0,1,3,2:T(2,128)(2,1)S(1)} %copy.158, bf16[1,4,18,2,256]{4,0,1,3,2:T(2,128)(2,1)} %copy.159, bf16[1,4,18,2,256]{4,0,1,3,2:T(2,128)(2,1)S(1)} %copy.160, bf16[1,4,18,2,256]{4,0,1,3,2:T(2,128)(2,1)S(1)} %copy.161, bf16[1,4,18,2,256]{4,0,1,3,2:T(2,128)(2,1)S(1)} %copy.162, ...), dimensions={0} | concatenate | bytes 1327104 | tf_op jit(solution)/shard_map/stack | solution.py:88
  35.1 0.0 collective-permute-done.2
  35.1 0.0 collective-permute-done.3
  35.1 0.0 copy-done
  35.1 1.5 %fusion.2 = bf16[18,2,64,256]{3,2,1,0:T(8,128)(2,1)S(1)} fusion(bf16[64,1,2,256]{3,0,2,1:T(8,128)(2,1)} %collective-permute-done.3, bf16[64,16,2,256]{3,0,2,1:T(8,128)(2,1)S(1)} %bitcast.57, bf16[64,1,2,256]{3,0,2,1:T(8,128)(2,1)} %collective-permute-done.2, f32[64]{0:T(128)S(1)} %copy-done.5, pred[18]{0:T(512)(128)(4,1)} %or_and_fusion, ...), kind=kOutput, calls=%fused_computation.3 | convolution fusion | flops 47185920 | bytes 3027730 | tf_op jit(solution)/shard_map/ok,krtw->rtow/dot_general | solution.py:92
  36.7 0.2 fusion.7
  36.9 0.1 pad_maximum_fusion
  37.1 1.3 %copy.178 = bf16[4,6,2,64,256]{4,3,1,0,2:T(8,128)(2,1)} copy(bf16[4,6,2,64,256]{4,3,2,1,0:T(8,128)(2,1)S(1)} %pad_maximum_fusion) | data formatting | bytes 3145728 | tf_op jit(solution)/shard_map/concatenate | solution.py:102
  38.4 0.0 all-to-all-done
  38.4 0.8 copy-done.1
  39.2 7.2 %all-to-all-start.1 = ((bf16[8,6,64,256]{3,2,1,0:T(8,128)(2,1)}), bf16[8,6,64,256]{3,2,1,0:T(8,128)(2,1)S(1)}, u32[]{:S(2)}, u32[]{:S(2)}) async-start(bf16[8,6,64,256]{3,2,1,0:T(8,128)(2,1)} %bitcast.21), calls=%async_computation.1 | async-start | bytes 3145728 | tf_op jit(solution)/shard_map/all_to_all | solution.py:104
  46.4 0.2 broadcast_in_dim_tile.4.bias_ref
  46.6 2.5 %reshape.38 = bf16[8,9,64,64]{3,2,1,0:T(8,128)(2,1)S(1)} reshape(bf16[8,2,18432]{2,1,0:T(2,128)(2,1)} %copy-done.1) | data formatting | bytes 1179648
  49.1 0.1 slice.74
  49.2 1.7 %maximum_maximum_fusion.pairs_ref = bf16[8,9,64,128]{3,2,1,0:T(8,128)(2,1)} fusion(bf16[7,9,64,64]{3,2,1,0:T(8,128)(2,1)S(1)} %slice.74, bf16[1,9,64,64]{3,2,1,0:T(8,128)(2,1)S(1)} %slice.73, bf16[8,9,64,64]{3,2,1,0:T(8,128)(2,1)S(1)} %reshape.38), kind=kLoop, calls=%fused_computation.6 | loop fusion | flops 3538944 | bytes 2359296 | tf_op jit(solution)/shard_map/concatenate | solution.py:31
  50.9 4.2 %shard_map.64.bank_ref = bf16[9,512,512]{2,1,0:T(8,128)(2,1)} custom-call(bf16[8,9,64,128]{3,2,1,0:T(8,128)(2,1)} %maximum_maximum_fusion.pairs_ref), custom_call_target="tpu_custom_call" | custom-call | tf_op jit(solution)/shard_map/pallas_call | solution.py:32
  55.1 12.8 %all-to-all-done.1.x_ref = bf16[8,6,64,256]{3,2,1,0:T(8,128)(2,1)S(1)} async-done(((bf16[8,6,64,256]{3,2,1,0:T(8,128)(2,1)}), bf16[8,6,64,256]{3,2,1,0:T(8,128)(2,1)S(1)}, u32[]{:S(2)}, u32[]{:S(2)}) %all-to-all-start.1) | async-done | bytes 1572896 | tf_op jit(solution)/shard_map/all_to_all | solution.py:104
  67.9 8.3 %shard_map.65 = bf16[8,4,64,256]{3,2,1,0:T(8,128)(2,1)S(1)} custom-call(bf16[9,512,512]{2,1,0:T(8,128)(2,1)} %shard_map.64.bank_ref, f32[512,1]{1,0:T(8,128)S(1)} %broadcast_in_dim_tile.4.bias_ref, bf16[8,6,64,256]{3,2,1,0:T(8,128)(2,1)S(1)} %all-to-all-done.1.x_ref), custom_call_target="tpu_custom_call" | custom-call | tf_op jit(solution)/shard_map/pallas_call | solution.py:62
  76.1 22.7 %all_to_all.15 = bf16[8,4,64,256]{3,2,1,0:T(8,128)(2,1)S(1)} all-to-all(bf16[8,4,64,256]{3,2,1,0:T(8,128)(2,1)S(1)} %shard_map.65), channel_id=1, replica_groups=mesh['rot'=8,'space'=32] {'rot'}, dimensions={0} | all-to-all | bytes 2097152 | tf_op jit(solution)/shard_map/all_to_all | solution.py:111
  98.8 2.1 %copy.172 = bf16[64,4,4,2,256]{4,3,2,1,0:T(2,128)(2,1)} copy(bf16[64,4,4,2,256]{4,0,2,1,3:T(8,128)(2,1)S(1)} %bitcast.54) | data formatting | bytes 2097152 | tf_op jit(solution)/shard_map/transpose | solution.py:113
  (12 shorter events, 0.1 us)
Async XLA Ops:
  0.0 35.1 %copy-start = (bf16[1,9,64,4]{2,3,1,0:T(4,128)(2,1)S(1)}, bf16[1,9,64,4]{2,3,1,0:T(4,128)(2,1)}, u32[]{:S(2)}) copy-start(bf16[1,9,64,4]{2,3,1,0:T(4,128)(2,1)} %param.8) | copy-start | bytes 13828
  0.0 13.8 %copy-start.3 = (bf16[1,9,64,64]{3,2,1,0:T(8,128)(2,1)S(1)}, bf16[1,9,64,64]{3,2,1,0:T(8,128)(2,1)}, u32[]{:S(2)}) copy-start(bf16[1,9,64,64]{3,2,1,0:T(8,128)(2,1)} %param.10) | copy-start | bytes 221188
  0.8 22.4 %collective-permute-start = (bf16[4,2,2,256]{3,2,1,0:T(2,128)(2,1)S(1)}, bf16[4,2,2,256]{3,2,1,0:T(2,128)(2,1)S(1)}, u32[]{:S(2)}, u32[]{:S(2)}) collective-permute-start(bf16[4,2,2,256]{3,2,1,0:T(2,128)(2,1)S(1)} %get-tuple-element.19), channel_id=1, source_target_pairs={{0,1},{1,2},{2,3},{3,4},{4,5},{5,6},{6,7},{7,8},{8,9},{9,10},{10,1... | collective-permute-start | bytes 24584 | tf_op jit(solution)/shard_map/ppermute | solution.py:15
  2.7 20.6 %collective-permute-start.1 = (bf16[4,2,2,256]{3,2,1,0:T(2,128)(2,1)S(1)}, bf16[4,2,2,256]{3,2,1,0:T(2,128)(2,1)S(1)}, u32[]{:S(2)}, u32[]{:S(2)}) collective-permute-start(bf16[4,2,2,256]{3,2,1,0:T(2,128)(2,1)S(1)} %get-tuple-element.18), channel_id=1, source_target_pairs={{1,0},{2,1},{3,2},{4,3},{5,4},{6,5},{7,6},{8,7},{9,8},{10,9},{11,1... | collective-permute-start | bytes 24584 | tf_op jit(solution)/shard_map/ppermute | solution.py:16
  8.2 26.9 %collective-permute-start.2 = (bf16[64,1,2,256]{3,0,2,1:T(8,128)(2,1)S(1)}, bf16[64,1,2,256]{3,0,2,1:T(8,128)(2,1)}, u32[]{:S(2)}, u32[]{:S(2)}) collective-permute-start(bf16[64,1,2,256]{3,0,2,1:T(8,128)(2,1)S(1)} %get-tuple-element.7), channel_id=1, source_target_pairs={{0,1},{1,2},{2,3},{3,4},{4,5},{5,6},{6,7},{7,8},{8,9},{9,10},{10,1... | collective-permute-start | bytes 196616 | tf_op jit(solution)/shard_map/ppermute | solution.py:15
  11.6 23.5 %collective-permute-start.3 = (bf16[64,1,2,256]{3,0,2,1:T(8,128)(2,1)S(1)}, bf16[64,1,2,256]{3,0,2,1:T(8,128)(2,1)}, u32[]{:S(2)}, u32[]{:S(2)}) collective-permute-start(bf16[64,1,2,256]{3,0,2,1:T(8,128)(2,1)S(1)} %get-tuple-element.8), channel_id=1, source_target_pairs={{1,0},{2,1},{3,2},{4,3},{5,4},{6,5},{7,6},{8,7},{9,8},{10,9},{11,1... | collective-permute-start | bytes 196616 | tf_op jit(solution)/shard_map/ppermute | solution.py:16
  14.1 9.2 %copy-start.2 = (bf16[4,16,2,256]{3,2,1,0:T(2,128)(2,1)S(1)}, bf16[4,16,2,256]{3,2,1,0:T(2,128)(2,1)}, u32[]{:S(2)}) copy-start(bf16[4,16,2,256]{3,2,1,0:T(2,128)(2,1)} %param.6) | copy-start | bytes 196612
  15.7 22.7 %all-to-all-start = ((bf16[8,2,18432]{2,1,0:T(2,128)(2,1)}), bf16[8,2,18432]{2,1,0:T(2,128)(2,1)S(1)}, u32[]{:S(2)}, u32[]{:S(2)}) async-start(bf16[8,2,18432]{2,1,0:T(2,128)(2,1)} %reshape.37), calls=%async_computation | async-start | bytes 1179648 | tf_op jit(solution)/shard_map/all_to_all | solution.py:107
  26.7 8.4 %copy-start.5 = (f32[64]{0:T(128)S(1)}, f32[64]{0:T(128)}, u32[]{:S(2)}) copy-start(f32[64]{0:T(128)} %param.9) | copy-start | bytes 772
  38.4 0.8 copy-start.1
  38.4 8.0 %copy-start.4 = (f32[64]{0:T(128)S(1)}, f32[64]{0:T(128)}, u32[]{:S(2)}) copy-start(f32[64]{0:T(128)} %param.11) | copy-start | bytes 772
  39.2 28.6 %all-to-all-start.1 = ((bf16[8,6,64,256]{3,2,1,0:T(8,128)(2,1)}), bf16[8,6,64,256]{3,2,1,0:T(8,128)(2,1)S(1)}, u32[]{:S(2)}, u32[]{:S(2)}) async-start(bf16[8,6,64,256]{3,2,1,0:T(8,128)(2,1)} %bitcast.21), calls=%async_computation.1 | async-start | bytes 3145728 | tf_op jit(solution)/shard_map/all_to_all | solution.py:104

commit v3 on v2

--- a/solution.py
+++ b/solution.py
@@ -85,11 +85,20 @@
     space = lax.axis_index("space")
 
     raster_padded = jnp.pad(padded_rows(raster, "space", 1, 2), ((0, 0), (0, 0), (0, 0), (1, 1)))
-    taps = jnp.stack(
-        [raster_padded[:, dy : dy + rows + 2, :, dx : dx + cols] for dy in range(3) for dx in range(3)], 0
-    ).reshape((-1, rows + 2) + raster.shape[2:])
     lift_matrix = jnp.transpose(lift_weight[0], (1, 0, 2)).reshape(channels, -1)
-    lifted = jnp.einsum("ok,krtw->rtow", lift_matrix, taps, preferred_element_type=jnp.float32)
+
+    def lift(first, count):
+        taps = jnp.stack(
+            [
+                raster_padded[:, first + dy : first + dy + count, :, dx : dx + cols]
+                for dy in range(3)
+                for dx in range(3)
+            ],
+            0,
+        ).reshape((-1, count) + raster.shape[2:])
+        return jnp.einsum("ok,krtw->rtow", lift_matrix, taps, preferred_element_type=jnp.float32)
+
+    lifted = jnp.concatenate([lift(0, 1), lift(1, rows), lift(rows + 1, 1)], axis=0)
     coarse = jnp.transpose(padded_rows(coarse_features[0], "space", 1, 1), (1, 2, 0, 3))
     lifted = lifted + lift_bias[None, None, :, None] + coarse.astype(jnp.float32)
     line = lax.broadcasted_iota(jnp.int32, (rows + 2, 1, 1, 1), 0)

time: 102 us -> 102 us (level)
  local copies, waits for them, and re-layouts: 23.4 us -> 22.2 us
  other arithmetic: 2.5 us -> 3.55 us
    another operation x11 -> x13, local copies, waits for them, and re-layouts: 11.6 us -> 8.41 us  [lift(): jnp.stack([raster_padded[:, first + dy:first + dy + count, :, dx:dx + col...]
    convert_element_type x0 -> x1, other arithmetic: none -> 1.47 us  [shards(): jnp.where(inside, jnp.maximum(lifted, 0.0), 0.0).astype(jnp.bfloat16)]
    slice x1 -> x2, local copies, waits for them, and re-layouts: 0.01 us -> 1.43 us  [padded_rows(): last = lax.slice_in_dim(array, length - width, length, axis=dim)]
    ppermute x0 -> x2, local copies, waits for them, and re-layouts: none -> 1.41 us  [the longest x1 0.7 us: padded_rows(): before = lax.ppermute(last, axis, up)]
    unnamed x17 -> x35, local copies, waits for them, and re-layouts: 6.81 us -> 6.73 us
where the time goes in v3:
time: 102 us; the launch traced here: 101 us
  starting transfers between devices  25.4 us (25%)
  blocking collectives  22.7 us (22%)
  local copies, waits for them, and re-layouts  22.2 us (22%)
  waiting for transfers between devices  12.8 us (13%)
  Pallas kernels  12.5 us (12%)
  other arithmetic  3.55 us (3%)
  matrix products  1.59 us (2%)
    all_to_all x1, blocking collectives, shards(): returned = lax.all_to_all(mixed, 'rot', 0, 0)  22.7 us
    all_to_all x1, waiting for transfers between devices, shards(): gathered = lax.all_to_all(windows, 'rot', 0, 0)  12.8 us
    another operation x13, local copies, waits for them, and re-layouts, lift(): jnp.stack([raster_padded[:, first + dy:first + dy + count, :, dx:dx + col...  8.41 us
    pallas_call x1, Pallas kernels, group_mix(): pl.pallas_call(mixing_kernel, grid=(rows_out,), in_specs=[pl.BlockSpec((9...  8.25 us
    all_to_all x1, starting transfers between devices, shards(): gathered = lax.all_to_all(windows, 'rot', 0, 0)  7.34 us
    all_to_all x1, starting transfers between devices, shards(): filters = lax.all_to_all(spread, 'rot', 0, 0)  6.93 us
    unnamed x35, local copies, waits for them, and re-layouts  6.73 us
    ppermute x2, starting transfers between devices, padded_rows(): after = lax.ppermute(leading, axis, down)  5.79 us
  transfers between devices with their start and end apart: 6, of which 1 were waited for; matrix products, arithmetic and copies ran while one was open for 24% of the time, Pallas kernels for 4%

profile of v3, /device:TPU:96, one launch (start us, length us, event | category | flops | bytes accessed | tf_op | source)
XLA Modules:
  0.0 101.0 jit_solution(3814240448592509532)
XLA Ops:
  0.0 0.8 fusion.11
  0.8 1.9 %collective-permute-start = (bf16[4,2,2,256]{3,2,0,1:T(2,128)(2,1)S(1)}, bf16[4,2,2,256]{3,2,0,1:T(2,128)(2,1)S(1)}, u32[]{:S(2)}, u32[]{:S(2)}) collective-permute-start(bf16[4,2,2,256]{3,2,0,1:T(2,128)(2,1)S(1)} %get-tuple-element.27), channel_id=1, source_target_pairs={{0,1},{1,2},{2,3},{3,4},{4,5},{5,6},{6,7},{7,8},{8,9},{9,10},{10,1... | collective-permute-start | bytes 24584 | tf_op jit(solution)/shard_map/ppermute | solution.py:15
  2.7 3.6 %collective-permute-start.1 = (bf16[4,2,2,256]{3,2,0,1:T(2,128)(2,1)S(1)}, bf16[4,2,2,256]{3,2,0,1:T(2,128)(2,1)S(1)}, u32[]{:S(2)}, u32[]{:S(2)}) collective-permute-start(bf16[4,2,2,256]{3,2,0,1:T(2,128)(2,1)S(1)} %get-tuple-element.28), channel_id=1, source_target_pairs={{1,0},{2,1},{3,2},{4,3},{5,4},{6,5},{7,6},{8,7},{9,8},{10,9},{11,1... | collective-permute-start | bytes 24584 | tf_op jit(solution)/shard_map/ppermute | solution.py:16
  6.3 1.8 %copy.288 = bf16[1,64,16,2,256]{4,1,3,2,0:T(8,128)(2,1)S(1)} copy(bf16[1,64,16,2,256]{4,3,2,1,0:T(2,128)(2,1)} %param.7) | data formatting | bytes 2097152 | tf_op args[1]
  8.2 0.7 fusion.10
  8.8 3.4 %collective-permute-start.2 = (bf16[64,1,2,256]{3,0,2,1:T(8,128)(2,1)}, bf16[64,1,2,256]{3,0,2,1:T(8,128)(2,1)}, u32[]{:S(2)}, u32[]{:S(2)}) collective-permute-start(bf16[64,1,2,256]{3,0,2,1:T(8,128)(2,1)} %get-tuple-element.7), channel_id=1, source_target_pairs={{0,1},{1,2},{2,3},{3,4},{4,5},{5,6},{6,7},{7,8},{8,9},{9,10},{10,1... | collective-permute-start | bytes 196616 | tf_op jit(solution)/shard_map/ppermute | solution.py:15
  12.2 2.1 %collective-permute-start.3 = (bf16[64,1,2,256]{3,0,2,1:T(8,128)(2,1)}, bf16[64,1,2,256]{3,0,2,1:T(8,128)(2,1)}, u32[]{:S(2)}, u32[]{:S(2)}) collective-permute-start(bf16[64,1,2,256]{3,0,2,1:T(8,128)(2,1)} %get-tuple-element.8), channel_id=1, source_target_pairs={{1,0},{2,1},{3,2},{4,3},{5,4},{6,5},{7,6},{8,7},{9,8},{10,9},{11,1... | collective-permute-start | bytes 196616 | tf_op jit(solution)/shard_map/ppermute | solution.py:16
  14.4 0.3 broadcast_in_dim.19
  14.7 1.6 %reshape.56 = bf16[8,2,18432]{2,1,0:T(2,128)(2,1)} reshape(bf16[8,9,64,64]{3,2,1,0:T(8,128)(2,1)S(1)} %broadcast_in_dim.19) | data formatting | bytes 1179648
  16.3 6.9 %all-to-all-start = ((bf16[8,2,18432]{2,1,0:T(2,128)(2,1)}), bf16[8,2,18432]{2,1,0:T(2,128)(2,1)S(1)}, u32[]{:S(2)}, u32[]{:S(2)}) async-start(bf16[8,2,18432]{2,1,0:T(2,128)(2,1)} %reshape.56), calls=%async_computation | async-start | bytes 1179648 | tf_op jit(solution)/shard_map/all_to_all | solution.py:116
  23.3 0.1 copy.240
  23.5 0.2 select_maximum_fusion
  23.7 0.3 slice_bitcast_fusion
  24.1 0.1 constant_dynamic-update-slice_fusion.6
  24.2 0.1 constant_dynamic-update-slice_fusion.5
  24.3 0.1 constant_dynamic-update-slice_fusion.3
  24.4 0.1 constant_dynamic-update-slice_fusion.2
  24.5 0.1 constant_dynamic-update-slice_fusion
  24.6 0.1 constant_dynamic-update-slice_fusion.9
  24.7 0.1 copy.236
  24.8 0.4 copy-done.6
  25.2 0.1 copy.238
  25.3 0.1 copy.239
  25.4 0.1 copy.241
  25.5 0.8 copy.242
  26.2 0.7 copy.244
  27.0 0.7 copy.226
  27.7 0.7 copy.234
  28.4 0.7 copy.237
  29.2 0.7 copy.243
  29.9 0.2 convolution_bitcast_fusion.1
  30.1 4.4 %stack.109 = bf16[9,4,16,2,256]{4,0,1,3,2:T(8,128)(2,1)S(1)} concatenate(bf16[1,4,16,2,256]{4,0,1,3,2:T(2,128)(2,1)S(1)} %copy.236, bf16[1,4,16,2,256]{4,0,1,3,2:T(2,128)(2,1)} %copy.237, bf16[1,4,16,2,256]{4,0,1,3,2:T(2,128)(2,1)S(1)} %copy.238, bf16[1,4,16,2,256]{4,0,1,3,2:T(2,128)(2,1)S(1)} %copy.239, bf16[1,4,16,2,256]{4,0,1,3,2:T(2,128)(2,1)S(1)} %copy.240, ...), dimensions={0} | concatenate | bytes 1179648 | tf_op jit(solution)/shard_map/stack | solution.py:91
  34.6 1.2 %convolution_bitcast_fusion = f32[16,2,64,256]{3,2,1,0:T(8,128)S(1)} fusion(bf16[9,4,16,2,256]{4,0,1,3,2:T(8,128)(2,1)S(1)} %stack.109, bf16[64,9,4,1,1]{0,2,1,4,3:T(4,128)(2,1)} %bitcast.136), kind=kOutput, calls=%fused_computation.5 | convolution fusion | flops 37748736 | bytes 2691584 | tf_op jit(solution)/shard_map/ok,krtw->rtow/dot_general | solution.py:99
  35.8 0.2 convolution_bitcast_fusion.2
  36.0 1.5 %fusion.3 = bf16[18,2,64,256]{3,2,1,0:T(8,128)(2,1)S(1)} fusion(f32[1,2,64,256]{3,2,1,0:T(8,128)S(1)} %convolution_bitcast_fusion.1, f32[16,2,64,256]{3,2,1,0:T(8,128)S(1)} %convolution_bitcast_fusion, f32[1,2,64,256]{3,2,1,0:T(8,128)S(1)} %convolution_bitcast_fusion.2, bf16[64,1,2,256]{3,0,2,1:T(8,128)(2,1)} %collective-permute-done.3, ...), kind=kLoop, calls=%fused_computation.4 | loop fusion | flops 5898240 | bytes 4718866 | tf_op jit(solution)/shard_map/convert_element_type | solution.py:106
  37.5 0.2 fusion.9
  37.8 0.1 pad_maximum_fusion
  37.9 1.3 %copy.272 = bf16[4,6,2,64,256]{4,3,1,0,2:T(8,128)(2,1)} copy(bf16[4,6,2,64,256]{4,3,2,1,0:T(8,128)(2,1)S(1)} %pad_maximum_fusion) | data formatting | bytes 3145728 | tf_op jit(solution)/shard_map/concatenate | solution.py:111
  39.2 7.3 %all-to-all-start.1 = ((bf16[8,6,64,256]{3,2,1,0:T(8,128)(2,1)}), bf16[8,6,64,256]{3,2,1,0:T(8,128)(2,1)S(1)}, u32[]{:S(2)}, u32[]{:S(2)}) async-start(bf16[8,6,64,256]{3,2,1,0:T(8,128)(2,1)} %bitcast.46), calls=%async_computation.1 | async-start | bytes 3145728 | tf_op jit(solution)/shard_map/all_to_all | solution.py:113
  46.6 0.2 broadcast_in_dim_tile.4.bias_ref
  46.8 2.5 %reshape.57 = bf16[8,9,64,64]{3,2,1,0:T(8,128)(2,1)S(1)} reshape(bf16[8,2,18432]{2,1,0:T(2,128)(2,1)} %copy-done) | data formatting | bytes 1179648
  49.3 0.1 slice.161
  49.4 1.7 %maximum_maximum_fusion.pairs_ref = bf16[8,9,64,128]{3,2,1,0:T(8,128)(2,1)} fusion(bf16[7,9,64,64]{3,2,1,0:T(8,128)(2,1)S(1)} %slice.161, bf16[1,9,64,64]{3,2,1,0:T(8,128)(2,1)S(1)} %slice.160, bf16[8,9,64,64]{3,2,1,0:T(8,128)(2,1)S(1)} %reshape.57), kind=kLoop, calls=%fused_computation.7 | loop fusion | flops 3538944 | bytes 2359296 | tf_op jit(solution)/shard_map/concatenate | solution.py:31
  51.0 4.2 %shard_map.64.bank_ref = bf16[9,512,512]{2,1,0:T(8,128)(2,1)} custom-call(bf16[8,9,64,128]{3,2,1,0:T(8,128)(2,1)} %maximum_maximum_fusion.pairs_ref), custom_call_target="tpu_custom_call" | custom-call | tf_op jit(solution)/shard_map/pallas_call | solution.py:32
  55.3 12.8 %all-to-all-done.1.x_ref = bf16[8,6,64,256]{3,2,1,0:T(8,128)(2,1)S(1)} async-done(((bf16[8,6,64,256]{3,2,1,0:T(8,128)(2,1)}), bf16[8,6,64,256]{3,2,1,0:T(8,128)(2,1)S(1)}, u32[]{:S(2)}, u32[]{:S(2)}) %all-to-all-start.1) | async-done | bytes 1572896 | tf_op jit(solution)/shard_map/all_to_all | solution.py:113
  68.0 8.2 %shard_map.65 = bf16[8,4,64,256]{3,2,1,0:T(8,128)(2,1)S(1)} custom-call(bf16[9,512,512]{2,1,0:T(8,128)(2,1)} %shard_map.64.bank_ref, f32[512,1]{1,0:T(8,128)S(1)} %broadcast_in_dim_tile.4.bias_ref, bf16[8,6,64,256]{3,2,1,0:T(8,128)(2,1)S(1)} %all-to-all-done.1.x_ref), custom_call_target="tpu_custom_call" | custom-call | tf_op jit(solution)/shard_map/pallas_call | solution.py:62
  76.3 22.7 %all_to_all.15 = bf16[8,4,64,256]{3,2,1,0:T(8,128)(2,1)S(1)} all-to-all(bf16[8,4,64,256]{3,2,1,0:T(8,128)(2,1)S(1)} %shard_map.65), channel_id=1, replica_groups=mesh['rot'=8,'space'=32] {'rot'}, dimensions={0} | all-to-all | bytes 2097152 | tf_op jit(solution)/shard_map/all_to_all | solution.py:120
  98.9 2.1 %copy.252 = bf16[64,4,4,2,256]{4,3,2,1,0:T(2,128)(2,1)} copy(bf16[64,4,4,2,256]{4,0,2,1,3:T(8,128)(2,1)S(1)} %bitcast.132) | data formatting | bytes 2097152 | tf_op jit(solution)/shard_map/transpose | solution.py:122
  (38 shorter events, 0.3 us)
Async XLA Ops:
  0.0 14.4 %copy-start.2 = (bf16[1,9,64,64]{3,2,1,0:T(8,128)(2,1)S(1)}, bf16[1,9,64,64]{3,2,1,0:T(8,128)(2,1)}, u32[]{:S(2)}) copy-start(bf16[1,9,64,64]{3,2,1,0:T(8,128)(2,1)} %param.10) | copy-start | bytes 221188
  0.8 22.7 %collective-permute-start = (bf16[4,2,2,256]{3,2,0,1:T(2,128)(2,1)S(1)}, bf16[4,2,2,256]{3,2,0,1:T(2,128)(2,1)S(1)}, u32[]{:S(2)}, u32[]{:S(2)}) collective-permute-start(bf16[4,2,2,256]{3,2,0,1:T(2,128)(2,1)S(1)} %get-tuple-element.27), channel_id=1, source_target_pairs={{0,1},{1,2},{2,3},{3,4},{4,5},{5,6},{6,7},{7,8},{8,9},{9,10},{10,1... | collective-permute-start | bytes 24584 | tf_op jit(solution)/shard_map/ppermute | solution.py:15
  2.7 20.8 %collective-permute-start.1 = (bf16[4,2,2,256]{3,2,0,1:T(2,128)(2,1)S(1)}, bf16[4,2,2,256]{3,2,0,1:T(2,128)(2,1)S(1)}, u32[]{:S(2)}, u32[]{:S(2)}) collective-permute-start(bf16[4,2,2,256]{3,2,0,1:T(2,128)(2,1)S(1)} %get-tuple-element.28), channel_id=1, source_target_pairs={{1,0},{2,1},{3,2},{4,3},{5,4},{6,5},{7,6},{8,7},{9,8},{10,9},{11,1... | collective-permute-start | bytes 24584 | tf_op jit(solution)/shard_map/ppermute | solution.py:16
  8.8 27.2 %collective-permute-start.2 = (bf16[64,1,2,256]{3,0,2,1:T(8,128)(2,1)}, bf16[64,1,2,256]{3,0,2,1:T(8,128)(2,1)}, u32[]{:S(2)}, u32[]{:S(2)}) collective-permute-start(bf16[64,1,2,256]{3,0,2,1:T(8,128)(2,1)} %get-tuple-element.7), channel_id=1, source_target_pairs={{0,1},{1,2},{2,3},{3,4},{4,5},{5,6},{6,7},{7,8},{8,9},{9,10},{10,1... | collective-permute-start | bytes 196616 | tf_op jit(solution)/shard_map/ppermute | solution.py:15
  12.2 23.8 %collective-permute-start.3 = (bf16[64,1,2,256]{3,0,2,1:T(8,128)(2,1)}, bf16[64,1,2,256]{3,0,2,1:T(8,128)(2,1)}, u32[]{:S(2)}, u32[]{:S(2)}) collective-permute-start(bf16[64,1,2,256]{3,0,2,1:T(8,128)(2,1)} %get-tuple-element.8), channel_id=1, source_target_pairs={{1,0},{2,1},{3,2},{4,3},{5,4},{6,5},{7,6},{8,7},{9,8},{10,9},{11,1... | collective-permute-start | bytes 196616 | tf_op jit(solution)/shard_map/ppermute | solution.py:16
  14.7 8.6 %copy-start.1 = (bf16[4,16,2,256]{3,2,1,0:T(2,128)(2,1)S(1)}, bf16[4,16,2,256]{3,2,1,0:T(2,128)(2,1)}, u32[]{:S(2)}) copy-start(bf16[4,16,2,256]{3,2,1,0:T(2,128)(2,1)} %param.6) | copy-start | bytes 196612
  14.7 8.6 %copy-start.5 = (bf16[1,9,64,4]{2,3,1,0:T(4,128)(2,1)S(1)}, bf16[1,9,64,4]{2,3,1,0:T(4,128)(2,1)}, u32[]{:S(2)}) copy-start(bf16[1,9,64,4]{2,3,1,0:T(4,128)(2,1)} %param.8) | copy-start | bytes 13828
  16.3 22.9 %all-to-all-start = ((bf16[8,2,18432]{2,1,0:T(2,128)(2,1)}), bf16[8,2,18432]{2,1,0:T(2,128)(2,1)S(1)}, u32[]{:S(2)}, u32[]{:S(2)}) async-start(bf16[8,2,18432]{2,1,0:T(2,128)(2,1)} %reshape.56), calls=%async_computation | async-start | bytes 1179648 | tf_op jit(solution)/shard_map/all_to_all | solution.py:116
  23.4 1.3 %copy-start.3 = (bf16[4,2,2,256]{3,2,0,1:T(2,128)(2,1)}, bf16[4,2,2,256]{3,2,0,1:T(2,128)(2,1)S(1)}, u32[]{:S(2)}) copy-start(bf16[4,2,2,256]{3,2,0,1:T(2,128)(2,1)S(1)} %collective-permute-done) | copy-start | bytes 24580
  23.5 1.3 %copy-start.4 = (bf16[4,2,2,256]{3,2,0,1:T(2,128)(2,1)}, bf16[4,2,2,256]{3,2,0,1:T(2,128)(2,1)S(1)}, u32[]{:S(2)}) copy-start(bf16[4,2,2,256]{3,2,0,1:T(2,128)(2,1)S(1)} %collective-permute-done.1) | copy-start | bytes 24580
  24.6 0.6 copy-start.6
  34.6 1.2 %copy-start.7 = (bf16[9,4,1,2,256]{4,3,1,2,0:T(2,128)(2,1)S(1)}, bf16[9,4,1,2,256]{4,3,1,2,0:T(2,128)(2,1)}, u32[]{:S(2)}) copy-start(bf16[9,4,1,2,256]{4,3,1,2,0:T(2,128)(2,1)} %copy-done.6) | copy-start | bytes 110596
  34.6 1.4 %copy-start.8 = (f32[64]{0:T(128)S(1)}, f32[64]{0:T(128)}, u32[]{:S(2)}) copy-start(f32[64]{0:T(128)} %param.9) | copy-start | bytes 772
  39.2 7.4 %copy-start = (bf16[8,2,18432]{2,1,0:T(2,128)(2,1)}, bf16[8,2,18432]{2,1,0:T(2,128)(2,1)S(1)}, u32[]{:S(2)}) copy-start(bf16[8,2,18432]{2,1,0:T(2,128)(2,1)S(1)} %all-to-all-done) | copy-start | bytes 1769476
  39.2 7.3 %copy-start.9 = (f32[64]{0:T(128)S(1)}, f32[64]{0:T(128)}, u32[]{:S(2)}) copy-start(f32[64]{0:T(128)} %param.11) | copy-start | bytes 772
  39.2 28.8 %all-to-all-start.1 = ((bf16[8,6,64,256]{3,2,1,0:T(8,128)(2,1)}), bf16[8,6,64,256]{3,2,1,0:T(8,128)(2,1)S(1)}, u32[]{:S(2)}, u32[]{:S(2)}) async-start(bf16[8,6,64,256]{3,2,1,0:T(8,128)(2,1)} %bitcast.46), calls=%async_computation.1 | async-start | bytes 3145728 | tf_op jit(solution)/shard_map/all_to_all | solution.py:113

commit v4 on v3

--- a/solution.py
+++ b/solution.py
@@ -112,8 +112,9 @@
     windows = jnp.transpose(windows, (2, 0, 1, 3, 4)).reshape((n, span + 2) + hidden_ext.shape[2:])
     gathered = lax.all_to_all(windows, "rot", 0, 0)
 
-    spread = jnp.broadcast_to(group_weight, (n,) + group_weight.shape[1:])
-    filters = lax.all_to_all(spread, "rot", 0, 0)
+    slots = jnp.zeros((n,) + group_weight.shape[1:], group_weight.dtype)
+    slots = lax.dynamic_update_index_in_dim(slots, group_weight[0], lax.axis_index("rot"), 0)
+    filters = lax.psum(slots, "rot")
     bias = jnp.tile(group_bias, n)[:, None]
     mixed = group_mix(circulant_bank(filters), bias, gathered)
 

time: 102 us -> 180 us (1.76)
  waiting for transfers between devices: 12.8 us -> 99.9 us
  between operations: 0.37 us -> 13.8 us
  local copies, waits for them, and re-layouts: 22.2 us -> 13.8 us
  starting transfers between devices: 25.4 us -> 18.2 us
  blocking collectives: 22.7 us -> 16.3 us
    psum x0 -> x1, waiting for transfers between devices: none -> 99.9 us  [shards(): filters = lax.psum(slots, 'rot')]
    all_to_all x1, waiting for transfers between devices: 12.8 us -> 0.01 us  [shards(): gathered = lax.all_to_all(windows, 'rot', 0, 0)]
    all_to_all x1 -> x0, starting transfers between devices: 6.93 us -> none  [shards(): filters = lax.all_to_all(spread, 'rot', 0, 0)]
    all_to_all x1, blocking collectives: 22.7 us -> 16.3 us  [shards(): returned = lax.all_to_all(mixed, 'rot', 0, 0)]
    another operation x13, local copies, waits for them, and re-layouts: 8.41 us -> 3.25 us  [lift(): jnp.stack([raster_padded[:, first + dy:first + dy + count, :, dx:dx + col...]
    unnamed x35 -> x27, local copies, waits for them, and re-layouts: 6.73 us -> 4.53 us
  transfers between devices with their start and end apart: 6 -> 6, of which waited for: 1 -> 1; matrix products, arithmetic and copies ran while one was open for 24% -> 5% of each run, Pallas kernels for 4% -> 2%
where the time goes in v4:
time: 180 us; the launch traced here: 179 us
  waiting for transfers between devices  99.9 us (56%)
  starting transfers between devices  18.2 us (10%)
  blocking collectives  16.3 us (9%)
  local copies, waits for them, and re-layouts  13.8 us (8%)
  between operations  13.8 us (8%)
  Pallas kernels  12.5 us (7%)
  other arithmetic  3.52 us (2%)
    psum x1, waiting for transfers between devices, shards(): filters = lax.psum(slots, 'rot')  99.9 us
    all_to_all x1, blocking collectives, shards(): returned = lax.all_to_all(mixed, 'rot', 0, 0)  16.3 us
    pallas_call x1, Pallas kernels, group_mix(): pl.pallas_call(mixing_kernel, grid=(rows_out,), in_specs=[pl.BlockSpec((9...  8.25 us
    all_to_all x1, starting transfers between devices, shards(): gathered = lax.all_to_all(windows, 'rot', 0, 0)  7.06 us
    ppermute x2, starting transfers between devices, padded_rows(): after = lax.ppermute(leading, axis, down)  5.79 us
    ppermute x2, starting transfers between devices, padded_rows(): before = lax.ppermute(last, axis, up)  5.33 us
    unnamed x27, local copies, waits for them, and re-layouts  4.53 us
    pallas_call x1, Pallas kernels, circulant_bank(): pl.pallas_call(bank_kernel, out_shape=jax.ShapeDtypeStruct((taps, count *...  4.22 us
  transfers between devices with their start and end apart: 6, of which 1 were waited for; matrix products, arithmetic and copies ran while one was open for 5% of the time, Pallas kernels for 2%

profile of v4, /device:TPU:96, one launch (start us, length us, event | category | flops | bytes accessed | tf_op | source)
XLA Modules:
  0.0 178.8 jit_solution(11319440780429107910)
XLA Ops:
  6.5 0.8 fusion.11
  7.3 1.9 %collective-permute-start = (bf16[4,2,2,256]{3,2,0,1:T(2,128)(2,1)S(1)}, bf16[4,2,2,256]{3,2,0,1:T(2,128)(2,1)S(1)}, u32[]{:S(2)}, u32[]{:S(2)}) collective-permute-start(bf16[4,2,2,256]{3,2,0,1:T(2,128)(2,1)S(1)} %get-tuple-element.27), channel_id=1, source_target_pairs={{0,1},{1,2},{2,3},{3,4},{4,5},{5,6},{6,7},{7,8},{8,9},{9,10},{10,1... | collective-permute-start | bytes 24584 | tf_op jit(solution)/shard_map/ppermute | solution.py:15
  9.3 3.6 %collective-permute-start.1 = (bf16[4,2,2,256]{3,2,0,1:T(2,128)(2,1)S(1)}, bf16[4,2,2,256]{3,2,0,1:T(2,128)(2,1)S(1)}, u32[]{:S(2)}, u32[]{:S(2)}) collective-permute-start(bf16[4,2,2,256]{3,2,0,1:T(2,128)(2,1)S(1)} %get-tuple-element.28), channel_id=1, source_target_pairs={{1,0},{2,1},{3,2},{4,3},{5,4},{6,5},{7,6},{8,7},{9,8},{10,9},{11,1... | collective-permute-start | bytes 24584 | tf_op jit(solution)/shard_map/ppermute | solution.py:16
  12.9 1.8 %copy.288 = bf16[1,64,16,2,256]{4,1,3,2,0:T(8,128)(2,1)S(1)} copy(bf16[1,64,16,2,256]{4,3,2,1,0:T(2,128)(2,1)} %param.7) | data formatting | bytes 2097152 | tf_op args[1]
  14.7 0.6 fusion.10
  15.4 3.4 %collective-permute-start.2 = (bf16[64,1,2,256]{3,0,2,1:T(8,128)(2,1)}, bf16[64,1,2,256]{3,0,2,1:T(8,128)(2,1)S(1)}, u32[]{:S(2)}, u32[]{:S(2)}) collective-permute-start(bf16[64,1,2,256]{3,0,2,1:T(8,128)(2,1)} %get-tuple-element.7), channel_id=1, source_target_pairs={{0,1},{1,2},{2,3},{3,4},{4,5},{5,6},{6,7},{7,8},{8,9},{9,10},{10,1... | collective-permute-start | bytes 196616 | tf_op jit(solution)/shard_map/ppermute | solution.py:15
  18.8 2.1 %collective-permute-start.3 = (bf16[64,1,2,256]{3,0,2,1:T(8,128)(2,1)}, bf16[64,1,2,256]{3,0,2,1:T(8,128)(2,1)}, u32[]{:S(2)}, u32[]{:S(2)}) collective-permute-start(bf16[64,1,2,256]{3,0,2,1:T(8,128)(2,1)} %get-tuple-element.8), channel_id=1, source_target_pairs={{1,0},{2,1},{3,2},{4,3},{5,4},{6,5},{7,6},{8,7},{9,8},{10,9},{11,1... | collective-permute-start | bytes 196616 | tf_op jit(solution)/shard_map/ppermute | solution.py:16
  21.0 0.1 copy.240
  21.1 0.2 select_maximum_fusion
  21.4 0.3 slice_bitcast_fusion
  21.8 0.1 constant_dynamic-update-slice_fusion.6
  21.9 0.1 constant_dynamic-update-slice_fusion.5
  22.0 0.1 constant_dynamic-update-slice_fusion.3
  22.1 0.1 constant_dynamic-update-slice_fusion.2
  22.1 0.1 constant_dynamic-update-slice_fusion
  22.2 0.1 constant_dynamic-update-slice_fusion.9
  22.3 0.1 copy.236
  22.4 0.1 copy.238
  22.5 0.1 copy.239
  22.7 0.1 copy.241
  22.8 0.1 copy.242
  22.9 0.1 copy.244
  23.0 0.1 fusion.4
  23.1 0.1 copy.237
  23.2 0.1 copy.243
  23.3 0.2 convolution_bitcast_fusion.1
  23.5 1.8 %stack.109 = bf16[9,4,16,2,256]{4,0,1,3,2:T(8,128)(2,1)S(1)} concatenate(bf16[1,4,16,2,256]{4,0,1,3,2:T(2,128)(2,1)S(1)} %copy.236, bf16[1,4,16,2,256]{4,0,1,3,2:T(2,128)(2,1)S(1)} %copy.237, bf16[1,4,16,2,256]{4,0,1,3,2:T(2,128)(2,1)S(1)} %copy.238, bf16[1,4,16,2,256]{4,0,1,3,2:T(2,128)(2,1)S(1)} %copy.239, bf16[1,4,16,2,256]{4,0,1,3,2:T(2,128)(2,1)S(1)} %copy.240, ...), dimensions={0} | concatenate | bytes 1179648 | tf_op jit(solution)/shard_map/stack | solution.py:91
  25.3 0.0 copy-start.5
  25.3 0.5 convolution_bitcast_fusion
  25.8 0.2 convolution_bitcast_fusion.2
  26.1 1.4 fusion.3
  27.5 0.2 fusion.9
  27.8 0.1 pad_maximum_fusion
  27.9 1.3 copy.272
  29.3 7.1 %all-to-all-start = ((bf16[8,6,64,256]{3,2,1,0:T(8,128)(2,1)}), bf16[8,6,64,256]{3,2,1,0:T(8,128)(2,1)S(1)}, u32[]{:S(2)}, u32[]{:S(2)}) async-start(bf16[8,6,64,256]{3,2,1,0:T(8,128)(2,1)} %bitcast.45), calls=%async_computation | async-start | bytes 3145728 | tf_op jit(solution)/shard_map/all_to_all | solution.py:113
  36.3 0.0 all-reduce.3.cloned.1.call-start
  36.4 0.3 broadcast_in_dim.16
  36.7 1.0 copy-done.1
  37.7 0.0 all-reduce.3.cloned.1.call-update
  37.8 0.2 broadcast_in_dim_tile.4.bias_ref
  38.0 99.9 %all-reduce.3.cloned.1.call-done = bf16[8,9,64,64]{3,2,1,0:T(8,128)(2,1)} async-done(((bf16[8,9,64,64]{3,2,1,0:T(8,128)(2,1)}), bf16[8,9,64,64]{3,2,1,0:T(8,128)(2,1)}) %all-reduce.3.cloned.1.call-update) | async-done | bytes 589840 | tf_op jit(solution)/shard_map/psum | solution.py:117
  137.8 1.3 copy-done
  139.1 0.4 slice-done
  139.5 1.7 maximum_maximum_fusion.pairs_ref
  141.2 4.2 %shard_map.64.bank_ref = bf16[9,512,512]{2,1,0:T(8,128)(2,1)} custom-call(bf16[8,9,64,128]{3,2,1,0:T(8,128)(2,1)} %maximum_maximum_fusion.pairs_ref), custom_call_target="tpu_custom_call" | custom-call | tf_op jit(solution)/shard_map/pallas_call | solution.py:32
  145.4 8.2 %shard_map.65 = bf16[8,4,64,256]{3,2,1,0:T(8,128)(2,1)S(1)} custom-call(bf16[9,512,512]{2,1,0:T(8,128)(2,1)} %shard_map.64.bank_ref, f32[512,1]{1,0:T(8,128)S(1)} %broadcast_in_dim_tile.4.bias_ref, bf16[8,6,64,256]{3,2,1,0:T(8,128)(2,1)S(1)} %all-to-all-done.x_ref), custom_call_target="tpu_custom_call" | custom-call | tf_op jit(solution)/shard_map/pallas_call | solution.py:62
  153.6 16.3 %all_to_all.10 = bf16[8,4,64,256]{3,2,1,0:T(8,128)(2,1)S(1)} all-to-all(bf16[8,4,64,256]{3,2,1,0:T(8,128)(2,1)S(1)} %shard_map.65), channel_id=1, replica_groups=mesh['rot'=8,'space'=32] {'rot'}, dimensions={0} | all-to-all | bytes 2097152 | tf_op jit(solution)/shard_map/all_to_all | solution.py:121
  169.9 2.1 %copy.252 = bf16[64,4,4,2,256]{4,3,2,1,0:T(2,128)(2,1)} copy(bf16[64,4,4,2,256]{4,0,2,1,3:T(8,128)(2,1)S(1)} %bitcast.131) | data formatting | bytes 2097152 | tf_op jit(solution)/shard_map/transpose | solution.py:123
  (34 shorter events, 0.2 us)
Async XLA Ops:
  6.5 14.4 %copy-start.2 = (bf16[4,16,2,256]{3,2,1,0:T(2,128)(2,1)S(1)}, bf16[4,16,2,256]{3,2,1,0:T(2,128)(2,1)}, u32[]{:S(2)}) copy-start(bf16[4,16,2,256]{3,2,1,0:T(2,128)(2,1)} %param.6) | copy-start | bytes 196612
  6.5 14.4 %copy-start.4 = (bf16[1,9,64,4]{2,3,1,0:T(4,128)(2,1)S(1)}, bf16[1,9,64,4]{2,3,1,0:T(4,128)(2,1)}, u32[]{:S(2)}) copy-start(bf16[1,9,64,4]{2,3,1,0:T(4,128)(2,1)} %param.8) | copy-start | bytes 13828
  7.3 13.8 %collective-permute-start = (bf16[4,2,2,256]{3,2,0,1:T(2,128)(2,1)S(1)}, bf16[4,2,2,256]{3,2,0,1:T(2,128)(2,1)S(1)}, u32[]{:S(2)}, u32[]{:S(2)}) collective-permute-start(bf16[4,2,2,256]{3,2,0,1:T(2,128)(2,1)S(1)} %get-tuple-element.27), channel_id=1, source_target_pairs={{0,1},{1,2},{2,3},{3,4},{4,5},{5,6},{6,7},{7,8},{8,9},{9,10},{10,1... | collective-permute-start | bytes 24584 | tf_op jit(solution)/shard_map/ppermute | solution.py:15
  9.3 11.9 %collective-permute-start.1 = (bf16[4,2,2,256]{3,2,0,1:T(2,128)(2,1)S(1)}, bf16[4,2,2,256]{3,2,0,1:T(2,128)(2,1)S(1)}, u32[]{:S(2)}, u32[]{:S(2)}) collective-permute-start(bf16[4,2,2,256]{3,2,0,1:T(2,128)(2,1)S(1)} %get-tuple-element.28), channel_id=1, source_target_pairs={{1,0},{2,1},{3,2},{4,3},{5,4},{6,5},{7,6},{8,7},{9,8},{10,9},{11,1... | collective-permute-start | bytes 24584 | tf_op jit(solution)/shard_map/ppermute | solution.py:16
  15.4 10.7 %collective-permute-start.2 = (bf16[64,1,2,256]{3,0,2,1:T(8,128)(2,1)}, bf16[64,1,2,256]{3,0,2,1:T(8,128)(2,1)S(1)}, u32[]{:S(2)}, u32[]{:S(2)}) collective-permute-start(bf16[64,1,2,256]{3,0,2,1:T(8,128)(2,1)} %get-tuple-element.7), channel_id=1, source_target_pairs={{0,1},{1,2},{2,3},{3,4},{4,5},{5,6},{6,7},{7,8},{8,9},{9,10},{10,1... | collective-permute-start | bytes 196616 | tf_op jit(solution)/shard_map/ppermute | solution.py:15
  18.8 7.3 %collective-permute-start.3 = (bf16[64,1,2,256]{3,0,2,1:T(8,128)(2,1)}, bf16[64,1,2,256]{3,0,2,1:T(8,128)(2,1)}, u32[]{:S(2)}, u32[]{:S(2)}) collective-permute-start(bf16[64,1,2,256]{3,0,2,1:T(8,128)(2,1)} %get-tuple-element.8), channel_id=1, source_target_pairs={{1,0},{2,1},{3,2},{4,3},{5,4},{6,5},{7,6},{8,7},{9,8},{10,9},{11,1... | collective-permute-start | bytes 196616 | tf_op jit(solution)/shard_map/ppermute | solution.py:16
  25.3 0.7 copy-start.5
  29.3 7.4 %copy-start.3 = (bf16[1,9,64,64]{3,2,1,0:T(8,128)(2,1)S(1)}, bf16[1,9,64,64]{3,2,1,0:T(8,128)(2,1)}, u32[]{:S(2)}) copy-start(bf16[1,9,64,64]{3,2,1,0:T(8,128)(2,1)} %param.10) | copy-start | bytes 221188
  29.3 116.1 %all-to-all-start = ((bf16[8,6,64,256]{3,2,1,0:T(8,128)(2,1)}), bf16[8,6,64,256]{3,2,1,0:T(8,128)(2,1)S(1)}, u32[]{:S(2)}, u32[]{:S(2)}) async-start(bf16[8,6,64,256]{3,2,1,0:T(8,128)(2,1)} %bitcast.45), calls=%async_computation | async-start | bytes 3145728 | tf_op jit(solution)/shard_map/all_to_all | solution.py:113
  36.3 1.4 copy-start.6
  36.3 101.5 %all-reduce.3.cloned.1.call-start = ((), (), s32[]{:S(2)}) async-start(), calls=%async_computation.2 | async-start | bytes 2359296 | tf_op jit(solution)/shard_map/psum | solution.py:117
  36.7 1.0 copy-start.1
  137.8 1.3 copy-start
  137.8 1.7 slice-start
  137.8 1.7 slice-start.1
Sparse Core Ops, SparseCore 0:
  39.8 98.0 all-reduce.2

commit v5 on v2

--- a/solution.py
+++ b/solution.py
@@ -84,12 +84,23 @@
     span = rows // quarters
     space = lax.axis_index("space")
 
-    raster_padded = jnp.pad(padded_rows(raster, "space", 1, 2), ((0, 0), (0, 0), (0, 0), (1, 1)))
-    taps = jnp.stack(
-        [raster_padded[:, dy : dy + rows + 2, :, dx : dx + cols] for dy in range(3) for dx in range(3)], 0
-    ).reshape((-1, rows + 2) + raster.shape[2:])
     lift_matrix = jnp.transpose(lift_weight[0], (1, 0, 2)).reshape(channels, -1)
-    lifted = jnp.einsum("ok,krtw->rtow", lift_matrix, taps, preferred_element_type=jnp.float32)
+    size = lax.axis_size("space")
+    above = lax.ppermute(raster[:, rows - 2 :], "space", [(i, i + 1) for i in range(size - 1)])
+    below = lax.ppermute(raster[:, :2], "space", [(i + 1, i) for i in range(size - 1)])
+
+    def lift(source):
+        count = source.shape[1] - 2
+        widened = jnp.transpose(jnp.pad(source, ((0, 0), (0, 0), (0, 0), (1, 1))), (1, 2, 0, 3))
+        taps = jnp.concatenate(
+            [widened[dy : dy + count, :, :, dx : dx + cols] for dy in range(3) for dx in range(3)], 2
+        )
+        return jnp.einsum("ok,rtkw->rtow", lift_matrix, taps, preferred_element_type=jnp.float32)
+
+    body = jnp.concatenate([above[:, 1:], raster, below[:, :1]], axis=1)
+    first = jnp.concatenate([above, raster[:, :1]], axis=1)
+    last = jnp.concatenate([raster[:, rows - 1 :], below], axis=1)
+    lifted = jnp.concatenate([lift(first), lift(body), lift(last)], axis=0)
     coarse = jnp.transpose(padded_rows(coarse_features[0], "space", 1, 1), (1, 2, 0, 3))
     lifted = lifted + lift_bias[None, None, :, None] + coarse.astype(jnp.float32)
     line = lax.broadcasted_iota(jnp.int32, (rows + 2, 1, 1, 1), 0)

time: 102 us -> 97.4 us (0.955)
  local copies, waits for them, and re-layouts: 23.4 us -> 17.4 us
  other arithmetic: 2.5 us -> 3.94 us
    another operation x11 -> x0, local copies, waits for them, and re-layouts: 11.6 us -> none  [shards(): jnp.stack([raster_padded[:, dy:dy + rows + 2, :, dx:dx + cols] for dy in...]
    ppermute x0 -> x2, starting transfers between devices: none -> 5.56 us  [the longest x1 3.64 us: shards(): lax.ppermute(raster[:, :2], 'space', [(i + 1, i) for i in range(size - 1)])]
    concatenate x1 -> x3, local copies, waits for them, and re-layouts: 0.02 us -> 4.57 us  [lift(): jnp.concatenate([widened[dy:dy + count, :, :, dx:dx + cols] for dy in ran...]
    ppermute x2 -> x1, starting transfers between devices: 5.79 us -> 2.14 us  [padded_rows(): after = lax.ppermute(leading, axis, down)]
    ppermute x2 -> x1, starting transfers between devices: 5.34 us -> 3.41 us  [padded_rows(): before = lax.ppermute(last, axis, up)]
    convert_element_type x0 -> x1, other arithmetic: none -> 1.31 us  [shards(): jnp.where(inside, jnp.maximum(lifted, 0.0), 0.0).astype(jnp.bfloat16)]
    unnamed x17 -> x10, local copies, waits for them, and re-layouts: 6.81 us -> 6.83 us
  transfers between devices with their start and end apart: 6 -> 6, of which waited for: 1 -> 1; matrix products, arithmetic and copies ran while one was open for 24% -> 21% of each run, Pallas kernels for 4% -> 4%
where the time goes in v5:
time: 97.4 us; the launch traced here: 96.8 us
  starting transfers between devices  25.4 us (26%)
  blocking collectives  22.7 us (23%)
  local copies, waits for them, and re-layouts  17.4 us (18%)
  waiting for transfers between devices  12.8 us (13%)
  Pallas kernels  12.4 us (13%)
  other arithmetic  3.94 us (4%)
  matrix products  1.97 us (2%)
    all_to_all x1, blocking collectives, shards(): returned = lax.all_to_all(mixed, 'rot', 0, 0)  22.7 us
    all_to_all x1, waiting for transfers between devices, shards(): gathered = lax.all_to_all(windows, 'rot', 0, 0)  12.8 us
    pallas_call x1, Pallas kernels, group_mix(): pl.pallas_call(mixing_kernel, grid=(rows_out,), in_specs=[pl.BlockSpec((9...  8.25 us
    all_to_all x1, starting transfers between devices, shards(): gathered = lax.all_to_all(windows, 'rot', 0, 0)  7.34 us
    all_to_all x1, starting transfers between devices, shards(): filters = lax.all_to_all(spread, 'rot', 0, 0)  6.93 us
    unnamed x10, local copies, waits for them, and re-layouts  6.83 us
    concatenate x3, local copies, waits for them, and re-layouts, lift(): jnp.concatenate([widened[dy:dy + count, :, :, dx:dx + cols] for dy in ran...  4.57 us
    pallas_call x1, Pallas kernels, circulant_bank(): pl.pallas_call(bank_kernel, out_shape=jax.ShapeDtypeStruct((taps, count *...  4.2 us
  transfers between devices with their start and end apart: 6, of which 1 were waited for; matrix products, arithmetic and copies ran while one was open for 21% of the time, Pallas kernels for 4%

profile of v5, /device:TPU:96, one launch (start us, length us, event | category | flops | bytes accessed | tf_op | source)
XLA Modules:
  0.0 96.8 jit_solution(17267688897804980818)
XLA Ops:
  0.0 0.0 copy-start
  0.0 0.9 copy.16
  1.0 1.9 %collective-permute-start = (bf16[4,2,2,256]{3,0,2,1:T(4,128)(2,1)S(1)}, bf16[4,2,2,256]{3,0,2,1:T(4,128)(2,1)S(1)}, u32[]{:S(2)}, u32[]{:S(2)}) collective-permute-start(bf16[4,2,2,256]{3,0,2,1:T(4,128)(2,1)S(1)} %get-tuple-element.20), channel_id=1, source_target_pairs={{0,1},{1,2},{2,3},{3,4},{4,5},{5,6},{6,7},{7,8},{8,9},{9,10},{10,1... | collective-permute-start | bytes 24584 | tf_op jit(solution)/shard_map/ppermute | solution.py:89
  2.9 3.6 %collective-permute-start.1 = (bf16[4,2,2,256]{3,0,2,1:T(4,128)(2,1)S(1)}, bf16[4,2,2,256]{3,0,2,1:T(4,128)(2,1)S(1)}, u32[]{:S(2)}, u32[]{:S(2)}) collective-permute-start(bf16[4,2,2,256]{3,0,2,1:T(4,128)(2,1)S(1)} %get-tuple-element.21), channel_id=1, source_target_pairs={{1,0},{2,1},{3,2},{4,3},{5,4},{6,5},{7,6},{8,7},{9,8},{10,9},{11,1... | collective-permute-start | bytes 24584 | tf_op jit(solution)/shard_map/ppermute | solution.py:90
  6.5 1.8 %copy.30 = bf16[1,64,16,2,256]{4,1,3,2,0:T(8,128)(2,1)S(1)} copy(bf16[1,64,16,2,256]{4,3,2,1,0:T(2,128)(2,1)} %param.7) | data formatting | bytes 2097152 | tf_op args[1]
  8.3 0.6 fusion.13
  9.0 3.4 %collective-permute-start.2 = (bf16[64,1,2,256]{3,0,2,1:T(8,128)(2,1)}, bf16[64,1,2,256]{3,0,2,1:T(8,128)(2,1)S(1)}, u32[]{:S(2)}, u32[]{:S(2)}) collective-permute-start(bf16[64,1,2,256]{3,0,2,1:T(8,128)(2,1)} %get-tuple-element.7), channel_id=1, source_target_pairs={{0,1},{1,2},{2,3},{3,4},{4,5},{5,6},{6,7},{7,8},{8,9},{9,10},{10,1... | collective-permute-start | bytes 196616 | tf_op jit(solution)/shard_map/ppermute | solution.py:15
  12.4 2.1 %collective-permute-start.3 = (bf16[64,1,2,256]{3,0,2,1:T(8,128)(2,1)S(1)}, bf16[64,1,2,256]{3,0,2,1:T(8,128)(2,1)S(1)}, u32[]{:S(2)}, u32[]{:S(2)}) collective-permute-start(bf16[64,1,2,256]{3,0,2,1:T(8,128)(2,1)S(1)} %get-tuple-element.8), channel_id=1, source_target_pairs={{1,0},{2,1},{3,2},{4,3},{5,4},{6,5},{7,6},{8,7},{9,8},{10,9},{11,1... | collective-permute-start | bytes 196616 | tf_op jit(solution)/shard_map/ppermute | solution.py:16
  14.6 0.0 copy-done
  14.6 0.3 broadcast_in_dim.19
  14.8 0.0 copy-start.1
  14.9 1.6 %reshape.51 = bf16[8,2,18432]{2,1,0:T(2,128)(2,1)} reshape(bf16[8,9,64,64]{3,2,1,0:T(8,128)(2,1)S(1)} %broadcast_in_dim.19) | data formatting | bytes 1179648
  16.5 6.9 %all-to-all-start = ((bf16[8,2,18432]{2,1,0:T(2,128)(2,1)}), bf16[8,2,18432]{2,1,0:T(2,128)(2,1)}, u32[]{:S(2)}, u32[]{:S(2)}) async-start(bf16[8,2,18432]{2,1,0:T(2,128)(2,1)} %reshape.51), calls=%async_computation | async-start | bytes 1179648 | tf_op jit(solution)/shard_map/all_to_all | solution.py:118
  23.4 0.6 or_and_fusion
  24.0 0.0 copy-done.1
  24.0 0.0 collective-permute-done
  24.1 0.0 collective-permute-done.1
  24.1 0.1 fusion.5
  24.2 0.3 fusion.14
  24.5 0.1 fusion.9
  24.6 0.1 fusion.18
  24.7 0.7 fusion.17
  25.4 3.7 %concatenate.39 = bf16[16,2,36,256]{3,2,1,0:T(8,128)(2,1)} concatenate(bf16[16,2,4,256]{3,2,1,0:T(4,128)(2,1)S(1)} %get-tuple-element.17, bf16[16,2,4,256]{3,2,1,0:T(4,128)(2,1)S(1)} %get-tuple-element.16, bf16[16,2,4,256]{3,2,1,0:T(4,128)(2,1)S(1)} %get-tuple-element.15, bf16[16,2,4,256]{3,2,1,0:T(4,128)(2,1)S(1)} %get-tuple-element.14, ...), dimensions={2} | concatenate | bytes 1179648 | tf_op jit(solution)/shard_map/concatenate | solution.py:95
  29.1 1.6 %convolution_bitcast_fusion = f32[16,2,64,256]{3,2,1,0:T(8,128)S(1)} fusion(bf16[16,2,36,256]{3,2,1,0:T(8,128)(2,1)} %concatenate.39, bf16[64,36,1,1]{0,1,2,3:T(8,128)(2,1)S(1)} %reshape.48), kind=kOutput, calls=%fused_computation.5 | convolution fusion | flops 37748736 | bytes 2691584 | tf_op jit(solution)/shard_map/ok,rtkw->rtow/dot_general | solution.py:98
  30.6 0.1 concatenate.41
  30.7 0.2 convolution_bitcast_fusion.1
  30.9 0.8 concatenate.37
  31.7 0.2 convolution_bitcast_fusion.2
  31.9 0.0 collective-permute-done.2
  31.9 0.0 collective-permute-done.3
  32.0 1.3 %fusion.3 = bf16[18,2,64,256]{3,2,1,0:T(8,128)(2,1)S(1)} fusion(f32[1,2,64,256]{3,2,1,0:T(8,128)S(1)} %convolution_bitcast_fusion.1, f32[16,2,64,256]{3,2,1,0:T(8,128)S(1)} %convolution_bitcast_fusion, f32[1,2,64,256]{3,2,1,0:T(8,128)S(1)} %convolution_bitcast_fusion.2, bf16[64,1,2,256]{3,0,2,1:T(8,128)(2,1)S(1)} %collective-permute-done.3, ...), kind=kLoop, calls=%fused_computation.4 | loop fusion | flops 5898240 | bytes 4718866 | tf_op jit(solution)/shard_map/convert_element_type | solution.py:108
  33.3 0.2 fusion.12
  33.6 0.1 pad_maximum_fusion
  33.7 1.3 %copy.28 = bf16[4,6,2,64,256]{4,3,1,0,2:T(8,128)(2,1)} copy(bf16[4,6,2,64,256]{4,3,2,1,0:T(8,128)(2,1)S(1)} %pad_maximum_fusion) | data formatting | bytes 3145728 | tf_op jit(solution)/shard_map/concatenate | solution.py:113
  35.0 0.0 all-to-all-done
  35.0 0.0 copy-start.2
  35.0 7.3 %all-to-all-start.1 = ((bf16[8,6,64,256]{3,2,1,0:T(8,128)(2,1)}), bf16[8,6,64,256]{3,2,1,0:T(8,128)(2,1)S(1)}, u32[]{:S(2)}, u32[]{:S(2)}) async-start(bf16[8,6,64,256]{3,2,1,0:T(8,128)(2,1)} %bitcast.20), calls=%async_computation.1 | async-start | bytes 3145728 | tf_op jit(solution)/shard_map/all_to_all | solution.py:115
  42.4 0.0 copy-done.2
  42.4 0.2 broadcast_in_dim_tile.4.bias_ref
  42.6 2.5 %reshape.52 = bf16[8,9,64,64]{3,2,1,0:T(8,128)(2,1)S(1)} reshape(bf16[8,2,18432]{2,1,0:T(2,128)(2,1)} %all-to-all-done) | data formatting | bytes 1179648
  45.1 0.1 slice.163
  45.2 1.7 %maximum_maximum_fusion.pairs_ref = bf16[8,9,64,128]{3,2,1,0:T(8,128)(2,1)} fusion(bf16[7,9,64,64]{3,2,1,0:T(8,128)(2,1)S(1)} %slice.163, bf16[1,9,64,64]{3,2,1,0:T(8,128)(2,1)S(1)} %slice.162, bf16[8,9,64,64]{3,2,1,0:T(8,128)(2,1)S(1)} %reshape.52), kind=kLoop, calls=%fused_computation.7 | loop fusion | flops 3538944 | bytes 2359296 | tf_op jit(solution)/shard_map/concatenate | solution.py:31
  46.8 4.2 %shard_map.64.bank_ref = bf16[9,512,512]{2,1,0:T(8,128)(2,1)} custom-call(bf16[8,9,64,128]{3,2,1,0:T(8,128)(2,1)} %maximum_maximum_fusion.pairs_ref), custom_call_target="tpu_custom_call" | custom-call | tf_op jit(solution)/shard_map/pallas_call | solution.py:32
  51.0 12.8 %all-to-all-done.1.x_ref = bf16[8,6,64,256]{3,2,1,0:T(8,128)(2,1)S(1)} async-done(((bf16[8,6,64,256]{3,2,1,0:T(8,128)(2,1)}), bf16[8,6,64,256]{3,2,1,0:T(8,128)(2,1)S(1)}, u32[]{:S(2)}, u32[]{:S(2)}) %all-to-all-start.1) | async-done | bytes 1572896 | tf_op jit(solution)/shard_map/all_to_all | solution.py:115
  63.8 8.2 %shard_map.65 = bf16[8,4,64,256]{3,2,1,0:T(8,128)(2,1)S(1)} custom-call(bf16[9,512,512]{2,1,0:T(8,128)(2,1)} %shard_map.64.bank_ref, f32[512,1]{1,0:T(8,128)S(1)} %broadcast_in_dim_tile.4.bias_ref, bf16[8,6,64,256]{3,2,1,0:T(8,128)(2,1)S(1)} %all-to-all-done.1.x_ref), custom_call_target="tpu_custom_call" | custom-call | tf_op jit(solution)/shard_map/pallas_call | solution.py:62
  72.1 22.7 %all_to_all.15 = bf16[8,4,64,256]{3,2,1,0:T(8,128)(2,1)S(1)} all-to-all(bf16[8,4,64,256]{3,2,1,0:T(8,128)(2,1)S(1)} %shard_map.65), channel_id=1, replica_groups=mesh['rot'=8,'space'=32] {'rot'}, dimensions={0} | all-to-all | bytes 2097152 | tf_op jit(solution)/shard_map/all_to_all | solution.py:122
  94.7 2.1 %copy.25 = bf16[64,4,4,2,256]{4,3,2,1,0:T(2,128)(2,1)} copy(bf16[64,4,4,2,256]{4,0,2,1,3:T(8,128)(2,1)S(1)} %bitcast.53) | data formatting | bytes 2097152 | tf_op jit(solution)/shard_map/transpose | solution.py:124
  (9 shorter events, 0.1 us)
Async XLA Ops:
  0.0 14.6 %copy-start = (bf16[1,9,64,64]{3,2,1,0:T(8,128)(2,1)S(1)}, bf16[1,9,64,64]{3,2,1,0:T(8,128)(2,1)}, u32[]{:S(2)}) copy-start(bf16[1,9,64,64]{3,2,1,0:T(8,128)(2,1)} %param.10) | copy-start | bytes 221188
  1.0 23.1 %collective-permute-start = (bf16[4,2,2,256]{3,0,2,1:T(4,128)(2,1)S(1)}, bf16[4,2,2,256]{3,0,2,1:T(4,128)(2,1)S(1)}, u32[]{:S(2)}, u32[]{:S(2)}) collective-permute-start(bf16[4,2,2,256]{3,0,2,1:T(4,128)(2,1)S(1)} %get-tuple-element.20), channel_id=1, source_target_pairs={{0,1},{1,2},{2,3},{3,4},{4,5},{5,6},{6,7},{7,8},{8,9},{9,10},{10,1... | collective-permute-start | bytes 24584 | tf_op jit(solution)/shard_map/ppermute | solution.py:89
  2.9 21.2 %collective-permute-start.1 = (bf16[4,2,2,256]{3,0,2,1:T(4,128)(2,1)S(1)}, bf16[4,2,2,256]{3,0,2,1:T(4,128)(2,1)S(1)}, u32[]{:S(2)}, u32[]{:S(2)}) collective-permute-start(bf16[4,2,2,256]{3,0,2,1:T(4,128)(2,1)S(1)} %get-tuple-element.21), channel_id=1, source_target_pairs={{1,0},{2,1},{3,2},{4,3},{5,4},{6,5},{7,6},{8,7},{9,8},{10,9},{11,1... | collective-permute-start | bytes 24584 | tf_op jit(solution)/shard_map/ppermute | solution.py:90
  9.0 23.0 %collective-permute-start.2 = (bf16[64,1,2,256]{3,0,2,1:T(8,128)(2,1)}, bf16[64,1,2,256]{3,0,2,1:T(8,128)(2,1)S(1)}, u32[]{:S(2)}, u32[]{:S(2)}) collective-permute-start(bf16[64,1,2,256]{3,0,2,1:T(8,128)(2,1)} %get-tuple-element.7), channel_id=1, source_target_pairs={{0,1},{1,2},{2,3},{3,4},{4,5},{5,6},{6,7},{7,8},{8,9},{9,10},{10,1... | collective-permute-start | bytes 196616 | tf_op jit(solution)/shard_map/ppermute | solution.py:15
  12.4 19.5 %collective-permute-start.3 = (bf16[64,1,2,256]{3,0,2,1:T(8,128)(2,1)S(1)}, bf16[64,1,2,256]{3,0,2,1:T(8,128)(2,1)S(1)}, u32[]{:S(2)}, u32[]{:S(2)}) collective-permute-start(bf16[64,1,2,256]{3,0,2,1:T(8,128)(2,1)S(1)} %get-tuple-element.8), channel_id=1, source_target_pairs={{1,0},{2,1},{3,2},{4,3},{5,4},{6,5},{7,6},{8,7},{9,8},{10,9},{11,1... | collective-permute-start | bytes 196616 | tf_op jit(solution)/shard_map/ppermute | solution.py:16
  14.8 9.2 %copy-start.1 = (bf16[1,9,64,4]{2,3,1,0:T(4,128)(2,1)S(1)}, bf16[1,9,64,4]{2,3,1,0:T(4,128)(2,1)}, u32[]{:S(2)}) copy-start(bf16[1,9,64,4]{2,3,1,0:T(4,128)(2,1)} %param.8) | copy-start | bytes 13828
  16.5 18.6 %all-to-all-start = ((bf16[8,2,18432]{2,1,0:T(2,128)(2,1)}), bf16[8,2,18432]{2,1,0:T(2,128)(2,1)}, u32[]{:S(2)}, u32[]{:S(2)}) async-start(bf16[8,2,18432]{2,1,0:T(2,128)(2,1)} %reshape.51), calls=%async_computation | async-start | bytes 1179648 | tf_op jit(solution)/shard_map/all_to_all | solution.py:118
  35.0 7.3 %copy-start.2 = (f32[64]{0:T(128)S(1)}, f32[64]{0:T(128)}, u32[]{:S(2)}) copy-start(f32[64]{0:T(128)} %param.11) | copy-start | bytes 772
  35.0 28.8 %all-to-all-start.1 = ((bf16[8,6,64,256]{3,2,1,0:T(8,128)(2,1)}), bf16[8,6,64,256]{3,2,1,0:T(8,128)(2,1)S(1)}, u32[]{:S(2)}, u32[]{:S(2)}) async-start(bf16[8,6,64,256]{3,2,1,0:T(8,128)(2,1)} %bitcast.20), calls=%async_computation.1 | async-start | bytes 3145728 | tf_op jit(solution)/shard_map/all_to_all | solution.py:115

commit v6 on v5

--- a/solution.py
+++ b/solution.py
@@ -4,17 +4,6 @@
 from jax.experimental import pallas as pl
 from jax.experimental.pallas import tpu as pltpu
 from jax.sharding import PartitionSpec as P
-
-
-def padded_rows(array, axis, dim, width):
-    size, length = lax.axis_size(axis), array.shape[dim]
-    up = [(i, i + 1) for i in range(size - 1)]
-    down = [(j, i) for i, j in up]
-    last = lax.slice_in_dim(array, length - width, length, axis=dim)
-    leading = lax.slice_in_dim(array, 0, width, axis=dim)
-    before = lax.ppermute(last, axis, up)
-    after = lax.ppermute(leading, axis, down)
-    return jnp.concatenate([before, array, after], axis=dim)
 
 
 def bank_kernel(pairs_ref, bank_ref):
@@ -73,11 +62,10 @@
     )(bank, bias, windows)
 
 
-def shards(raster, coarse_features, lift_weight, lift_bias, group_weight, group_bias):
+def layer(raster, coarse_features, lift_weight, lift_bias, group_weight, group_bias):
     n = lax.axis_size("rot")
     channels = lift_weight.shape[2]
     rows = raster.shape[1]
-    chunk = rows // n
 
     tiles, cols = raster.shape[2], raster.shape[3]
     quarters = n // tiles
@@ -86,8 +74,21 @@
 
     lift_matrix = jnp.transpose(lift_weight[0], (1, 0, 2)).reshape(channels, -1)
     size = lax.axis_size("space")
-    above = lax.ppermute(raster[:, rows - 2 :], "space", [(i, i + 1) for i in range(size - 1)])
-    below = lax.ppermute(raster[:, :2], "space", [(i + 1, i) for i in range(size - 1)])
+    coarse_own = coarse_features[0]
+    halo_shape = (-1,) + raster.shape[2:]
+
+    def edges(raster_rows, coarse_row):
+        return jnp.concatenate([raster_rows.reshape(halo_shape), coarse_row.reshape(halo_shape)], 0)
+
+    up = [(i, i + 1) for i in range(size - 1)]
+    from_above = lax.ppermute(edges(raster[:, rows - 2 :], coarse_own[:, rows - 1]), "space", up)
+    from_below = lax.ppermute(edges(raster[:, :2], coarse_own[:, 0]), "space", [(j, i) for i, j in up])
+    split_at = 2 * raster.shape[0]
+    above = from_above[:split_at].reshape((-1, 2) + raster.shape[2:])
+    below = from_below[:split_at].reshape((-1, 2) + raster.shape[2:])
+    coarse_ext = jnp.concatenate(
+        [from_above[split_at:][:, None], coarse_own, from_below[split_at:][:, None]], axis=1
+    )
 
     def lift(source):
         count = source.shape[1] - 2
@@ -101,7 +102,7 @@
     first = jnp.concatenate([above, raster[:, :1]], axis=1)
     last = jnp.concatenate([raster[:, rows - 1 :], below], axis=1)
     lifted = jnp.concatenate([lift(first), lift(body), lift(last)], axis=0)
-    coarse = jnp.transpose(padded_rows(coarse_features[0], "space", 1, 1), (1, 2, 0, 3))
+    coarse = jnp.transpose(coarse_ext, (1, 2, 0, 3))
     lifted = lifted + lift_bias[None, None, :, None] + coarse.astype(jnp.float32)
     line = lax.broadcasted_iota(jnp.int32, (rows + 2, 1, 1, 1), 0)
     inside = ((line > 0) | (space > 0)) & ((line < rows + 1) | (space < lax.axis_size("space") - 1))
@@ -114,8 +115,10 @@
     windows = jnp.transpose(windows, (2, 0, 1, 3, 4)).reshape((n, span + 2) + hidden_ext.shape[2:])
     gathered = lax.all_to_all(windows, "rot", 0, 0)
 
-    spread = jnp.broadcast_to(group_weight, (n,) + group_weight.shape[1:])
-    filters = lax.all_to_all(spread, "rot", 0, 0)
+    came = [group_weight[0]] + [
+        lax.ppermute(group_weight[0], "rot", [(i, (i + d) % n) for i in range(n)]) for d in range(1, n)
+    ]
+    filters = jnp.roll(jnp.stack([came[(-j) % n] for j in range(n)]), lax.axis_index("rot"), axis=0)
     bias = jnp.tile(group_bias, n)[:, None]
     mixed = group_mix(circulant_bank(filters), bias, gathered)
 
@@ -127,7 +130,7 @@
 
 def solution(mesh):
     return jax.shard_map(
-        shards,
+        layer,
         mesh=mesh,
         in_specs=(
             P(None, "space", None, None),

time: 97.4 us -> 109 us (1.12)
  waiting for transfers between devices: 12.8 us -> 20.1 us
  local copies, waits for them, and re-layouts: 17.4 us -> 24.1 us
  starting transfers between devices: 25.4 us -> 27.6 us
  blocking collectives: 22.7 us -> 20.5 us
  other arithmetic: 3.94 us -> 2.65 us
    ppermute x4 -> x9, waiting for transfers between devices: 0.01 us -> 20.1 us  [the longest x7 20.1 us: layer(): lax.ppermute(group_weight[0], 'rot', [(i, (i + d) % n) for i in range(n)])]
    all_to_all x2 -> x1, waiting for transfers between devices: 12.8 us -> 0.01 us  [layer(): gathered = lax.all_to_all(windows, 'rot', 0, 0)]
    unnamed x10 -> x33, local copies, waits for them, and re-layouts: 6.83 us -> 15.9 us
    ppermute x4 -> x9, starting transfers between devices: 11.1 us -> 20.2 us  [the longest x7 14.6 us: layer(): lax.ppermute(group_weight[0], 'rot', [(i, (i + d) % n) for i in range(n)])]
    all_to_all x2 -> x1, starting transfers between devices: 14.3 us -> 7.36 us  [layer(): gathered = lax.all_to_all(windows, 'rot', 0, 0)]
    concatenate x3, local copies, waits for them, and re-layouts: 4.57 us -> 0.6 us  [lift(): jnp.concatenate([widened[dy:dy + count, :, :, dx:dx + cols] for dy in ran...]
    slice x2, local copies, waits for them, and re-layouts: 0.08 us -> 2.36 us  [circulant_bank(): pairs = jnp.concatenate([filters, jnp.roll(filters, 1, axis=0)], axis=-1)]
    all_to_all x1, blocking collectives: 22.7 us -> 20.5 us  [layer(): returned = lax.all_to_all(mixed, 'rot', 0, 0)]
  transfers between devices with their start and end apart: 6 -> 10, of which waited for: 1 -> 2; matrix products, arithmetic and copies ran while one was open for 21% -> 23% of each run, Pallas kernels for 4% -> 4%
where the time goes in v6:
time: 109 us
  starting transfers between devices  27.6 us (25%)
  local copies, waits for them, and re-layouts  24.1 us (22%)
  blocking collectives  20.5 us (19%)
  waiting for transfers between devices  20.1 us (18%)
  Pallas kernels  12.5 us (11%)
  other arithmetic  2.65 us (2%)
    all_to_all x1, blocking collectives, layer(): returned = lax.all_to_all(mixed, 'rot', 0, 0)  20.5 us
    ppermute x7, waiting for transfers between devices, layer(): lax.ppermute(group_weight[0], 'rot', [(i, (i + d) % n) for i in range(n)])  20.1 us
    unnamed x33, local copies, waits for them, and re-layouts  15.9 us
    ppermute x7, starting transfers between devices, layer(): lax.ppermute(group_weight[0], 'rot', [(i, (i + d) % n) for i in range(n)])  14.6 us
    pallas_call x1, Pallas kernels, group_mix(): pl.pallas_call(mixing_kernel, grid=(rows_out,), in_specs=[pl.BlockSpec((9...  8.25 us
    all_to_all x1, starting transfers between devices, layer(): gathered = lax.all_to_all(windows, 'rot', 0, 0)  7.36 us
    pallas_call x1, Pallas kernels, circulant_bank(): pl.pallas_call(bank_kernel, out_shape=jax.ShapeDtypeStruct((taps, count *...  4.22 us
    ppermute x1, starting transfers between devices, layer(): lax.ppermute(edges(raster[:, :2], coarse_own[:, 0]), 'space', [(j, i) for...  3.64 us
  transfers between devices with their start and end apart: 10, of which 2 were waited for; matrix products, arithmetic and copies ran while one was open for 23% of the time, Pallas kernels for 4%

profile of v6, /device:TPU:96, one launch (start us, length us, event | category | flops | bytes accessed | tf_op | source)
XLA Modules:
  0.0 108.7 jit_solution(15778926495795629407)
XLA Ops:
  0.0 5.6 %collective-permute-start = (bf16[9,64,64]{2,1,0:T(8,128)(2,1)}, bf16[9,64,64]{2,1,0:T(8,128)(2,1)S(1)}, u32[]{:S(2)}, u32[]{:S(2)}) collective-permute-start(bf16[9,64,64]{2,1,0:T(8,128)(2,1)} %bitcast.88), channel_id=1, source_target_pairs={{0,224},{32,0},{64,32},{96,64},{128,96},{160,128},{192,160},{224,1... | collective-permute-start | bytes 221192 | tf_op jit(solution)/shard_map/ppermute | solution.py:119
  5.6 0.6 collective-permute-start.1
  6.2 0.9 collective-permute-start.2
  7.1 1.8 %copy.38 = bf16[1,64,16,2,256]{4,1,3,2,0:T(8,128)(2,1)S(1)} copy(bf16[1,64,16,2,256]{4,3,2,1,0:T(2,128)(2,1)} %param.7) | data formatting | bytes 2097152 | tf_op args[1]
  9.0 1.9 %collective-permute-start.7 = (bf16[72,2,256]{2,0,1:T(8,128)(2,1)S(1)}, bf16[72,2,256]{2,0,1:T(8,128)(2,1)S(1)}, u32[]{:S(2)}, u32[]{:S(2)}) collective-permute-start(bf16[72,2,256]{2,0,1:T(8,128)(2,1)S(1)} %pad_maximum_fusion.1), channel_id=1, source_target_pairs={{0,1},{1,2},{2,3},{3,4},{4,5},{5,6},{6,7},{7,8},{8,9},{9,10},{10,1... | collective-permute-start | bytes 221192 | tf_op jit(solution)/shard_map/ppermute | solution.py:84
  11.0 3.6 %collective-permute-start.8 = (bf16[72,2,256]{2,0,1:T(8,128)(2,1)S(1)}, bf16[72,2,256]{2,0,1:T(8,128)(2,1)S(1)}, u32[]{:S(2)}, u32[]{:S(2)}) collective-permute-start(bf16[72,2,256]{2,0,1:T(8,128)(2,1)S(1)} %pad_maximum_fusion.2), channel_id=1, source_target_pairs={{1,0},{2,1},{3,2},{4,3},{5,4},{6,5},{7,6},{8,7},{9,8},{10,9},{11,1... | collective-permute-start | bytes 221192 | tf_op jit(solution)/shard_map/ppermute | solution.py:85
  14.7 0.7 constant_dynamic-update-slice_fusion.1
  15.4 0.2 broadcast_in_dim_tile.4.bias_ref
  15.7 3.1 %collective-permute-start.3 = (bf16[9,64,64]{2,1,0:T(8,128)(2,1)S(1)}, bf16[9,64,64]{2,1,0:T(8,128)(2,1)}, u32[]{:S(2)}, u32[]{:S(2)}) collective-permute-start(bf16[9,64,64]{2,1,0:T(8,128)(2,1)S(1)} %bitcast.91), channel_id=1, source_target_pairs={{0,128},{32,160},{64,192},{96,224},{128,0},{160,32},{192,64},{224,... | collective-permute-start | bytes 221192 | tf_op jit(solution)/shard_map/ppermute | solution.py:119
  18.8 0.3 collective-permute-start.4
  19.6 0.2 convolution_bitcast_fusion.1
  19.9 0.2 convolution_bitcast_fusion.2
  20.2 0.1 fusion.5
  20.3 0.3 fusion.13
  20.6 0.4 concatenate.53
  21.0 0.5 convolution_bitcast_fusion
  21.5 0.4 copy-done.4
  21.9 0.6 fusion.3
  22.5 0.3 fusion.12
  22.8 0.1 pad_maximum_fusion
  23.0 1.3 %copy.36 = bf16[4,6,2,64,256]{4,3,1,0,2:T(8,128)(2,1)} copy(bf16[4,6,2,64,256]{4,3,2,1,0:T(8,128)(2,1)S(1)} %pad_maximum_fusion) | data formatting | bytes 3145728 | tf_op jit(solution)/shard_map/concatenate | solution.py:114
  24.3 7.4 %all-to-all-start = ((bf16[8,6,64,256]{3,2,1,0:T(8,128)(2,1)}), bf16[8,6,64,256]{3,2,1,0:T(8,128)(2,1)S(1)}, u32[]{:S(2)}, u32[]{:S(2)}) async-start(bf16[8,6,64,256]{3,2,1,0:T(8,128)(2,1)} %bitcast.35), calls=%async_computation | async-start | bytes 3145728 | tf_op jit(solution)/shard_map/all_to_all | solution.py:116
  31.7 3.5 %collective-permute-start.5 = (bf16[9,64,64]{2,1,0:T(8,128)(2,1)S(1)}, bf16[9,64,64]{2,1,0:T(8,128)(2,1)S(1)}, u32[]{:S(2)}, u32[]{:S(2)}) collective-permute-start(bf16[9,64,64]{2,1,0:T(8,128)(2,1)S(1)} %bitcast.93), channel_id=1, source_target_pairs={{0,64},{32,96},{64,128},{96,160},{128,192},{160,224},{192,0},{224,... | collective-permute-start | bytes 221192 | tf_op jit(solution)/shard_map/ppermute | solution.py:119
  35.2 0.7 bitcast_dynamic-update-slice_fusion.12
  35.8 0.6 collective-permute-start.6
  36.4 0.7 bitcast_dynamic-update-slice_fusion.10
  37.1 0.7 bitcast_dynamic-update-slice_fusion.8
  37.8 1.6 %bitcast_dynamic-update-slice_fusion.6 = bf16[16,9,64,64]{3,2,1,0:T(8,128)(2,1)} fusion(bf16[16,9,64,64]{3,2,1,0:T(8,128)(2,1)} %bitcast_dynamic-update-slice_fusion.8, bf16[9,64,64]{2,1,0:T(8,128)(2,1)} %collective-permute-done.3), kind=kLoop, calls=%fused_computation.20 | loop fusion | bytes 294912
  39.3 1.6 %bitcast_dynamic-update-slice_fusion.4 = bf16[16,9,64,64]{3,2,1,0:T(8,128)(2,1)} fusion(bf16[16,9,64,64]{3,2,1,0:T(8,128)(2,1)} %bitcast_dynamic-update-slice_fusion.6, bf16[9,64,64]{2,1,0:T(8,128)(2,1)} %collective-permute-done.4), kind=kLoop, calls=%fused_computation.18 | loop fusion | bytes 294912
  40.9 17.7 %collective-permute-done.5 = bf16[9,64,64]{2,1,0:T(8,128)(2,1)S(1)} collective-permute-done((bf16[9,64,64]{2,1,0:T(8,128)(2,1)S(1)}, bf16[9,64,64]{2,1,0:T(8,128)(2,1)S(1)}, u32[]{:S(2)}, u32[]{:S(2)}) %collective-permute-start.5) | collective-permute-done | bytes 73760 | tf_op jit(solution)/shard_map/ppermute | solution.py:119
  58.6 0.7 bitcast_dynamic-update-slice_fusion.2
  59.3 2.4 %collective-permute-done.6 = bf16[9,64,64]{2,1,0:T(8,128)(2,1)S(1)} collective-permute-done((bf16[9,64,64]{2,1,0:T(8,128)(2,1)S(1)}, bf16[9,64,64]{2,1,0:T(8,128)(2,1)S(1)}, u32[]{:S(2)}, u32[]{:S(2)}) %collective-permute-start.6) | collective-permute-done | bytes 73760 | tf_op jit(solution)/shard_map/ppermute | solution.py:119
  61.6 0.7 bitcast_dynamic-update-slice_fusion
  62.3 0.7 constant_dynamic-update-slice_fusion
  63.0 0.7 bitcast_dynamic-update-slice_fusion.13
  63.6 0.7 bitcast_dynamic-update-slice_fusion.11
  64.3 0.7 bitcast_dynamic-update-slice_fusion.9
  65.0 1.6 %bitcast_dynamic-update-slice_fusion.7 = bf16[16,9,64,64]{3,2,1,0:T(8,128)(2,1)} fusion(bf16[16,9,64,64]{3,2,1,0:T(8,128)(2,1)} %bitcast_dynamic-update-slice_fusion.9, bf16[9,64,64]{2,1,0:T(8,128)(2,1)} %collective-permute-done.3), kind=kLoop, calls=%fused_computation.21 | loop fusion | bytes 294912
  66.6 1.6 %bitcast_dynamic-update-slice_fusion.5 = bf16[16,9,64,64]{3,2,1,0:T(8,128)(2,1)} fusion(bf16[16,9,64,64]{3,2,1,0:T(8,128)(2,1)} %bitcast_dynamic-update-slice_fusion.7, bf16[9,64,64]{2,1,0:T(8,128)(2,1)} %collective-permute-done.4), kind=kLoop, calls=%fused_computation.19 | loop fusion | bytes 294912
  68.1 0.7 bitcast_dynamic-update-slice_fusion.3
  68.8 0.7 bitcast_dynamic-update-slice_fusion.1
  69.5 1.1 constant_dynamic-slice_fusion.1
  70.6 1.3 %constant_dynamic-slice_fusion = bf16[7,9,64,64]{3,2,1,0:T(8,128)(2,1)S(1)} fusion(bf16[16,9,64,64]{3,2,1,0:T(8,128)(2,1)} %bitcast_dynamic-update-slice_fusion.1, s32[]{:T(128)S(6)} %select_n.18), kind=kLoop, calls=%fused_computation.50 | loop fusion | bytes 1032196 | tf_op jit(solution)/shard_map/jit(_roll_static)/slice | solution.py:20
  72.0 1.7 %maximum_maximum_fusion.pairs_ref = bf16[8,9,64,128]{3,2,1,0:T(8,128)(2,1)} fusion(bf16[7,9,64,64]{3,2,1,0:T(8,128)(2,1)S(1)} %constant_dynamic-slice_fusion, bf16[1,9,64,64]{3,2,1,0:T(8,128)(2,1)S(1)} %constant_dynamic-slice_fusion.1, bf16[8,9,64,64]{3,2,1,0:T(8,128)(2,1)S(1)} %constant_dynamic-slice_fusion.2), kind=kLoop, calls=%fused_computation.7 | loop fusion | flops 3538944 | bytes 2359296 | tf_op jit(solution)/shard_map/concatenate | solution.py:20
  73.6 4.2 %shard_map.64.bank_ref = bf16[9,512,512]{2,1,0:T(8,128)(2,1)} custom-call(bf16[8,9,64,128]{3,2,1,0:T(8,128)(2,1)} %maximum_maximum_fusion.pairs_ref), custom_call_target="tpu_custom_call" | custom-call | tf_op jit(solution)/shard_map/pallas_call | solution.py:21
  77.9 8.2 %shard_map.65 = bf16[8,4,64,256]{3,2,1,0:T(8,128)(2,1)S(1)} custom-call(bf16[9,512,512]{2,1,0:T(8,128)(2,1)} %shard_map.64.bank_ref, f32[512,1]{1,0:T(8,128)S(1)} %broadcast_in_dim_tile.4.bias_ref, bf16[8,6,64,256]{3,2,1,0:T(8,128)(2,1)S(1)} %all-to-all-done.x_ref), custom_call_target="tpu_custom_call" | custom-call | tf_op jit(solution)/shard_map/pallas_call | solution.py:51
  86.1 20.5 %all_to_all.10 = bf16[8,4,64,256]{3,2,1,0:T(8,128)(2,1)S(1)} all-to-all(bf16[8,4,64,256]{3,2,1,0:T(8,128)(2,1)S(1)} %shard_map.65), channel_id=1, replica_groups=mesh['rot'=8,'space'=32] {'rot'}, dimensions={0} | all-to-all | bytes 2097152 | tf_op jit(solution)/shard_map/all_to_all | solution.py:125
  106.6 2.1 %copy.31 = bf16[64,4,4,2,256]{4,3,2,1,0:T(2,128)(2,1)} copy(bf16[64,4,4,2,256]{4,0,2,1,3:T(8,128)(2,1)S(1)} %bitcast.86) | data formatting | bytes 2097152 | tf_op jit(solution)/shard_map/transpose | solution.py:127
  (52 shorter events, 0.9 us)
Async XLA Ops:
  0.0 14.7 %copy-start.1 = (bf16[1,9,64,64]{3,2,1,0:T(8,128)(2,1)S(1)}, bf16[1,9,64,64]{3,2,1,0:T(8,128)(2,1)}, u32[]{:S(2)}) copy-start(bf16[1,9,64,64]{3,2,1,0:T(8,128)(2,1)} %param.10) | copy-start | bytes 221188
  0.0 8.9 %copy-start.2 = (bf16[4,16,2,256]{3,2,1,0:T(2,128)(2,1)S(1)}, bf16[4,16,2,256]{3,2,1,0:T(2,128)(2,1)}, u32[]{:S(2)}) copy-start(bf16[4,16,2,256]{3,2,1,0:T(2,128)(2,1)} %param.6) | copy-start | bytes 196612
  0.0 14.7 %copy-start.5 = (bf16[1,9,64,4]{2,3,1,0:T(4,128)(2,1)S(1)}, bf16[1,9,64,4]{2,3,1,0:T(4,128)(2,1)}, u32[]{:S(2)}) copy-start(bf16[1,9,64,4]{2,3,1,0:T(4,128)(2,1)} %param.8) | copy-start | bytes 13828
  0.0 15.4 %copy-start.7 = (f32[64]{0:T(128)S(1)}, f32[64]{0:T(128)}, u32[]{:S(2)}) copy-start(f32[64]{0:T(128)} %param.11) | copy-start | bytes 772
  0.0 31.6 %collective-permute-start = (bf16[9,64,64]{2,1,0:T(8,128)(2,1)}, bf16[9,64,64]{2,1,0:T(8,128)(2,1)S(1)}, u32[]{:S(2)}, u32[]{:S(2)}) collective-permute-start(bf16[9,64,64]{2,1,0:T(8,128)(2,1)} %bitcast.88), channel_id=1, source_target_pairs={{0,224},{32,0},{64,32},{96,64},{128,96},{160,128},{192,160},{224,1... | collective-permute-start | bytes 221192 | tf_op jit(solution)/shard_map/ppermute | solution.py:119
  5.6 30.3 %collective-permute-start.1 = (bf16[9,64,64]{2,1,0:T(8,128)(2,1)}, bf16[9,64,64]{2,1,0:T(8,128)(2,1)S(1)}, u32[]{:S(2)}, u32[]{:S(2)}) collective-permute-start(bf16[9,64,64]{2,1,0:T(8,128)(2,1)} %bitcast.89), channel_id=1, source_target_pairs={{0,192},{32,224},{64,0},{96,32},{128,64},{160,96},{192,128},{224,1... | collective-permute-start | bytes 221192 | tf_op jit(solution)/shard_map/ppermute | solution.py:119
  6.2 30.9 %collective-permute-start.2 = (bf16[9,64,64]{2,1,0:T(8,128)(2,1)}, bf16[9,64,64]{2,1,0:T(8,128)(2,1)S(1)}, u32[]{:S(2)}, u32[]{:S(2)}) collective-permute-start(bf16[9,64,64]{2,1,0:T(8,128)(2,1)} %bitcast.90), channel_id=1, source_target_pairs={{0,160},{32,192},{64,224},{96,0},{128,32},{160,64},{192,96},{224,1... | collective-permute-start | bytes 221192 | tf_op jit(solution)/shard_map/ppermute | solution.py:119
  9.0 6.7 %collective-permute-start.7 = (bf16[72,2,256]{2,0,1:T(8,128)(2,1)S(1)}, bf16[72,2,256]{2,0,1:T(8,128)(2,1)S(1)}, u32[]{:S(2)}, u32[]{:S(2)}) collective-permute-start(bf16[72,2,256]{2,0,1:T(8,128)(2,1)S(1)} %pad_maximum_fusion.1), channel_id=1, source_target_pairs={{0,1},{1,2},{2,3},{3,4},{4,5},{5,6},{6,7},{7,8},{8,9},{9,10},{10,1... | collective-permute-start | bytes 221192 | tf_op jit(solution)/shard_map/ppermute | solution.py:84
  11.0 7.9 %collective-permute-start.8 = (bf16[72,2,256]{2,0,1:T(8,128)(2,1)S(1)}, bf16[72,2,256]{2,0,1:T(8,128)(2,1)S(1)}, u32[]{:S(2)}, u32[]{:S(2)}) collective-permute-start(bf16[72,2,256]{2,0,1:T(8,128)(2,1)S(1)} %pad_maximum_fusion.2), channel_id=1, source_target_pairs={{1,0},{2,1},{3,2},{4,3},{5,4},{6,5},{7,6},{8,7},{9,8},{10,9},{11,1... | collective-permute-start | bytes 221192 | tf_op jit(solution)/shard_map/ppermute | solution.py:85
  15.7 22.1 %collective-permute-start.3 = (bf16[9,64,64]{2,1,0:T(8,128)(2,1)S(1)}, bf16[9,64,64]{2,1,0:T(8,128)(2,1)}, u32[]{:S(2)}, u32[]{:S(2)}) collective-permute-start(bf16[9,64,64]{2,1,0:T(8,128)(2,1)S(1)} %bitcast.91), channel_id=1, source_target_pairs={{0,128},{32,160},{64,192},{96,224},{128,0},{160,32},{192,64},{224,... | collective-permute-start | bytes 221192 | tf_op jit(solution)/shard_map/ppermute | solution.py:119
  18.8 1.8 %copy-start.3 = (bf16[72,2,256]{2,0,1:T(8,128)(2,1)}, bf16[72,2,256]{2,0,1:T(8,128)(2,1)S(1)}, u32[]{:S(2)}) copy-start(bf16[72,2,256]{2,0,1:T(8,128)(2,1)S(1)} %collective-permute-done.8) | copy-start | bytes 221188
  18.8 20.5 %collective-permute-start.4 = (bf16[9,64,64]{2,1,0:T(8,128)(2,1)S(1)}, bf16[9,64,64]{2,1,0:T(8,128)(2,1)}, u32[]{:S(2)}, u32[]{:S(2)}) collective-permute-start(bf16[9,64,64]{2,1,0:T(8,128)(2,1)S(1)} %bitcast.92), channel_id=1, source_target_pairs={{0,96},{32,128},{64,160},{96,192},{128,224},{160,0},{192,32},{224,... | collective-permute-start | bytes 221192 | tf_op jit(solution)/shard_map/ppermute | solution.py:119
  20.6 1.3 %copy-start.6 = (f32[64]{0:T(128)S(1)}, f32[64]{0:T(128)}, u32[]{:S(2)}) copy-start(f32[64]{0:T(128)} %param.9) | copy-start | bytes 772
  21.0 0.9 copy-start.4
  24.3 53.6 %all-to-all-start = ((bf16[8,6,64,256]{3,2,1,0:T(8,128)(2,1)}), bf16[8,6,64,256]{3,2,1,0:T(8,128)(2,1)S(1)}, u32[]{:S(2)}, u32[]{:S(2)}) async-start(bf16[8,6,64,256]{3,2,1,0:T(8,128)(2,1)} %bitcast.35), calls=%async_computation | async-start | bytes 3145728 | tf_op jit(solution)/shard_map/all_to_all | solution.py:116
  31.7 27.0 %collective-permute-start.5 = (bf16[9,64,64]{2,1,0:T(8,128)(2,1)S(1)}, bf16[9,64,64]{2,1,0:T(8,128)(2,1)S(1)}, u32[]{:S(2)}, u32[]{:S(2)}) collective-permute-start(bf16[9,64,64]{2,1,0:T(8,128)(2,1)S(1)} %bitcast.93), channel_id=1, source_target_pairs={{0,64},{32,96},{64,128},{96,160},{128,192},{160,224},{192,0},{224,... | collective-permute-start | bytes 221192 | tf_op jit(solution)/shard_map/ppermute | solution.py:119
  35.8 25.8 %collective-permute-start.6 = (bf16[9,64,64]{2,1,0:T(8,128)(2,1)S(1)}, bf16[9,64,64]{2,1,0:T(8,128)(2,1)S(1)}, u32[]{:S(2)}, u32[]{:S(2)}) collective-permute-start(bf16[9,64,64]{2,1,0:T(8,128)(2,1)S(1)} %bitcast.94), channel_id=1, source_target_pairs={{0,32},{32,64},{64,96},{96,128},{128,160},{160,192},{192,224},{224... | collective-permute-start | bytes 221192 | tf_op jit(solution)/shard_map/ppermute | solution.py:119
  69.5 2.4 %copy-start = (bf16[16,9,64,64]{3,2,1,0:T(8,128)(2,1)S(1)}, bf16[16,9,64,64]{3,2,1,0:T(8,128)(2,1)}, u32[]{:S(2)}) copy-start(bf16[16,9,64,64]{3,2,1,0:T(8,128)(2,1)} %bitcast_dynamic-update-slice_fusion.1) | copy-start | bytes 3538948

commit v7 on v6

--- a/solution.py
+++ b/solution.py
@@ -62,10 +62,11 @@
     )(bank, bias, windows)
 
 
-def layer(raster, coarse_features, lift_weight, lift_bias, group_weight, group_bias):
+def shards(raster, coarse_features, lift_weight, lift_bias, group_weight, group_bias):
     n = lax.axis_size("rot")
     channels = lift_weight.shape[2]
     rows = raster.shape[1]
+    chunk = rows // n
 
     tiles, cols = raster.shape[2], raster.shape[3]
     quarters = n // tiles
@@ -115,10 +116,8 @@
     windows = jnp.transpose(windows, (2, 0, 1, 3, 4)).reshape((n, span + 2) + hidden_ext.shape[2:])
     gathered = lax.all_to_all(windows, "rot", 0, 0)
 
-    came = [group_weight[0]] + [
-        lax.ppermute(group_weight[0], "rot", [(i, (i + d) % n) for i in range(n)]) for d in range(1, n)
-    ]
-    filters = jnp.roll(jnp.stack([came[(-j) % n] for j in range(n)]), lax.axis_index("rot"), axis=0)
+    spread = jnp.broadcast_to(group_weight, (n,) + group_weight.shape[1:])
+    filters = lax.all_to_all(spread, "rot", 0, 0)
     bias = jnp.tile(group_bias, n)[:, None]
     mixed = group_mix(circulant_bank(filters), bias, gathered)
 
@@ -130,7 +129,7 @@
 
 def solution(mesh):
     return jax.shard_map(
-        layer,
+        shards,
         mesh=mesh,
         in_specs=(
             P(None, "space", None, None),

time: 109 us -> 86.6 us (0.79)
  local copies, waits for them, and re-layouts: 24.1 us -> 11.5 us
  starting transfers between devices: 27.6 us -> 16.9 us
  blocking collectives: 20.5 us -> 21.9 us
    ppermute x9 -> x2, waiting for transfers between devices: 20.1 us -> 0.01 us  [the longest x1 0.01 us: shards(): lax.ppermute(edges(raster[:, rows - 2:], coarse_own[:, rows - 1]), 'space...]
    all_to_all x1 -> x2, waiting for transfers between devices: 0.01 us -> 19.5 us  [the longest x1 12.4 us: shards(): gathered = lax.all_to_all(windows, 'rot', 0, 0)]
    ppermute x9 -> x2, starting transfers between devices: 20.2 us -> 5.56 us  [the longest x1 3.64 us: shards(): lax.ppermute(edges(raster[:, :2], coarse_own[:, 0]), 'space', [(j, i) for...]
    unnamed x33 -> x16, local copies, waits for them, and re-layouts: 15.9 us -> 6.14 us
    all_to_all x1 -> x2, starting transfers between devices: 7.36 us -> 11.3 us  [the longest x1 6.93 us: shards(): filters = lax.all_to_all(spread, 'rot', 0, 0)]
    slice x2, local copies, waits for them, and re-layouts: 2.36 us -> 0.08 us  [circulant_bank(): pairs = jnp.concatenate([filters, jnp.roll(filters, 1, axis=0)], axis=-1)]
    all_to_all x1, blocking collectives: 20.5 us -> 21.9 us  [shards(): returned = lax.all_to_all(mixed, 'rot', 0, 0)]
  transfers between devices with their start and end apart: 10 -> 4, of which waited for: 2 -> 2; matrix products, arithmetic and copies ran while one was open for 23% -> 13% of each run, Pallas kernels for 4% -> 5%
where the time goes in v7:
time: 86.6 us; the launch traced here: 86.2 us
  blocking collectives  21.9 us (25%)
  waiting for transfers between devices  19.5 us (23%)
  starting transfers between devices  16.9 us (20%)
  Pallas kernels  12.4 us (14%)
  local copies, waits for them, and re-layouts  11.5 us (13%)
  other arithmetic  2.65 us (3%)
  matrix products  0.89 us (1%)
    all_to_all x1, blocking collectives, shards(): returned = lax.all_to_all(mixed, 'rot', 0, 0)  21.9 us
    all_to_all x1, waiting for transfers between devices, shards(): gathered = lax.all_to_all(windows, 'rot', 0, 0)  12.4 us
    pallas_call x1, Pallas kernels, group_mix(): pl.pallas_call(mixing_kernel, grid=(rows_out,), in_specs=[pl.BlockSpec((9...  8.25 us
    all_to_all x1, waiting for transfers between devices, shards(): filters = lax.all_to_all(spread, 'rot', 0, 0)  7.13 us
    all_to_all x1, starting transfers between devices, shards(): filters = lax.all_to_all(spread, 'rot', 0, 0)  6.93 us
    unnamed x16, local copies, waits for them, and re-layouts  6.14 us
    all_to_all x1, starting transfers between devices, shards(): gathered = lax.all_to_all(windows, 'rot', 0, 0)  4.4 us
    pallas_call x1, Pallas kernels, circulant_bank(): pl.pallas_call(bank_kernel, out_shape=jax.ShapeDtypeStruct((taps, count *...  4.2 us
  transfers between devices with their start and end apart: 4, of which 2 were waited for; matrix products, arithmetic and copies ran while one was open for 13% of the time, Pallas kernels for 5%

profile of v7, /device:TPU:96, one launch (start us, length us, event | category | flops | bytes accessed | tf_op | source)
XLA Modules:
  0.0 86.2 jit_solution(8089749254388790352)
XLA Ops:
  0.0 0.0 copy-start.2
  0.0 0.0 copy-start.1
  0.0 1.8 %copy.38 = bf16[1,64,16,2,256]{4,1,3,2,0:T(8,128)(2,1)S(1)} copy(bf16[1,64,16,2,256]{4,3,2,1,0:T(2,128)(2,1)} %param.7) | data formatting | bytes 2097152 | tf_op args[1]
  1.9 0.0 copy-done.2
  1.9 1.9 %collective-permute-start = (bf16[72,2,256]{2,0,1:T(8,128)(2,1)S(1)}, bf16[72,2,256]{2,0,1:T(8,128)(2,1)S(1)}, u32[]{:S(2)}, u32[]{:S(2)}) collective-permute-start(bf16[72,2,256]{2,0,1:T(8,128)(2,1)S(1)} %pad_maximum_fusion.1), channel_id=1, source_target_pairs={{0,1},{1,2},{2,3},{3,4},{4,5},{5,6},{6,7},{7,8},{8,9},{9,10},{10,1... | collective-permute-start | bytes 221192 | tf_op jit(solution)/shard_map/ppermute | solution.py:85
  3.9 3.6 %collective-permute-start.1 = (bf16[72,2,256]{2,0,1:T(8,128)(2,1)S(1)}, bf16[72,2,256]{2,0,1:T(8,128)(2,1)S(1)}, u32[]{:S(2)}, u32[]{:S(2)}) collective-permute-start(bf16[72,2,256]{2,0,1:T(8,128)(2,1)S(1)} %pad_maximum_fusion.2), channel_id=1, source_target_pairs={{1,0},{2,1},{3,2},{4,3},{5,4},{6,5},{7,6},{8,7},{9,8},{10,9},{11,1... | collective-permute-start | bytes 221192 | tf_op jit(solution)/shard_map/ppermute | solution.py:86
  7.5 0.0 copy-done.1
  7.5 0.3 broadcast_in_dim.25
  7.8 0.0 copy-start.3
  7.8 1.6 %reshape.67 = bf16[8,2,18432]{2,1,0:T(2,128)(2,1)} reshape(bf16[8,9,64,64]{3,2,1,0:T(8,128)(2,1)S(1)} %broadcast_in_dim.25) | data formatting | bytes 1179648
  9.4 6.9 %all-to-all-start = ((bf16[8,2,18432]{2,1,0:T(2,128)(2,1)}), bf16[8,2,18432]{2,1,0:T(2,128)(2,1)S(1)}, u32[]{:S(2)}, u32[]{:S(2)}) async-start(bf16[8,2,18432]{2,1,0:T(2,128)(2,1)} %reshape.67), calls=%async_computation | async-start | bytes 1179648 | tf_op jit(solution)/shard_map/all_to_all | solution.py:120
  16.4 0.1 copy.19
  16.4 0.0 copy-done.3
  16.5 0.0 collective-permute-done
  16.6 0.0 collective-permute-done.1
  16.7 0.1 fusion.9
  16.8 0.1 fusion.16
  16.8 0.1 fusion.5
  17.0 0.3 fusion.13
  17.3 0.1 fusion.17
  17.4 0.1 concatenate.44
  17.5 0.2 convolution_bitcast_fusion.2
  17.7 0.1 concatenate.49
  17.8 0.2 convolution_bitcast_fusion.1
  18.0 0.4 concatenate.47
  18.4 0.0 copy-start.4
  18.4 0.5 convolution_bitcast_fusion
  18.9 0.1 copy-done.4
  19.1 0.6 fusion.3
  19.7 0.2 fusion.12
  20.0 0.1 pad_maximum_fusion
  20.1 1.3 %copy.36 = bf16[4,6,2,64,256]{4,3,1,0,2:T(8,128)(2,1)} copy(bf16[4,6,2,64,256]{4,3,2,1,0:T(8,128)(2,1)S(1)} %pad_maximum_fusion) | data formatting | bytes 3145728 | tf_op jit(solution)/shard_map/concatenate | solution.py:115
  21.4 7.1 %all-to-all-done = bf16[8,2,18432]{2,1,0:T(2,128)(2,1)S(1)} async-done(((bf16[8,2,18432]{2,1,0:T(2,128)(2,1)}), bf16[8,2,18432]{2,1,0:T(2,128)(2,1)S(1)}, u32[]{:S(2)}, u32[]{:S(2)}) %all-to-all-start) | async-done | bytes 589856 | tf_op jit(solution)/shard_map/all_to_all | solution.py:120
  28.5 0.0 copy-start
  28.5 0.0 copy-start.5
  28.5 4.4 %all-to-all-start.1 = ((bf16[8,6,64,256]{3,2,1,0:T(8,128)(2,1)}), bf16[8,6,64,256]{3,2,1,0:T(8,128)(2,1)S(1)}, u32[]{:S(2)}, u32[]{:S(2)}) async-start(bf16[8,6,64,256]{3,2,1,0:T(8,128)(2,1)} %bitcast.28), calls=%async_computation.1 | async-start | bytes 3145728 | tf_op jit(solution)/shard_map/all_to_all | solution.py:117
  32.9 0.0 copy-done
  32.9 0.0 copy-done.5
  33.0 0.2 broadcast_in_dim_tile.4.bias_ref
  33.2 2.5 %reshape.68 = bf16[8,9,64,64]{3,2,1,0:T(8,128)(2,1)S(1)} reshape(bf16[8,2,18432]{2,1,0:T(2,128)(2,1)} %copy-done) | data formatting | bytes 1179648
  35.6 0.1 slice.179
  35.7 1.7 %maximum_maximum_fusion.pairs_ref = bf16[8,9,64,128]{3,2,1,0:T(8,128)(2,1)} fusion(bf16[7,9,64,64]{3,2,1,0:T(8,128)(2,1)S(1)} %slice.179, bf16[1,9,64,64]{3,2,1,0:T(8,128)(2,1)S(1)} %slice.178, bf16[8,9,64,64]{3,2,1,0:T(8,128)(2,1)S(1)} %reshape.68), kind=kLoop, calls=%fused_computation.7 | loop fusion | flops 3538944 | bytes 2359296 | tf_op jit(solution)/shard_map/concatenate | solution.py:20
  37.4 4.2 %shard_map.64.bank_ref = bf16[9,512,512]{2,1,0:T(8,128)(2,1)} custom-call(bf16[8,9,64,128]{3,2,1,0:T(8,128)(2,1)} %maximum_maximum_fusion.pairs_ref), custom_call_target="tpu_custom_call" | custom-call | tf_op jit(solution)/shard_map/pallas_call | solution.py:21
  41.6 12.4 %all-to-all-done.1.x_ref = bf16[8,6,64,256]{3,2,1,0:T(8,128)(2,1)S(1)} async-done(((bf16[8,6,64,256]{3,2,1,0:T(8,128)(2,1)}), bf16[8,6,64,256]{3,2,1,0:T(8,128)(2,1)S(1)}, u32[]{:S(2)}, u32[]{:S(2)}) %all-to-all-start.1) | async-done | bytes 1572896 | tf_op jit(solution)/shard_map/all_to_all | solution.py:117
  54.0 8.2 %shard_map.65 = bf16[8,4,64,256]{3,2,1,0:T(8,128)(2,1)S(1)} custom-call(bf16[9,512,512]{2,1,0:T(8,128)(2,1)} %shard_map.64.bank_ref, f32[512,1]{1,0:T(8,128)S(1)} %broadcast_in_dim_tile.4.bias_ref, bf16[8,6,64,256]{3,2,1,0:T(8,128)(2,1)S(1)} %all-to-all-done.1.x_ref), custom_call_target="tpu_custom_call" | custom-call | tf_op jit(solution)/shard_map/pallas_call | solution.py:51
  62.3 21.9 %all_to_all.15 = bf16[8,4,64,256]{3,2,1,0:T(8,128)(2,1)S(1)} all-to-all(bf16[8,4,64,256]{3,2,1,0:T(8,128)(2,1)S(1)} %shard_map.65), channel_id=1, replica_groups=mesh['rot'=8,'space'=32] {'rot'}, dimensions={0} | all-to-all | bytes 2097152 | tf_op jit(solution)/shard_map/all_to_all | solution.py:124
  84.2 2.1 %copy.31 = bf16[64,4,4,2,256]{4,3,2,1,0:T(2,128)(2,1)} copy(bf16[64,4,4,2,256]{4,0,2,1,3:T(8,128)(2,1)S(1)} %bitcast.65) | data formatting | bytes 2097152 | tf_op jit(solution)/shard_map/transpose | solution.py:126
  (23 shorter events, 0.2 us)
Async XLA Ops:
  0.0 1.9 %copy-start.2 = (bf16[4,16,2,256]{3,2,1,0:T(2,128)(2,1)S(1)}, bf16[4,16,2,256]{3,2,1,0:T(2,128)(2,1)}, u32[]{:S(2)}) copy-start(bf16[4,16,2,256]{3,2,1,0:T(2,128)(2,1)} %param.6) | copy-start | bytes 196612
  0.0 7.5 %copy-start.1 = (bf16[1,9,64,64]{3,2,1,0:T(8,128)(2,1)S(1)}, bf16[1,9,64,64]{3,2,1,0:T(8,128)(2,1)}, u32[]{:S(2)}) copy-start(bf16[1,9,64,64]{3,2,1,0:T(8,128)(2,1)} %param.10) | copy-start | bytes 221188
  1.9 14.6 %collective-permute-start = (bf16[72,2,256]{2,0,1:T(8,128)(2,1)S(1)}, bf16[72,2,256]{2,0,1:T(8,128)(2,1)S(1)}, u32[]{:S(2)}, u32[]{:S(2)}) collective-permute-start(bf16[72,2,256]{2,0,1:T(8,128)(2,1)S(1)} %pad_maximum_fusion.1), channel_id=1, source_target_pairs={{0,1},{1,2},{2,3},{3,4},{4,5},{5,6},{6,7},{7,8},{8,9},{9,10},{10,1... | collective-permute-start | bytes 221192 | tf_op jit(solution)/shard_map/ppermute | solution.py:85
  3.9 12.7 %collective-permute-start.1 = (bf16[72,2,256]{2,0,1:T(8,128)(2,1)S(1)}, bf16[72,2,256]{2,0,1:T(8,128)(2,1)S(1)}, u32[]{:S(2)}, u32[]{:S(2)}) collective-permute-start(bf16[72,2,256]{2,0,1:T(8,128)(2,1)S(1)} %pad_maximum_fusion.2), channel_id=1, source_target_pairs={{1,0},{2,1},{3,2},{4,3},{5,4},{6,5},{7,6},{8,7},{9,8},{10,9},{11,1... | collective-permute-start | bytes 221192 | tf_op jit(solution)/shard_map/ppermute | solution.py:86
  7.8 8.6 %copy-start.3 = (bf16[1,9,64,4]{2,3,1,0:T(4,128)(2,1)S(1)}, bf16[1,9,64,4]{2,3,1,0:T(4,128)(2,1)}, u32[]{:S(2)}) copy-start(bf16[1,9,64,4]{2,3,1,0:T(4,128)(2,1)} %param.8) | copy-start | bytes 13828
  9.4 19.1 %all-to-all-start = ((bf16[8,2,18432]{2,1,0:T(2,128)(2,1)}), bf16[8,2,18432]{2,1,0:T(2,128)(2,1)S(1)}, u32[]{:S(2)}, u32[]{:S(2)}) async-start(bf16[8,2,18432]{2,1,0:T(2,128)(2,1)} %reshape.67), calls=%async_computation | async-start | bytes 1179648 | tf_op jit(solution)/shard_map/all_to_all | solution.py:120
  18.4 0.7 copy-start.4
  28.5 4.4 %copy-start = (bf16[8,2,18432]{2,1,0:T(2,128)(2,1)}, bf16[8,2,18432]{2,1,0:T(2,128)(2,1)S(1)}, u32[]{:S(2)}) copy-start(bf16[8,2,18432]{2,1,0:T(2,128)(2,1)S(1)} %all-to-all-done) | copy-start | bytes 1769476
  28.5 4.4 %copy-start.5 = (f32[64]{0:T(128)S(1)}, f32[64]{0:T(128)}, u32[]{:S(2)}) copy-start(f32[64]{0:T(128)} %param.11) | copy-start | bytes 772
  28.5 25.5 %all-to-all-start.1 = ((bf16[8,6,64,256]{3,2,1,0:T(8,128)(2,1)}), bf16[8,6,64,256]{3,2,1,0:T(8,128)(2,1)S(1)}, u32[]{:S(2)}, u32[]{:S(2)}) async-start(bf16[8,6,64,256]{3,2,1,0:T(8,128)(2,1)} %bitcast.28), calls=%async_computation.1 | async-start | bytes 3145728 | tf_op jit(solution)/shard_map/all_to_all | solution.py:117

commit v8 on v7

--- a/solution.py
+++ b/solution.py
@@ -26,8 +26,8 @@
 
 def mixing_kernel(bank_ref, bias_ref, x_ref, o_ref):
     row = pl.program_id(0)
-    count, channels, cols = x_ref.shape[0], x_ref.shape[2], x_ref.shape[3]
-    planes = [jnp.concatenate([x_ref[h, row + dy] for h in range(count)], axis=0) for dy in range(3)]
+    count, channels, cols = o_ref.shape[0], o_ref.shape[2], o_ref.shape[3]
+    planes = [x_ref[row + dy] for dy in range(3)]
     sums = []
     for dx in range(3):
         total = None
@@ -44,17 +44,17 @@
         o_ref[g, 0] = mixed[g * channels : (g + 1) * channels]
 
 
-def group_mix(bank, bias, windows):
-    count, rows_in, channels, cols = windows.shape
+def group_mix(bank, bias, windows, count):
+    rows_in, full, cols = windows.shape
+    channels = full // count
     rows_out = rows_in - 2
-    full = count * channels
     return pl.pallas_call(
         mixing_kernel,
         grid=(rows_out,),
         in_specs=[
             pl.BlockSpec((9, full, full), lambda r: (0, 0, 0)),
             pl.BlockSpec((full, 1), lambda r: (0, 0)),
-            pl.BlockSpec(windows.shape, lambda r: (0, 0, 0, 0)),
+            pl.BlockSpec(windows.shape, lambda r: (0, 0, 0)),
         ],
         out_specs=pl.BlockSpec((count, 1, channels, cols), lambda r: (0, r, 0, 0)),
         out_shape=jax.ShapeDtypeStruct((count, rows_out, channels, cols), jnp.bfloat16),
@@ -114,12 +114,14 @@
     bottom = lax.slice_in_dim(hidden_ext, 2, rows + 2, axis=0).reshape(split)
     windows = jnp.concatenate([top, lax.slice_in_dim(bottom, span - 2, span, axis=1)], axis=1)
     windows = jnp.transpose(windows, (2, 0, 1, 3, 4)).reshape((n, span + 2) + hidden_ext.shape[2:])
-    gathered = lax.all_to_all(windows, "rot", 0, 0)
+    gathered = lax.all_to_all(windows, "rot", 0, 1)
+    gathered = gathered.reshape((gathered.shape[0], n * channels, cols))
 
-    spread = jnp.broadcast_to(group_weight, (n,) + group_weight.shape[1:])
-    filters = lax.all_to_all(spread, "rot", 0, 0)
+    dense = group_weight[0].reshape(2, -1)
+    spread = jnp.broadcast_to(dense, (n,) + dense.shape)
+    filters = lax.all_to_all(spread, "rot", 0, 0).reshape((n,) + group_weight.shape[1:])
     bias = jnp.tile(group_bias, n)[:, None]
-    mixed = group_mix(circulant_bank(filters), bias, gathered)
+    mixed = group_mix(circulant_bank(filters), bias, gathered, n)
 
     returned = lax.all_to_all(mixed, "rot", 0, 0)
     returned = returned.reshape((tiles, quarters) + returned.shape[1:])

time: 86.6 us -> 86.2 us (level)
  waiting for transfers between devices: 19.5 us -> 16.5 us
  other arithmetic: 2.65 us -> 4.23 us
  local copies, waits for them, and re-layouts: 11.5 us -> 12.5 us
    unnamed x16 -> x12, local copies, waits for them, and re-layouts: 6.14 us -> 2.06 us
    all_to_all x2, waiting for transfers between devices: 19.5 us -> 16.5 us  [the longest x1 9.41 us: shards(): gathered = lax.all_to_all(windows, 'rot', 0, 1)]
    slice x2 -> x4, local copies, waits for them, and re-layouts: 0.08 us -> 2.18 us  [circulant_bank(): pairs = jnp.concatenate([filters, jnp.roll(filters, 1, axis=0)], axis=-1)]
    reshape x0 -> x1, local copies, waits for them, and re-layouts: none -> 1.8 us  [shards(): lax.all_to_all(spread, 'rot', 0, 0).reshape((n,) + group_weight.shape[1:])]
    concatenate x1, other arithmetic: 1.67 us -> 3.25 us  [circulant_bank(): pairs = jnp.concatenate([filters, jnp.roll(filters, 1, axis=0)], axis=-1)]
    transpose x0 -> x1, local copies, waits for them, and re-layouts: none -> 1.31 us  [shards(): jnp.transpose(windows, (2, 0, 1, 3, 4))]
    concatenate x1 -> x0, local copies, waits for them, and re-layouts: 1.3 us -> none  [shards(): jnp.concatenate([top, lax.slice_in_dim(bottom, span - 2, span, axis=1)],...]
  transfers between devices with their start and end apart: 4 -> 4, of which waited for: 2 -> 2; matrix products, arithmetic and copies ran while one was open for 13% -> 16% of each run, Pallas kernels for 5% -> 5%
where the time goes in v8:
time: 86.2 us; the launch traced here: 85.8 us
  blocking collectives  21.9 us (25%)
  starting transfers between devices  16.9 us (20%)
  waiting for transfers between devices  16.5 us (19%)
  local copies, waits for them, and re-layouts  12.5 us (15%)
  Pallas kernels  12.5 us (15%)
  other arithmetic  4.23 us (5%)
  matrix products  0.89 us (1%)
    all_to_all x1, blocking collectives, shards(): returned = lax.all_to_all(mixed, 'rot', 0, 0)  21.9 us
    all_to_all x1, waiting for transfers between devices, shards(): gathered = lax.all_to_all(windows, 'rot', 0, 1)  9.41 us
    pallas_call x1, Pallas kernels, group_mix(): pl.pallas_call(mixing_kernel, grid=(rows_out,), in_specs=[pl.BlockSpec((9...  8.27 us
    all_to_all x1, waiting for transfers between devices, shards(): lax.all_to_all(spread, 'rot', 0, 0).reshape((n,) + group_weight.shape[1:])  7.1 us
    all_to_all x1, starting transfers between devices, shards(): lax.all_to_all(spread, 'rot', 0, 0).reshape((n,) + group_weight.shape[1:])  6.93 us
    all_to_all x1, starting transfers between devices, shards(): gathered = lax.all_to_all(windows, 'rot', 0, 1)  4.4 us
    pallas_call x1, Pallas kernels, circulant_bank(): pl.pallas_call(bank_kernel, out_shape=jax.ShapeDtypeStruct((taps, count *...  4.2 us
    ppermute x1, starting transfers between devices, shards(): lax.ppermute(edges(raster[:, :2], coarse_own[:, 0]), 'space', [(j, i) for...  3.64 us
  transfers between devices with their start and end apart: 4, of which 2 were waited for; matrix products, arithmetic and copies ran while one was open for 16% of the time, Pallas kernels for 5%

profile of v8, /device:TPU:96, one launch (start us, length us, event | category | flops | bytes accessed | tf_op | source)
XLA Modules:
  0.0 85.8 jit_solution(2126447629450809470)
XLA Ops:
  0.0 0.0 copy-start.1
  0.0 0.0 copy-start
  0.0 1.8 %copy.50 = bf16[1,64,16,2,256]{4,1,3,2,0:T(8,128)(2,1)S(1)} copy(bf16[1,64,16,2,256]{4,3,2,1,0:T(2,128)(2,1)} %param.7) | data formatting | bytes 2097152 | tf_op args[1]
  1.9 0.0 copy-start.2
  1.9 0.0 copy-done.1
  1.9 1.9 %collective-permute-start = (bf16[72,2,256]{2,0,1:T(8,128)(2,1)S(1)}, bf16[72,2,256]{2,0,1:T(8,128)(2,1)S(1)}, u32[]{:S(2)}, u32[]{:S(2)}) collective-permute-start(bf16[72,2,256]{2,0,1:T(8,128)(2,1)S(1)} %pad_maximum_fusion), channel_id=1, source_target_pairs={{0,1},{1,2},{2,3},{3,4},{4,5},{5,6},{6,7},{7,8},{8,9},{9,10},{10,1... | collective-permute-start | bytes 221192 | tf_op jit(solution)/shard_map/ppermute | solution.py:85
  3.9 3.6 %collective-permute-start.1 = (bf16[72,2,256]{2,0,1:T(8,128)(2,1)S(1)}, bf16[72,2,256]{2,0,1:T(8,128)(2,1)S(1)}, u32[]{:S(2)}, u32[]{:S(2)}) collective-permute-start(bf16[72,2,256]{2,0,1:T(8,128)(2,1)S(1)} %pad_maximum_fusion.1), channel_id=1, source_target_pairs={{1,0},{2,1},{3,2},{4,3},{5,4},{6,5},{7,6},{8,7},{9,8},{10,9},{11,1... | collective-permute-start | bytes 221192 | tf_op jit(solution)/shard_map/ppermute | solution.py:86
  7.6 0.0 copy-done
  7.6 0.2 reshape_squeeze.6
  7.7 1.1 %broadcast_in_dim.20 = bf16[8,2,18432]{2,1,0:T(2,128)(2,1)} broadcast(bf16[2,18432]{1,0:T(2,128)(2,1)S(1)} %reshape_squeeze.6), dimensions={1,2} | broadcast | bytes 663552 | tf_op jit(solution)/shard_map/broadcast_in_dim | solution.py:121
  8.9 6.9 %all-to-all-start = ((bf16[8,2,18432]{2,1,0:T(2,128)(2,1)}), bf16[8,2,18432]{2,1,0:T(2,128)(2,1)S(1)}, u32[]{:S(2)}, u32[]{:S(2)}) async-start(bf16[8,2,18432]{2,1,0:T(2,128)(2,1)} %broadcast_in_dim.20), calls=%async_computation | async-start | bytes 1179648 | tf_op jit(solution)/shard_map/all_to_all | solution.py:122
  15.8 0.1 copy.33
  15.9 0.0 copy-done.2
  15.9 0.0 collective-permute-done
  16.0 0.0 collective-permute-done.1
  16.1 0.1 fusion.9
  16.2 0.1 fusion.16
  16.3 0.1 fusion.5
  16.4 0.3 fusion.13
  16.7 0.1 fusion.17
  16.8 0.1 concatenate.44
  16.9 0.2 convolution_bitcast_fusion.2
  17.1 0.1 concatenate.49
  17.2 0.2 convolution_bitcast_fusion.1
  17.4 0.4 concatenate.47
  17.8 0.0 copy-start.3
  17.8 0.5 convolution_bitcast_fusion
  18.3 0.1 copy-done.3
  18.5 0.6 fusion.3
  19.1 0.3 fusion.12
  19.4 0.1 maximum_bitcast_fusion
  19.5 1.3 %copy.42 = bf16[2,4,6,64,256]{4,3,2,1,0:T(8,128)(2,1)} copy(bf16[2,4,6,64,256]{4,3,0,2,1:T(8,128)(2,1)S(1)} %maximum_bitcast_fusion) | data formatting | bytes 3145728 | tf_op jit(solution)/shard_map/transpose | solution.py:116
  20.8 7.1 %all-to-all-done = bf16[8,2,18432]{2,1,0:T(2,128)(2,1)S(1)} async-done(((bf16[8,2,18432]{2,1,0:T(2,128)(2,1)}), bf16[8,2,18432]{2,1,0:T(2,128)(2,1)S(1)}, u32[]{:S(2)}, u32[]{:S(2)}) %all-to-all-start) | async-done | bytes 589856 | tf_op jit(solution)/shard_map/all_to_all | solution.py:122
  28.0 4.4 %all-to-all-start.1 = ((bf16[8,6,1,64,256]{4,3,1,2,0:T(8,128)(2,1)}), bf16[8,6,1,64,256]{4,3,1,2,0:T(8,128)(2,1)S(1)}, u32[]{:S(2)}, u32[]{:S(2)}) async-start(bf16[8,6,1,64,256]{4,3,1,2,0:T(8,128)(2,1)} %bitcast.27), calls=%async_computation.1 | async-start | bytes 3145728 | tf_op jit(solution)/shard_map/all_to_all | solution.py:117
  32.4 0.0 copy-done.4
  32.4 0.2 broadcast_in_dim_tile.4.bias_ref
  32.6 0.4 slice.187
  32.9 1.6 %slice.143 = bf16[7,9,64,64]{3,2,1,0:T(8,128)(2,1)} reshape(bf16[7,2,18432]{2,1,0:T(2,128)(2,1)S(1)} %slice.187) | data formatting | bytes 1032192 | tf_op jit(solution)/shard_map/jit(_roll_static)/slice | solution.py:20
  34.6 0.1 slice.186
  34.6 0.1 slice.141
  34.8 1.8 %reshape.55 = bf16[8,9,64,64]{3,2,1,0:T(8,128)(2,1)} reshape(bf16[8,2,18432]{2,1,0:T(2,128)(2,1)S(1)} %all-to-all-done) | data formatting | bytes 1179648 | tf_op jit(solution)/shard_map/reshape | solution.py:122
  36.6 3.3 %maximum_maximum_fusion.pairs_ref = bf16[8,9,64,128]{3,2,1,0:T(8,128)(2,1)} fusion(bf16[7,9,64,64]{3,2,1,0:T(8,128)(2,1)} %slice.143, bf16[1,9,64,64]{3,2,1,0:T(8,128)(2,1)S(1)} %slice.141, bf16[8,9,64,64]{3,2,1,0:T(8,128)(2,1)} %reshape.55), kind=kLoop, calls=%fused_computation.7 | loop fusion | flops 3538944 | bytes 2359296 | tf_op jit(solution)/shard_map/concatenate | solution.py:20
  39.8 4.2 %shard_map.64.bank_ref = bf16[9,512,512]{2,1,0:T(8,128)(2,1)} custom-call(bf16[8,9,64,128]{3,2,1,0:T(8,128)(2,1)} %maximum_maximum_fusion.pairs_ref), custom_call_target="tpu_custom_call" | custom-call | tf_op jit(solution)/shard_map/pallas_call | solution.py:21
  44.0 9.4 %all-to-all-done.1 = bf16[8,6,1,64,256]{4,3,1,2,0:T(8,128)(2,1)S(1)} async-done(((bf16[8,6,1,64,256]{4,3,1,2,0:T(8,128)(2,1)}), bf16[8,6,1,64,256]{4,3,1,2,0:T(8,128)(2,1)S(1)}, u32[]{:S(2)}, u32[]{:S(2)}) %all-to-all-start.1) | async-done | bytes 1572896 | tf_op jit(solution)/shard_map/all_to_all | solution.py:117
  53.4 0.1 copy.43
  53.5 8.3 %shard_map.65 = bf16[8,4,64,256]{3,2,1,0:T(8,128)(2,1)S(1)} custom-call(bf16[9,512,512]{2,1,0:T(8,128)(2,1)} %shard_map.64.bank_ref, f32[512,1]{1,0:T(8,128)S(1)} %broadcast_in_dim_tile.4.bias_ref, bf16[6,512,256]{2,1,0:T(8,128)(2,1)S(1)} %bitcast.67), custom_call_target="tpu_custom_call" | custom-call | tf_op jit(solution)/shard_map/pallas_call | solution.py:51
  61.8 21.9 %all_to_all.25 = bf16[8,4,64,256]{3,2,1,0:T(8,128)(2,1)S(1)} all-to-all(bf16[8,4,64,256]{3,2,1,0:T(8,128)(2,1)S(1)} %shard_map.65), channel_id=1, replica_groups=mesh['rot'=8,'space'=32] {'rot'}, dimensions={0} | all-to-all | bytes 2097152 | tf_op jit(solution)/shard_map/all_to_all | solution.py:126
  83.7 2.1 %copy.45 = bf16[64,4,4,2,256]{4,3,2,1,0:T(2,128)(2,1)} copy(bf16[64,4,4,2,256]{4,0,2,1,3:T(8,128)(2,1)S(1)} %bitcast.72) | data formatting | bytes 2097152 | tf_op jit(solution)/shard_map/transpose | solution.py:128
  (23 shorter events, 0.2 us)
Async XLA Ops:
  0.0 1.9 %copy-start.1 = (bf16[4,16,2,256]{3,2,1,0:T(2,128)(2,1)S(1)}, bf16[4,16,2,256]{3,2,1,0:T(2,128)(2,1)}, u32[]{:S(2)}) copy-start(bf16[4,16,2,256]{3,2,1,0:T(2,128)(2,1)} %param.6) | copy-start | bytes 196612
  0.0 7.5 %copy-start = (bf16[1,9,64,64]{3,2,1,0:T(8,128)(2,1)S(1)}, bf16[1,9,64,64]{3,2,1,0:T(8,128)(2,1)}, u32[]{:S(2)}) copy-start(bf16[1,9,64,64]{3,2,1,0:T(8,128)(2,1)} %param.10) | copy-start | bytes 221188
  1.9 14.0 %copy-start.2 = (bf16[1,9,64,4]{2,3,1,0:T(4,128)(2,1)S(1)}, bf16[1,9,64,4]{2,3,1,0:T(4,128)(2,1)}, u32[]{:S(2)}) copy-start(bf16[1,9,64,4]{2,3,1,0:T(4,128)(2,1)} %param.8) | copy-start | bytes 13828
  1.9 14.0 %collective-permute-start = (bf16[72,2,256]{2,0,1:T(8,128)(2,1)S(1)}, bf16[72,2,256]{2,0,1:T(8,128)(2,1)S(1)}, u32[]{:S(2)}, u32[]{:S(2)}) collective-permute-start(bf16[72,2,256]{2,0,1:T(8,128)(2,1)S(1)} %pad_maximum_fusion), channel_id=1, source_target_pairs={{0,1},{1,2},{2,3},{3,4},{4,5},{5,6},{6,7},{7,8},{8,9},{9,10},{10,1... | collective-permute-start | bytes 221192 | tf_op jit(solution)/shard_map/ppermute | solution.py:85
  3.9 12.1 %collective-permute-start.1 = (bf16[72,2,256]{2,0,1:T(8,128)(2,1)S(1)}, bf16[72,2,256]{2,0,1:T(8,128)(2,1)S(1)}, u32[]{:S(2)}, u32[]{:S(2)}) collective-permute-start(bf16[72,2,256]{2,0,1:T(8,128)(2,1)S(1)} %pad_maximum_fusion.1), channel_id=1, source_target_pairs={{1,0},{2,1},{3,2},{4,3},{5,4},{6,5},{7,6},{8,7},{9,8},{10,9},{11,1... | collective-permute-start | bytes 221192 | tf_op jit(solution)/shard_map/ppermute | solution.py:86
  8.9 19.1 %all-to-all-start = ((bf16[8,2,18432]{2,1,0:T(2,128)(2,1)}), bf16[8,2,18432]{2,1,0:T(2,128)(2,1)S(1)}, u32[]{:S(2)}, u32[]{:S(2)}) async-start(bf16[8,2,18432]{2,1,0:T(2,128)(2,1)} %broadcast_in_dim.20), calls=%async_computation | async-start | bytes 1179648 | tf_op jit(solution)/shard_map/all_to_all | solution.py:122
  17.8 0.7 copy-start.3
  28.0 4.4 %copy-start.4 = (f32[64]{0:T(128)S(1)}, f32[64]{0:T(128)}, u32[]{:S(2)}) copy-start(f32[64]{0:T(128)} %param.11) | copy-start | bytes 772
  28.0 25.5 %all-to-all-start.1 = ((bf16[8,6,1,64,256]{4,3,1,2,0:T(8,128)(2,1)}), bf16[8,6,1,64,256]{4,3,1,2,0:T(8,128)(2,1)S(1)}, u32[]{:S(2)}, u32[]{:S(2)}) async-start(bf16[8,6,1,64,256]{4,3,1,2,0:T(8,128)(2,1)} %bitcast.27), calls=%async_computation.1 | async-start | bytes 3145728 | tf_op jit(solution)/shard_map/all_to_all | solution.py:117

commit v9 on v8

--- a/solution.py
+++ b/solution.py
@@ -62,11 +62,10 @@
     )(bank, bias, windows)
 
 
-def shards(raster, coarse_features, lift_weight, lift_bias, group_weight, group_bias):
+def layer(raster, coarse_features, lift_weight, lift_bias, group_weight, group_bias):
     n = lax.axis_size("rot")
     channels = lift_weight.shape[2]
     rows = raster.shape[1]
-    chunk = rows // n
 
     tiles, cols = raster.shape[2], raster.shape[3]
     quarters = n // tiles
@@ -119,7 +118,8 @@
 
     dense = group_weight[0].reshape(2, -1)
     spread = jnp.broadcast_to(dense, (n,) + dense.shape)
-    filters = lax.all_to_all(spread, "rot", 0, 0).reshape((n,) + group_weight.shape[1:])
+    filters = lax.all_to_all(spread, "rot", 0, 0)
+    filters = filters.reshape((n,) + group_weight.shape[1:])
     bias = jnp.tile(group_bias, n)[:, None]
     mixed = group_mix(circulant_bank(filters), bias, gathered, n)
 
@@ -131,7 +131,7 @@
 
 def solution(mesh):
     return jax.shard_map(
-        shards,
+        layer,
         mesh=mesh,
         in_specs=(
             P(None, "space", None, None),

time: 86.2 us -> 86.2 us (level)
  no operation moved by 1% of the time
where the time goes in v9:
time: 86.2 us; the launch traced here: 85.8 us
  blocking collectives  21.9 us (25%)
  starting transfers between devices  16.9 us (20%)
  waiting for transfers between devices  16.5 us (19%)
  local copies, waits for them, and re-layouts  12.5 us (15%)
  Pallas kernels  12.5 us (15%)
  other arithmetic  4.23 us (5%)
  matrix products  0.89 us (1%)
    all_to_all x1, blocking collectives, layer(): returned = lax.all_to_all(mixed, 'rot', 0, 0)  21.9 us
    all_to_all x1, waiting for transfers between devices, layer(): gathered = lax.all_to_all(windows, 'rot', 0, 1)  9.41 us
    pallas_call x1, Pallas kernels, group_mix(): pl.pallas_call(mixing_kernel, grid=(rows_out,), in_specs=[pl.BlockSpec((9...  8.27 us
    all_to_all x1, waiting for transfers between devices, layer(): filters = lax.all_to_all(spread, 'rot', 0, 0)  7.1 us
    all_to_all x1, starting transfers between devices, layer(): filters = lax.all_to_all(spread, 'rot', 0, 0)  6.93 us
    all_to_all x1, starting transfers between devices, layer(): gathered = lax.all_to_all(windows, 'rot', 0, 1)  4.4 us
    pallas_call x1, Pallas kernels, circulant_bank(): pl.pallas_call(bank_kernel, out_shape=jax.ShapeDtypeStruct((taps, count *...  4.2 us
    ppermute x1, starting transfers between devices, layer(): lax.ppermute(edges(raster[:, :2], coarse_own[:, 0]), 'space', [(j, i) for...  3.64 us
  transfers between devices with their start and end apart: 4, of which 2 were waited for; matrix products, arithmetic and copies ran while one was open for 16% of the time, Pallas kernels for 5%

profile of v9, /device:TPU:96, one launch (start us, length us, event | category | flops | bytes accessed | tf_op | source)
XLA Modules:
  0.0 85.8 jit_solution(2126447629450809470)
XLA Ops:
  0.0 0.0 copy-start.1
  0.0 0.0 copy-start
  0.0 1.8 %copy.50 = bf16[1,64,16,2,256]{4,1,3,2,0:T(8,128)(2,1)S(1)} copy(bf16[1,64,16,2,256]{4,3,2,1,0:T(2,128)(2,1)} %param.7) | data formatting | bytes 2097152 | tf_op args[1]
  1.9 0.0 copy-start.2
  1.9 0.0 copy-done.1
  1.9 1.9 %collective-permute-start = (bf16[72,2,256]{2,0,1:T(8,128)(2,1)S(1)}, bf16[72,2,256]{2,0,1:T(8,128)(2,1)S(1)}, u32[]{:S(2)}, u32[]{:S(2)}) collective-permute-start(bf16[72,2,256]{2,0,1:T(8,128)(2,1)S(1)} %pad_maximum_fusion), channel_id=1, source_target_pairs={{0,1},{1,2},{2,3},{3,4},{4,5},{5,6},{6,7},{7,8},{8,9},{9,10},{10,1... | collective-permute-start | bytes 221192 | tf_op jit(solution)/shard_map/ppermute | solution.py:84
  3.9 3.6 %collective-permute-start.1 = (bf16[72,2,256]{2,0,1:T(8,128)(2,1)S(1)}, bf16[72,2,256]{2,0,1:T(8,128)(2,1)S(1)}, u32[]{:S(2)}, u32[]{:S(2)}) collective-permute-start(bf16[72,2,256]{2,0,1:T(8,128)(2,1)S(1)} %pad_maximum_fusion.1), channel_id=1, source_target_pairs={{1,0},{2,1},{3,2},{4,3},{5,4},{6,5},{7,6},{8,7},{9,8},{10,9},{11,1... | collective-permute-start | bytes 221192 | tf_op jit(solution)/shard_map/ppermute | solution.py:85
  7.6 0.0 copy-done
  7.6 0.2 reshape_squeeze.6
  7.7 1.1 %broadcast_in_dim.20 = bf16[8,2,18432]{2,1,0:T(2,128)(2,1)} broadcast(bf16[2,18432]{1,0:T(2,128)(2,1)S(1)} %reshape_squeeze.6), dimensions={1,2} | broadcast | bytes 663552 | tf_op jit(solution)/shard_map/broadcast_in_dim | solution.py:120
  8.9 6.9 %all-to-all-start = ((bf16[8,2,18432]{2,1,0:T(2,128)(2,1)}), bf16[8,2,18432]{2,1,0:T(2,128)(2,1)S(1)}, u32[]{:S(2)}, u32[]{:S(2)}) async-start(bf16[8,2,18432]{2,1,0:T(2,128)(2,1)} %broadcast_in_dim.20), calls=%async_computation | async-start | bytes 1179648 | tf_op jit(solution)/shard_map/all_to_all | solution.py:121
  15.8 0.1 copy.33
  15.9 0.0 copy-done.2
  15.9 0.0 collective-permute-done
  16.0 0.0 collective-permute-done.1
  16.1 0.1 fusion.9
  16.2 0.1 fusion.16
  16.3 0.1 fusion.5
  16.4 0.3 fusion.13
  16.7 0.1 fusion.17
  16.8 0.1 concatenate.44
  16.9 0.2 convolution_bitcast_fusion.2
  17.1 0.1 concatenate.49
  17.2 0.2 convolution_bitcast_fusion.1
  17.4 0.4 concatenate.47
  17.8 0.0 copy-start.3
  17.8 0.5 convolution_bitcast_fusion
  18.3 0.1 copy-done.3
  18.5 0.6 fusion.3
  19.1 0.3 fusion.12
  19.4 0.1 maximum_bitcast_fusion
  19.5 1.3 %copy.42 = bf16[2,4,6,64,256]{4,3,2,1,0:T(8,128)(2,1)} copy(bf16[2,4,6,64,256]{4,3,0,2,1:T(8,128)(2,1)S(1)} %maximum_bitcast_fusion) | data formatting | bytes 3145728 | tf_op jit(solution)/shard_map/transpose | solution.py:115
  20.8 7.1 %all-to-all-done = bf16[8,2,18432]{2,1,0:T(2,128)(2,1)S(1)} async-done(((bf16[8,2,18432]{2,1,0:T(2,128)(2,1)}), bf16[8,2,18432]{2,1,0:T(2,128)(2,1)S(1)}, u32[]{:S(2)}, u32[]{:S(2)}) %all-to-all-start) | async-done | bytes 589856 | tf_op jit(solution)/shard_map/all_to_all | solution.py:121
  28.0 4.4 %all-to-all-start.1 = ((bf16[8,6,1,64,256]{4,3,1,2,0:T(8,128)(2,1)}), bf16[8,6,1,64,256]{4,3,1,2,0:T(8,128)(2,1)S(1)}, u32[]{:S(2)}, u32[]{:S(2)}) async-start(bf16[8,6,1,64,256]{4,3,1,2,0:T(8,128)(2,1)} %bitcast.27), calls=%async_computation.1 | async-start | bytes 3145728 | tf_op jit(solution)/shard_map/all_to_all | solution.py:116
  32.4 0.0 copy-done.4
  32.4 0.2 broadcast_in_dim_tile.4.bias_ref
  32.6 0.4 slice.187
  32.9 1.6 %slice.143 = bf16[7,9,64,64]{3,2,1,0:T(8,128)(2,1)} reshape(bf16[7,2,18432]{2,1,0:T(2,128)(2,1)S(1)} %slice.187) | data formatting | bytes 1032192 | tf_op jit(solution)/shard_map/jit(_roll_static)/slice | solution.py:20
  34.6 0.1 slice.186
  34.6 0.1 slice.141
  34.8 1.8 %reshape.55 = bf16[8,9,64,64]{3,2,1,0:T(8,128)(2,1)} reshape(bf16[8,2,18432]{2,1,0:T(2,128)(2,1)S(1)} %all-to-all-done) | data formatting | bytes 1179648 | tf_op jit(solution)/shard_map/reshape | solution.py:122
  36.6 3.3 %maximum_maximum_fusion.pairs_ref = bf16[8,9,64,128]{3,2,1,0:T(8,128)(2,1)} fusion(bf16[7,9,64,64]{3,2,1,0:T(8,128)(2,1)} %slice.143, bf16[1,9,64,64]{3,2,1,0:T(8,128)(2,1)S(1)} %slice.141, bf16[8,9,64,64]{3,2,1,0:T(8,128)(2,1)} %reshape.55), kind=kLoop, calls=%fused_computation.7 | loop fusion | flops 3538944 | bytes 2359296 | tf_op jit(solution)/shard_map/concatenate | solution.py:20
  39.8 4.2 %shard_map.64.bank_ref = bf16[9,512,512]{2,1,0:T(8,128)(2,1)} custom-call(bf16[8,9,64,128]{3,2,1,0:T(8,128)(2,1)} %maximum_maximum_fusion.pairs_ref), custom_call_target="tpu_custom_call" | custom-call | tf_op jit(solution)/shard_map/pallas_call | solution.py:21
  44.0 9.4 %all-to-all-done.1 = bf16[8,6,1,64,256]{4,3,1,2,0:T(8,128)(2,1)S(1)} async-done(((bf16[8,6,1,64,256]{4,3,1,2,0:T(8,128)(2,1)}), bf16[8,6,1,64,256]{4,3,1,2,0:T(8,128)(2,1)S(1)}, u32[]{:S(2)}, u32[]{:S(2)}) %all-to-all-start.1) | async-done | bytes 1572896 | tf_op jit(solution)/shard_map/all_to_all | solution.py:116
  53.4 0.1 copy.43
  53.5 8.3 %shard_map.65 = bf16[8,4,64,256]{3,2,1,0:T(8,128)(2,1)S(1)} custom-call(bf16[9,512,512]{2,1,0:T(8,128)(2,1)} %shard_map.64.bank_ref, f32[512,1]{1,0:T(8,128)S(1)} %broadcast_in_dim_tile.4.bias_ref, bf16[6,512,256]{2,1,0:T(8,128)(2,1)S(1)} %bitcast.67), custom_call_target="tpu_custom_call" | custom-call | tf_op jit(solution)/shard_map/pallas_call | solution.py:51
  61.8 21.9 %all_to_all.25 = bf16[8,4,64,256]{3,2,1,0:T(8,128)(2,1)S(1)} all-to-all(bf16[8,4,64,256]{3,2,1,0:T(8,128)(2,1)S(1)} %shard_map.65), channel_id=1, replica_groups=mesh['rot'=8,'space'=32] {'rot'}, dimensions={0} | all-to-all | bytes 2097152 | tf_op jit(solution)/shard_map/all_to_all | solution.py:126
  83.7 2.1 %copy.45 = bf16[64,4,4,2,256]{4,3,2,1,0:T(2,128)(2,1)} copy(bf16[64,4,4,2,256]{4,0,2,1,3:T(8,128)(2,1)S(1)} %bitcast.72) | data formatting | bytes 2097152 | tf_op jit(solution)/shard_map/transpose | solution.py:128
  (23 shorter events, 0.2 us)
Async XLA Ops:
  0.0 1.9 %copy-start.1 = (bf16[4,16,2,256]{3,2,1,0:T(2,128)(2,1)S(1)}, bf16[4,16,2,256]{3,2,1,0:T(2,128)(2,1)}, u32[]{:S(2)}) copy-start(bf16[4,16,2,256]{3,2,1,0:T(2,128)(2,1)} %param.6) | copy-start | bytes 196612
  0.0 7.5 %copy-start = (bf16[1,9,64,64]{3,2,1,0:T(8,128)(2,1)S(1)}, bf16[1,9,64,64]{3,2,1,0:T(8,128)(2,1)}, u32[]{:S(2)}) copy-start(bf16[1,9,64,64]{3,2,1,0:T(8,128)(2,1)} %param.10) | copy-start | bytes 221188
  1.9 14.0 %copy-start.2 = (bf16[1,9,64,4]{2,3,1,0:T(4,128)(2,1)S(1)}, bf16[1,9,64,4]{2,3,1,0:T(4,128)(2,1)}, u32[]{:S(2)}) copy-start(bf16[1,9,64,4]{2,3,1,0:T(4,128)(2,1)} %param.8) | copy-start | bytes 13828
  1.9 14.0 %collective-permute-start = (bf16[72,2,256]{2,0,1:T(8,128)(2,1)S(1)}, bf16[72,2,256]{2,0,1:T(8,128)(2,1)S(1)}, u32[]{:S(2)}, u32[]{:S(2)}) collective-permute-start(bf16[72,2,256]{2,0,1:T(8,128)(2,1)S(1)} %pad_maximum_fusion), channel_id=1, source_target_pairs={{0,1},{1,2},{2,3},{3,4},{4,5},{5,6},{6,7},{7,8},{8,9},{9,10},{10,1... | collective-permute-start | bytes 221192 | tf_op jit(solution)/shard_map/ppermute | solution.py:84
  3.9 12.1 %collective-permute-start.1 = (bf16[72,2,256]{2,0,1:T(8,128)(2,1)S(1)}, bf16[72,2,256]{2,0,1:T(8,128)(2,1)S(1)}, u32[]{:S(2)}, u32[]{:S(2)}) collective-permute-start(bf16[72,2,256]{2,0,1:T(8,128)(2,1)S(1)} %pad_maximum_fusion.1), channel_id=1, source_target_pairs={{1,0},{2,1},{3,2},{4,3},{5,4},{6,5},{7,6},{8,7},{9,8},{10,9},{11,1... | collective-permute-start | bytes 221192 | tf_op jit(solution)/shard_map/ppermute | solution.py:85
  8.9 19.1 %all-to-all-start = ((bf16[8,2,18432]{2,1,0:T(2,128)(2,1)}), bf16[8,2,18432]{2,1,0:T(2,128)(2,1)S(1)}, u32[]{:S(2)}, u32[]{:S(2)}) async-start(bf16[8,2,18432]{2,1,0:T(2,128)(2,1)} %broadcast_in_dim.20), calls=%async_computation | async-start | bytes 1179648 | tf_op jit(solution)/shard_map/all_to_all | solution.py:121
  17.8 0.7 copy-start.3
  28.0 4.4 %copy-start.4 = (f32[64]{0:T(128)S(1)}, f32[64]{0:T(128)}, u32[]{:S(2)}) copy-start(f32[64]{0:T(128)} %param.11) | copy-start | bytes 772
  28.0 25.5 %all-to-all-start.1 = ((bf16[8,6,1,64,256]{4,3,1,2,0:T(8,128)(2,1)}), bf16[8,6,1,64,256]{4,3,1,2,0:T(8,128)(2,1)S(1)}, u32[]{:S(2)}, u32[]{:S(2)}) async-start(bf16[8,6,1,64,256]{4,3,1,2,0:T(8,128)(2,1)} %bitcast.27), calls=%async_computation.1 | async-start | bytes 3145728 | tf_op jit(solution)/shard_map/all_to_all | solution.py:116

commit v10 on v9

--- a/solution.py
+++ b/solution.py
@@ -24,24 +24,29 @@
     )(pairs)
 
 
-def mixing_kernel(bank_ref, bias_ref, x_ref, o_ref):
-    row = pl.program_id(0)
+def mixing_kernel(bank_ref, bias_ref, x_ref, o_ref, acc_ref):
+    dx, row = pl.program_id(0), pl.program_id(1)
     count, channels, cols = o_ref.shape[0], o_ref.shape[2], o_ref.shape[3]
-    planes = [x_ref[row + dy] for dy in range(3)]
-    sums = []
-    for dx in range(3):
-        total = None
-        for dy in range(3):
-            term = jnp.dot(bank_ref[3 * dy + dx], planes[dy], preferred_element_type=jnp.float32)
-            total = term if total is None else total + term
-        sums.append(total)
-    column = lax.broadcasted_iota(jnp.int32, sums[0].shape, 1)
-    left = jnp.where(column == 0, 0.0, pltpu.roll(sums[0], 1, 1))
-    right = jnp.where(column == cols - 1, 0.0, pltpu.roll(sums[2], cols - 1, 1))
-    mixed = sums[1] + left + right + bias_ref[...]
-    mixed = jnp.maximum(mixed, 0.0).astype(o_ref.dtype)
-    for g in range(count):
-        o_ref[g, 0] = mixed[g * channels : (g + 1) * channels]
+    total = None
+    for dy in range(3):
+        term = jnp.dot(bank_ref[dy, 0], x_ref[row + dy], preferred_element_type=jnp.float32)
+        total = term if total is None else total + term
+    column = lax.broadcasted_iota(jnp.int32, total.shape, 1)
+
+    @pl.when(dx == 0)
+    def _():
+        acc_ref[row] = jnp.where(column == 0, 0.0, pltpu.roll(total, 1, 1))
+
+    @pl.when(dx == 1)
+    def _():
+        acc_ref[row] += total
+
+    @pl.when(dx == 2)
+    def _():
+        right = jnp.where(column == cols - 1, 0.0, pltpu.roll(total, cols - 1, 1))
+        mixed = jnp.maximum(acc_ref[row] + right + bias_ref[...], 0.0).astype(o_ref.dtype)
+        for g in range(count):
+            o_ref[g, 0] = mixed[g * channels : (g + 1) * channels]
 
 
 def group_mix(bank, bias, windows, count):
@@ -50,16 +55,17 @@
     rows_out = rows_in - 2
     return pl.pallas_call(
         mixing_kernel,
-        grid=(rows_out,),
+        grid=(3, rows_out),
         in_specs=[
-            pl.BlockSpec((9, full, full), lambda r: (0, 0, 0)),
-            pl.BlockSpec((full, 1), lambda r: (0, 0)),
-            pl.BlockSpec(windows.shape, lambda r: (0, 0, 0)),
+            pl.BlockSpec((3, 1, full, full), lambda dx, r: (0, dx, 0, 0)),
+            pl.BlockSpec((full, 1), lambda dx, r: (0, 0)),
+            pl.BlockSpec(windows.shape, lambda dx, r: (0, 0, 0)),
         ],
-        out_specs=pl.BlockSpec((count, 1, channels, cols), lambda r: (0, r, 0, 0)),
+        out_specs=pl.BlockSpec((count, 1, channels, cols), lambda dx, r: (0, jnp.where(dx == 2, r, 0), 0, 0)),
         out_shape=jax.ShapeDtypeStruct((count, rows_out, channels, cols), jnp.bfloat16),
+        scratch_shapes=[pltpu.VMEM((rows_out, full, cols), jnp.float32)],
         compiler_params=pltpu.CompilerParams(vmem_limit_bytes=48 * 1024 * 1024),
-    )(bank, bias, windows)
+    )(bank.reshape(3, 3, full, full), bias, windows)
 
 
 def layer(raster, coarse_features, lift_weight, lift_bias, group_weight, group_bias):

time: 86.2 us -> 90.3 us (1.048)
  Pallas kernels: 12.5 us -> 16.5 us
    pallas_call x1, Pallas kernels: 8.27 us -> 12.3 us  [group_mix(): pl.pallas_call(mixing_kernel, grid=(3, rows_out), in_specs=[pl.BlockSpec(...]
  transfers between devices with their start and end apart: 4 -> 4, of which waited for: 2 -> 2; matrix products, arithmetic and copies ran while one was open for 16% -> 15% of each run, Pallas kernels for 5% -> 5%
where the time goes in v10:
time: 90.3 us; the launch traced here: 89.8 us
  blocking collectives  21.9 us (24%)
  starting transfers between devices  16.9 us (19%)
  waiting for transfers between devices  16.5 us (18%)
  Pallas kernels  16.5 us (18%)
  local copies, waits for them, and re-layouts  12.5 us (14%)
  other arithmetic  4.23 us (5%)
    all_to_all x1, blocking collectives, layer(): returned = lax.all_to_all(mixed, 'rot', 0, 0)  21.9 us
    pallas_call x1, Pallas kernels, group_mix(): pl.pallas_call(mixing_kernel, grid=(3, rows_out), in_specs=[pl.BlockSpec(...  12.3 us
    all_to_all x1, waiting for transfers between devices, layer(): gathered = lax.all_to_all(windows, 'rot', 0, 1)  9.41 us
    all_to_all x1, waiting for transfers between devices, layer(): filters = lax.all_to_all(spread, 'rot', 0, 0)  7.1 us
    all_to_all x1, starting transfers between devices, layer(): filters = lax.all_to_all(spread, 'rot', 0, 0)  6.93 us
    all_to_all x1, starting transfers between devices, layer(): gathered = lax.all_to_all(windows, 'rot', 0, 1)  4.4 us
    pallas_call x1, Pallas kernels, circulant_bank(): pl.pallas_call(bank_kernel, out_shape=jax.ShapeDtypeStruct((taps, count *...  4.2 us
    ppermute x1, starting transfers between devices, layer(): lax.ppermute(edges(raster[:, :2], coarse_own[:, 0]), 'space', [(j, i) for...  3.64 us
  transfers between devices with their start and end apart: 4, of which 2 were waited for; matrix products, arithmetic and copies ran while one was open for 15% of the time, Pallas kernels for 5%

profile of v10, /device:TPU:96, one launch (start us, length us, event | category | flops | bytes accessed | tf_op | source)
XLA Modules:
  0.0 89.8 jit_solution(12747260786918286466)
XLA Ops:
  0.0 0.0 copy-start.1
  0.0 0.0 copy-start
  0.0 1.8 %copy.50 = bf16[1,64,16,2,256]{4,1,3,2,0:T(8,128)(2,1)S(1)} copy(bf16[1,64,16,2,256]{4,3,2,1,0:T(2,128)(2,1)} %param.7) | data formatting | bytes 2097152 | tf_op args[1]
  1.9 0.0 copy-start.2
  1.9 0.0 copy-done.1
  1.9 1.9 %collective-permute-start = (bf16[72,2,256]{2,0,1:T(8,128)(2,1)S(1)}, bf16[72,2,256]{2,0,1:T(8,128)(2,1)S(1)}, u32[]{:S(2)}, u32[]{:S(2)}) collective-permute-start(bf16[72,2,256]{2,0,1:T(8,128)(2,1)S(1)} %pad_maximum_fusion), channel_id=1, source_target_pairs={{0,1},{1,2},{2,3},{3,4},{4,5},{5,6},{6,7},{7,8},{8,9},{9,10},{10,1... | collective-permute-start | bytes 221192 | tf_op jit(solution)/shard_map/ppermute | solution.py:90
  3.9 3.6 %collective-permute-start.1 = (bf16[72,2,256]{2,0,1:T(8,128)(2,1)S(1)}, bf16[72,2,256]{2,0,1:T(8,128)(2,1)S(1)}, u32[]{:S(2)}, u32[]{:S(2)}) collective-permute-start(bf16[72,2,256]{2,0,1:T(8,128)(2,1)S(1)} %pad_maximum_fusion.1), channel_id=1, source_target_pairs={{1,0},{2,1},{3,2},{4,3},{5,4},{6,5},{7,6},{8,7},{9,8},{10,9},{11,1... | collective-permute-start | bytes 221192 | tf_op jit(solution)/shard_map/ppermute | solution.py:91
  7.6 0.0 copy-done
  7.6 0.2 reshape_squeeze.6
  7.7 1.1 %broadcast_in_dim.20 = bf16[8,2,18432]{2,1,0:T(2,128)(2,1)} broadcast(bf16[2,18432]{1,0:T(2,128)(2,1)S(1)} %reshape_squeeze.6), dimensions={1,2} | broadcast | bytes 663552 | tf_op jit(solution)/shard_map/broadcast_in_dim | solution.py:126
  8.9 6.9 %all-to-all-start = ((bf16[8,2,18432]{2,1,0:T(2,128)(2,1)}), bf16[8,2,18432]{2,1,0:T(2,128)(2,1)S(1)}, u32[]{:S(2)}, u32[]{:S(2)}) async-start(bf16[8,2,18432]{2,1,0:T(2,128)(2,1)} %broadcast_in_dim.20), calls=%async_computation | async-start | bytes 1179648 | tf_op jit(solution)/shard_map/all_to_all | solution.py:127
  15.8 0.1 copy.33
  15.9 0.0 copy-done.2
  15.9 0.0 collective-permute-done
  16.0 0.0 collective-permute-done.1
  16.1 0.1 fusion.9
  16.2 0.1 fusion.16
  16.3 0.1 fusion.5
  16.4 0.3 fusion.13
  16.7 0.1 fusion.17
  16.8 0.1 concatenate.44
  16.9 0.2 convolution_bitcast_fusion.2
  17.1 0.1 concatenate.49
  17.2 0.2 convolution_bitcast_fusion.1
  17.4 0.4 concatenate.47
  17.8 0.0 copy-start.3
  17.8 0.5 convolution_bitcast_fusion
  18.3 0.1 copy-done.3
  18.5 0.6 fusion.3
  19.1 0.3 fusion.12
  19.4 0.1 maximum_bitcast_fusion
  19.5 1.3 %copy.42 = bf16[2,4,6,64,256]{4,3,2,1,0:T(8,128)(2,1)} copy(bf16[2,4,6,64,256]{4,3,0,2,1:T(8,128)(2,1)S(1)} %maximum_bitcast_fusion) | data formatting | bytes 3145728 | tf_op jit(solution)/shard_map/transpose | solution.py:121
  20.8 7.1 %all-to-all-done = bf16[8,2,18432]{2,1,0:T(2,128)(2,1)S(1)} async-done(((bf16[8,2,18432]{2,1,0:T(2,128)(2,1)}), bf16[8,2,18432]{2,1,0:T(2,128)(2,1)S(1)}, u32[]{:S(2)}, u32[]{:S(2)}) %all-to-all-start) | async-done | bytes 589856 | tf_op jit(solution)/shard_map/all_to_all | solution.py:127
  28.0 4.4 %all-to-all-start.1 = ((bf16[8,6,1,64,256]{4,3,1,2,0:T(8,128)(2,1)}), bf16[8,6,1,64,256]{4,3,1,2,0:T(8,128)(2,1)S(1)}, u32[]{:S(2)}, u32[]{:S(2)}) async-start(bf16[8,6,1,64,256]{4,3,1,2,0:T(8,128)(2,1)} %bitcast.28), calls=%async_computation.1 | async-start | bytes 3145728 | tf_op jit(solution)/shard_map/all_to_all | solution.py:122
  32.4 0.0 copy-done.4
  32.4 0.2 broadcast_in_dim_tile.4.bias_ref
  32.6 0.4 slice.187
  32.9 1.6 %slice.143 = bf16[7,9,64,64]{3,2,1,0:T(8,128)(2,1)} reshape(bf16[7,2,18432]{2,1,0:T(2,128)(2,1)S(1)} %slice.187) | data formatting | bytes 1032192 | tf_op jit(solution)/shard_map/jit(_roll_static)/slice | solution.py:20
  34.6 0.1 slice.186
  34.6 0.1 slice.141
  34.8 1.8 %reshape.58 = bf16[8,9,64,64]{3,2,1,0:T(8,128)(2,1)} reshape(bf16[8,2,18432]{2,1,0:T(2,128)(2,1)S(1)} %all-to-all-done) | data formatting | bytes 1179648 | tf_op jit(solution)/shard_map/reshape | solution.py:128
  36.6 3.3 %maximum_maximum_fusion.pairs_ref = bf16[8,9,64,128]{3,2,1,0:T(8,128)(2,1)} fusion(bf16[7,9,64,64]{3,2,1,0:T(8,128)(2,1)} %slice.143, bf16[1,9,64,64]{3,2,1,0:T(8,128)(2,1)S(1)} %slice.141, bf16[8,9,64,64]{3,2,1,0:T(8,128)(2,1)} %reshape.58), kind=kLoop, calls=%fused_computation.7 | loop fusion | flops 3538944 | bytes 2359296 | tf_op jit(solution)/shard_map/concatenate | solution.py:20
  39.8 4.2 %shard_map.64 = bf16[9,512,512]{2,1,0:T(8,128)(2,1)} custom-call(bf16[8,9,64,128]{3,2,1,0:T(8,128)(2,1)} %maximum_maximum_fusion.pairs_ref), custom_call_target="tpu_custom_call" | custom-call | tf_op jit(solution)/shard_map/pallas_call | solution.py:21
  44.0 9.4 %all-to-all-done.1 = bf16[8,6,1,64,256]{4,3,1,2,0:T(8,128)(2,1)S(1)} async-done(((bf16[8,6,1,64,256]{4,3,1,2,0:T(8,128)(2,1)}), bf16[8,6,1,64,256]{4,3,1,2,0:T(8,128)(2,1)S(1)}, u32[]{:S(2)}, u32[]{:S(2)}) %all-to-all-start.1) | async-done | bytes 1572896 | tf_op jit(solution)/shard_map/all_to_all | solution.py:122
  53.4 0.1 copy.43
  53.5 12.3 %shard_map.65 = bf16[8,4,64,256]{3,2,1,0:T(8,128)(2,1)S(1)} custom-call(bf16[3,3,512,512]{3,2,1,0:T(8,128)(2,1)} %bitcast.69, f32[512,1]{1,0:T(8,128)S(1)} %broadcast_in_dim_tile.4.bias_ref, bf16[6,512,256]{2,1,0:T(8,128)(2,1)S(1)} %bitcast.68), custom_call_target="tpu_custom_call" | custom-call | tf_op jit(solution)/shard_map/pallas_call | solution.py:56
  65.8 21.9 %all_to_all.25 = bf16[8,4,64,256]{3,2,1,0:T(8,128)(2,1)S(1)} all-to-all(bf16[8,4,64,256]{3,2,1,0:T(8,128)(2,1)S(1)} %shard_map.65), channel_id=1, replica_groups=mesh['rot'=8,'space'=32] {'rot'}, dimensions={0} | all-to-all | bytes 2097152 | tf_op jit(solution)/shard_map/all_to_all | solution.py:132
  87.7 2.1 %copy.45 = bf16[64,4,4,2,256]{4,3,2,1,0:T(2,128)(2,1)} copy(bf16[64,4,4,2,256]{4,0,2,1,3:T(8,128)(2,1)S(1)} %bitcast.74) | data formatting | bytes 2097152 | tf_op jit(solution)/shard_map/transpose | solution.py:134
  (23 shorter events, 0.2 us)
Async XLA Ops:
  0.0 1.9 %copy-start.1 = (bf16[4,16,2,256]{3,2,1,0:T(2,128)(2,1)S(1)}, bf16[4,16,2,256]{3,2,1,0:T(2,128)(2,1)}, u32[]{:S(2)}) copy-start(bf16[4,16,2,256]{3,2,1,0:T(2,128)(2,1)} %param.6) | copy-start | bytes 196612
  0.0 7.5 %copy-start = (bf16[1,9,64,64]{3,2,1,0:T(8,128)(2,1)S(1)}, bf16[1,9,64,64]{3,2,1,0:T(8,128)(2,1)}, u32[]{:S(2)}) copy-start(bf16[1,9,64,64]{3,2,1,0:T(8,128)(2,1)} %param.10) | copy-start | bytes 221188
  1.9 14.0 %copy-start.2 = (bf16[1,9,64,4]{2,3,1,0:T(4,128)(2,1)S(1)}, bf16[1,9,64,4]{2,3,1,0:T(4,128)(2,1)}, u32[]{:S(2)}) copy-start(bf16[1,9,64,4]{2,3,1,0:T(4,128)(2,1)} %param.8) | copy-start | bytes 13828
  1.9 14.0 %collective-permute-start = (bf16[72,2,256]{2,0,1:T(8,128)(2,1)S(1)}, bf16[72,2,256]{2,0,1:T(8,128)(2,1)S(1)}, u32[]{:S(2)}, u32[]{:S(2)}) collective-permute-start(bf16[72,2,256]{2,0,1:T(8,128)(2,1)S(1)} %pad_maximum_fusion), channel_id=1, source_target_pairs={{0,1},{1,2},{2,3},{3,4},{4,5},{5,6},{6,7},{7,8},{8,9},{9,10},{10,1... | collective-permute-start | bytes 221192 | tf_op jit(solution)/shard_map/ppermute | solution.py:90
  3.9 12.1 %collective-permute-start.1 = (bf16[72,2,256]{2,0,1:T(8,128)(2,1)S(1)}, bf16[72,2,256]{2,0,1:T(8,128)(2,1)S(1)}, u32[]{:S(2)}, u32[]{:S(2)}) collective-permute-start(bf16[72,2,256]{2,0,1:T(8,128)(2,1)S(1)} %pad_maximum_fusion.1), channel_id=1, source_target_pairs={{1,0},{2,1},{3,2},{4,3},{5,4},{6,5},{7,6},{8,7},{9,8},{10,9},{11,1... | collective-permute-start | bytes 221192 | tf_op jit(solution)/shard_map/ppermute | solution.py:91
  8.9 19.1 %all-to-all-start = ((bf16[8,2,18432]{2,1,0:T(2,128)(2,1)}), bf16[8,2,18432]{2,1,0:T(2,128)(2,1)S(1)}, u32[]{:S(2)}, u32[]{:S(2)}) async-start(bf16[8,2,18432]{2,1,0:T(2,128)(2,1)} %broadcast_in_dim.20), calls=%async_computation | async-start | bytes 1179648 | tf_op jit(solution)/shard_map/all_to_all | solution.py:127
  17.8 0.7 copy-start.3
  28.0 4.4 %copy-start.4 = (f32[64]{0:T(128)S(1)}, f32[64]{0:T(128)}, u32[]{:S(2)}) copy-start(f32[64]{0:T(128)} %param.11) | copy-start | bytes 772
  28.0 25.5 %all-to-all-start.1 = ((bf16[8,6,1,64,256]{4,3,1,2,0:T(8,128)(2,1)}), bf16[8,6,1,64,256]{4,3,1,2,0:T(8,128)(2,1)S(1)}, u32[]{:S(2)}, u32[]{:S(2)}) async-start(bf16[8,6,1,64,256]{4,3,1,2,0:T(8,128)(2,1)} %bitcast.28), calls=%async_computation.1 | async-start | bytes 3145728 | tf_op jit(solution)/shard_map/all_to_all | solution.py:122

commit v11 on v9

--- a/solution.py
+++ b/solution.py
@@ -25,9 +25,9 @@
 
 
 def mixing_kernel(bank_ref, bias_ref, x_ref, o_ref):
-    row = pl.program_id(0)
-    count, channels, cols = o_ref.shape[0], o_ref.shape[2], o_ref.shape[3]
-    planes = [x_ref[row + dy] for dy in range(3)]
+    count, rows_out, channels, cols = o_ref.shape
+    width = rows_out * cols
+    planes = [x_ref[:, dy * cols : dy * cols + width] for dy in range(3)]
     sums = []
     for dx in range(3):
         total = None
@@ -35,28 +35,22 @@
             term = jnp.dot(bank_ref[3 * dy + dx], planes[dy], preferred_element_type=jnp.float32)
             total = term if total is None else total + term
         sums.append(total)
-    column = lax.broadcasted_iota(jnp.int32, sums[0].shape, 1)
+    column = lax.broadcasted_iota(jnp.int32, sums[0].shape, 1) % cols
     left = jnp.where(column == 0, 0.0, pltpu.roll(sums[0], 1, 1))
-    right = jnp.where(column == cols - 1, 0.0, pltpu.roll(sums[2], cols - 1, 1))
+    right = jnp.where(column == cols - 1, 0.0, pltpu.roll(sums[2], width - 1, 1))
     mixed = sums[1] + left + right + bias_ref[...]
     mixed = jnp.maximum(mixed, 0.0).astype(o_ref.dtype)
     for g in range(count):
-        o_ref[g, 0] = mixed[g * channels : (g + 1) * channels]
+        for row in range(rows_out):
+            o_ref[g, row] = mixed[g * channels : (g + 1) * channels, row * cols : (row + 1) * cols]
 
 
-def group_mix(bank, bias, windows, count):
-    rows_in, full, cols = windows.shape
+def group_mix(bank, bias, windows, count, cols):
+    full, wide = windows.shape
     channels = full // count
-    rows_out = rows_in - 2
+    rows_out = wide // cols - 2
     return pl.pallas_call(
         mixing_kernel,
-        grid=(rows_out,),
-        in_specs=[
-            pl.BlockSpec((9, full, full), lambda r: (0, 0, 0)),
-            pl.BlockSpec((full, 1), lambda r: (0, 0)),
-            pl.BlockSpec(windows.shape, lambda r: (0, 0, 0)),
-        ],
-        out_specs=pl.BlockSpec((count, 1, channels, cols), lambda r: (0, r, 0, 0)),
         out_shape=jax.ShapeDtypeStruct((count, rows_out, channels, cols), jnp.bfloat16),
         compiler_params=pltpu.CompilerParams(vmem_limit_bytes=48 * 1024 * 1024),
     )(bank, bias, windows)
@@ -112,16 +106,15 @@
     top = lax.slice_in_dim(hidden_ext, 0, rows, axis=0).reshape(split)
     bottom = lax.slice_in_dim(hidden_ext, 2, rows + 2, axis=0).reshape(split)
     windows = jnp.concatenate([top, lax.slice_in_dim(bottom, span - 2, span, axis=1)], axis=1)
-    windows = jnp.transpose(windows, (2, 0, 1, 3, 4)).reshape((n, span + 2) + hidden_ext.shape[2:])
-    gathered = lax.all_to_all(windows, "rot", 0, 1)
-    gathered = gathered.reshape((gathered.shape[0], n * channels, cols))
+    windows = jnp.transpose(windows, (2, 0, 3, 1, 4)).reshape((n, channels, (span + 2) * cols))
+    gathered = lax.all_to_all(windows, "rot", 0, 0).reshape((n * channels, (span + 2) * cols))
 
     dense = group_weight[0].reshape(2, -1)
     spread = jnp.broadcast_to(dense, (n,) + dense.shape)
     filters = lax.all_to_all(spread, "rot", 0, 0)
     filters = filters.reshape((n,) + group_weight.shape[1:])
     bias = jnp.tile(group_bias, n)[:, None]
-    mixed = group_mix(circulant_bank(filters), bias, gathered, n)
+    mixed = group_mix(circulant_bank(filters), bias, gathered, n, cols)
 
     returned = lax.all_to_all(mixed, "rot", 0, 0)
     returned = returned.reshape((tiles, quarters) + returned.shape[1:])

time: 86.2 us -> 85.7 us (level)
  waiting for transfers between devices: 16.5 us -> 11.4 us
  local copies, waits for them, and re-layouts: 12.5 us -> 17 us
    all_to_all x1, waiting for transfers between devices: 7.1 us -> 3.6 us  [layer(): filters = lax.all_to_all(spread, 'rot', 0, 0)]
    reshape x0 -> x2, local copies, waits for them, and re-layouts: none -> 3.45 us  [the longest x1 2.63 us: layer(): jnp.transpose(windows, (2, 0, 3, 1, 4))]
    slice x4, local copies, waits for them, and re-layouts: 2.18 us -> 4.3 us  [circulant_bank(): pairs = jnp.concatenate([filters, jnp.roll(filters, 1, axis=0)], axis=-1)]
    all_to_all x1, waiting for transfers between devices: 9.41 us -> 7.83 us  [layer(): lax.all_to_all(windows, 'rot', 0, 0)]
    transpose x1 -> x0, local copies, waits for them, and re-layouts: 1.31 us -> none  [layer(): jnp.transpose(windows, (2, 0, 1, 3, 4))]
    transpose x1, other arithmetic: 0.14 us -> 1.1 us  [layer(): jnp.transpose(windows, (2, 0, 3, 1, 4))]
    unnamed x12 -> x13, local copies, waits for them, and re-layouts: 2.06 us -> 2.46 us
  transfers between devices with their start and end apart: 4 -> 4, of which waited for: 2 -> 2; matrix products, arithmetic and copies ran while one was open for 16% -> 22% of each run, Pallas kernels for 5% -> 5%
where the time goes in v11:
time: 85.7 us; the launch traced here: 85.3 us
  blocking collectives  21.9 us (26%)
  local copies, waits for them, and re-layouts  17 us (20%)
  starting transfers between devices  16.8 us (20%)
  Pallas kernels  11.9 us (14%)
  waiting for transfers between devices  11.4 us (13%)
  other arithmetic  4.98 us (6%)
  matrix products  0.89 us (1%)
    all_to_all x1, blocking collectives, layer(): returned = lax.all_to_all(mixed, 'rot', 0, 0)  21.9 us
    all_to_all x1, waiting for transfers between devices, layer(): lax.all_to_all(windows, 'rot', 0, 0)  7.83 us
    pallas_call x1, Pallas kernels, group_mix(): pl.pallas_call(mixing_kernel, out_shape=jax.ShapeDtypeStruct((count, rows...  7.69 us
    all_to_all x1, starting transfers between devices, layer(): filters = lax.all_to_all(spread, 'rot', 0, 0)  6.93 us
    slice x4, local copies, waits for them, and re-layouts, circulant_bank(): pairs = jnp.concatenate([filters, jnp.roll(filters, 1, axis=0)], axis=-1)  4.3 us
    all_to_all x1, starting transfers between devices, layer(): lax.all_to_all(windows, 'rot', 0, 0)  4.26 us
    pallas_call x1, Pallas kernels, circulant_bank(): pl.pallas_call(bank_kernel, out_shape=jax.ShapeDtypeStruct((taps, count *...  4.2 us
    ppermute x1, starting transfers between devices, layer(): lax.ppermute(edges(raster[:, :2], coarse_own[:, 0]), 'space', [(j, i) for...  3.64 us
  transfers between devices with their start and end apart: 4, of which 2 were waited for; matrix products, arithmetic and copies ran while one was open for 22% of the time, Pallas kernels for 5%

profile of v11, /device:TPU:96, one launch (start us, length us, event | category | flops | bytes accessed | tf_op | source)
XLA Modules:
  0.0 85.3 jit_solution(354534383768846669)
XLA Ops:
  0.0 0.0 copy-start.1
  0.0 0.0 copy-start.2
  0.0 1.8 %copy.36 = bf16[1,64,16,2,256]{4,1,3,2,0:T(8,128)(2,1)S(1)} copy(bf16[1,64,16,2,256]{4,3,2,1,0:T(2,128)(2,1)} %param.7) | data formatting | bytes 2097152 | tf_op args[1]
  1.9 0.0 copy-done.1
  1.9 1.9 %collective-permute-start = (bf16[72,2,256]{2,0,1:T(8,128)(2,1)S(1)}, bf16[72,2,256]{2,0,1:T(8,128)(2,1)S(1)}, u32[]{:S(2)}, u32[]{:S(2)}) collective-permute-start(bf16[72,2,256]{2,0,1:T(8,128)(2,1)S(1)} %pad_maximum_fusion), channel_id=1, source_target_pairs={{0,1},{1,2},{2,3},{3,4},{4,5},{5,6},{6,7},{7,8},{8,9},{9,10},{10,1... | collective-permute-start | bytes 221192 | tf_op jit(solution)/shard_map/ppermute | solution.py:78
  3.9 3.6 %collective-permute-start.1 = (bf16[72,2,256]{2,0,1:T(8,128)(2,1)S(1)}, bf16[72,2,256]{2,0,1:T(8,128)(2,1)S(1)}, u32[]{:S(2)}, u32[]{:S(2)}) collective-permute-start(bf16[72,2,256]{2,0,1:T(8,128)(2,1)S(1)} %pad_maximum_fusion.1), channel_id=1, source_target_pairs={{1,0},{2,1},{3,2},{4,3},{5,4},{6,5},{7,6},{8,7},{9,8},{10,9},{11,1... | collective-permute-start | bytes 221192 | tf_op jit(solution)/shard_map/ppermute | solution.py:79
  7.5 0.0 copy-done
  7.6 0.2 reshape_squeeze.3
  7.7 1.1 %broadcast_in_dim.20 = bf16[8,2,18432]{2,1,0:T(2,128)(2,1)} broadcast(bf16[2,18432]{1,0:T(2,128)(2,1)S(1)} %reshape_squeeze.3), dimensions={1,2} | broadcast | bytes 663552 | tf_op jit(solution)/shard_map/broadcast_in_dim | solution.py:113
  8.9 6.9 %all-to-all-start = ((bf16[8,2,18432]{2,1,0:T(2,128)(2,1)}), bf16[8,2,18432]{2,1,0:T(2,128)(2,1)S(1)}, u32[]{:S(2)}, u32[]{:S(2)}) async-start(bf16[8,2,18432]{2,1,0:T(2,128)(2,1)} %broadcast_in_dim.20), calls=%async_computation | async-start | bytes 1179648 | tf_op jit(solution)/shard_map/all_to_all | solution.py:114
  15.8 0.1 copy.18
  15.8 0.0 copy-done.2
  15.9 0.0 collective-permute-done
  16.0 0.0 collective-permute-done.1
  16.1 0.1 fusion.9
  16.2 0.1 fusion.16
  16.3 0.1 fusion.5
  16.4 0.3 fusion.13
  16.7 0.1 fusion.17
  16.8 0.1 concatenate.44
  16.9 0.2 convolution_bitcast_fusion.2
  17.1 0.1 concatenate.49
  17.2 0.2 convolution_bitcast_fusion.1
  17.4 0.0 copy-start.3
  17.4 0.4 concatenate.47
  17.8 0.5 convolution_bitcast_fusion
  18.3 0.0 copy-done.3
  18.3 0.6 fusion.3
  18.9 0.2 fusion.12
  19.2 0.8 copy.28
  20.1 0.5 copy.34
  20.6 1.1 %maximum_bitcast_fusion = bf16[2,4,64,6,256]{4,3,2,1,0:T(8,128)(2,1)S(1)} fusion(bf16[4,2,2,64,256]{4,1,3,0,2:T(2,128)(2,1)S(1)} %copy.34, bf16[4,4,2,64,256]{4,1,3,0,2:T(4,128)(2,1)S(1)} %copy.28), kind=kLoop, calls=%fused_computation.5 | loop fusion | flops 3145728 | bytes 3145728 | tf_op jit(solution)/shard_map/transpose | solution.py:109
  21.7 2.6 %reshape.70 = bf16[8,64,1536]{2,1,0:T(8,128)(2,1)} reshape(bf16[2,4,64,6,256]{4,3,2,1,0:T(8,128)(2,1)S(1)} %maximum_bitcast_fusion) | data formatting | bytes 3145728 | tf_op jit(solution)/shard_map/reshape | solution.py:109
  24.3 3.6 %all-to-all-done = bf16[8,2,18432]{2,1,0:T(2,128)(2,1)S(1)} async-done(((bf16[8,2,18432]{2,1,0:T(2,128)(2,1)}), bf16[8,2,18432]{2,1,0:T(2,128)(2,1)S(1)}, u32[]{:S(2)}, u32[]{:S(2)}) %all-to-all-start) | async-done | bytes 589856 | tf_op jit(solution)/shard_map/all_to_all | solution.py:114
  27.9 4.3 %all-to-all-start.1 = ((bf16[8,64,1536]{2,1,0:T(8,128)(2,1)}), bf16[8,64,1536]{2,1,0:T(8,128)(2,1)S(1)}, u32[]{:S(2)}, u32[]{:S(2)}) async-start(bf16[8,64,1536]{2,1,0:T(8,128)(2,1)} %reshape.70), calls=%async_computation.1 | async-start | bytes 3145728 | tf_op jit(solution)/shard_map/all_to_all | solution.py:110
  32.2 0.0 copy-done.4
  32.2 0.2 broadcast_in_dim_tile.4.bias_ref
  32.4 1.1 %slice.187 = bf16[7,2,18432]{2,1,0:T(2,128)(2,1)} slice(bf16[8,2,18432]{2,1,0:T(2,128)(2,1)S(1)} %all-to-all-done), slice={[0:7], [0:2], [0:18432]} | slice | bytes 1032192 | tf_op jit(solution)/shard_map/jit(_roll_static)/slice | solution.py:20
  33.6 2.3 %slice.143 = bf16[7,9,64,64]{3,2,1,0:T(8,128)(2,1)S(1)} reshape(bf16[7,2,18432]{2,1,0:T(2,128)(2,1)} %slice.187) | data formatting | bytes 1032192 | tf_op jit(solution)/shard_map/jit(_roll_static)/slice | solution.py:20
  35.9 0.1 slice.186
  35.9 0.8 slice.141
  36.7 1.8 %reshape.60 = bf16[8,9,64,64]{3,2,1,0:T(8,128)(2,1)} reshape(bf16[8,2,18432]{2,1,0:T(2,128)(2,1)S(1)} %all-to-all-done) | data formatting | bytes 1179648 | tf_op jit(solution)/shard_map/reshape | solution.py:115
  38.5 3.0 %maximum_maximum_fusion.pairs_ref = bf16[8,9,64,128]{3,2,1,0:T(8,128)(2,1)} fusion(bf16[7,9,64,64]{3,2,1,0:T(8,128)(2,1)S(1)} %slice.143, bf16[1,9,64,64]{3,2,1,0:T(8,128)(2,1)} %slice.141, bf16[8,9,64,64]{3,2,1,0:T(8,128)(2,1)} %reshape.60), kind=kLoop, calls=%fused_computation.7 | loop fusion | flops 3538944 | bytes 2359296 | tf_op jit(solution)/shard_map/concatenate | solution.py:20
  41.6 4.2 %shard_map.64.bank_ref = bf16[9,512,512]{2,1,0:T(8,128)(2,1)} custom-call(bf16[8,9,64,128]{3,2,1,0:T(8,128)(2,1)} %maximum_maximum_fusion.pairs_ref), custom_call_target="tpu_custom_call" | custom-call | tf_op jit(solution)/shard_map/pallas_call | solution.py:21
  45.8 7.8 %all-to-all-done.1 = bf16[8,64,1536]{2,1,0:T(8,128)(2,1)S(1)} async-done(((bf16[8,64,1536]{2,1,0:T(8,128)(2,1)}), bf16[8,64,1536]{2,1,0:T(8,128)(2,1)S(1)}, u32[]{:S(2)}, u32[]{:S(2)}) %all-to-all-start.1) | async-done | bytes 1572896 | tf_op jit(solution)/shard_map/all_to_all | solution.py:110
  53.6 7.7 %shard_map.65 = bf16[8,4,64,256]{3,2,1,0:T(8,128)(2,1)S(1)} custom-call(bf16[9,512,512]{2,1,0:T(8,128)(2,1)} %shard_map.64.bank_ref, f32[512,1]{1,0:T(8,128)S(1)} %broadcast_in_dim_tile.4.bias_ref, bf16[512,1536]{1,0:T(8,128)(2,1)S(1)} %bitcast.63), custom_call_target="tpu_custom_call" | custom-call | tf_op jit(solution)/shard_map/pallas_call | solution.py:52
  61.3 21.9 %all_to_all.15 = bf16[8,4,64,256]{3,2,1,0:T(8,128)(2,1)S(1)} all-to-all(bf16[8,4,64,256]{3,2,1,0:T(8,128)(2,1)S(1)} %shard_map.65), channel_id=1, replica_groups=mesh['rot'=8,'space'=32] {'rot'}, dimensions={0} | all-to-all | bytes 2097152 | tf_op jit(solution)/shard_map/all_to_all | solution.py:119
  83.2 2.1 %copy.30 = bf16[64,4,4,2,256]{4,3,2,1,0:T(2,128)(2,1)} copy(bf16[64,4,4,2,256]{4,0,2,1,3:T(8,128)(2,1)S(1)} %bitcast.66) | data formatting | bytes 2097152 | tf_op jit(solution)/shard_map/transpose | solution.py:121
  (24 shorter events, 0.2 us)
Async XLA Ops:
  0.0 1.9 %copy-start.1 = (bf16[4,16,2,256]{3,2,1,0:T(2,128)(2,1)S(1)}, bf16[4,16,2,256]{3,2,1,0:T(2,128)(2,1)}, u32[]{:S(2)}) copy-start(bf16[4,16,2,256]{3,2,1,0:T(2,128)(2,1)} %param.6) | copy-start | bytes 196612
  0.0 7.5 %copy-start = (bf16[1,9,64,64]{3,2,1,0:T(8,128)(2,1)S(1)}, bf16[1,9,64,64]{3,2,1,0:T(8,128)(2,1)}, u32[]{:S(2)}) copy-start(bf16[1,9,64,64]{3,2,1,0:T(8,128)(2,1)} %param.10) | copy-start | bytes 221188
  0.0 15.8 %copy-start.2 = (bf16[1,9,64,4]{2,3,1,0:T(4,128)(2,1)S(1)}, bf16[1,9,64,4]{2,3,1,0:T(4,128)(2,1)}, u32[]{:S(2)}) copy-start(bf16[1,9,64,4]{2,3,1,0:T(4,128)(2,1)} %param.8) | copy-start | bytes 13828
  1.9 14.0 %collective-permute-start = (bf16[72,2,256]{2,0,1:T(8,128)(2,1)S(1)}, bf16[72,2,256]{2,0,1:T(8,128)(2,1)S(1)}, u32[]{:S(2)}, u32[]{:S(2)}) collective-permute-start(bf16[72,2,256]{2,0,1:T(8,128)(2,1)S(1)} %pad_maximum_fusion), channel_id=1, source_target_pairs={{0,1},{1,2},{2,3},{3,4},{4,5},{5,6},{6,7},{7,8},{8,9},{9,10},{10,1... | collective-permute-start | bytes 221192 | tf_op jit(solution)/shard_map/ppermute | solution.py:78
  3.9 12.1 %collective-permute-start.1 = (bf16[72,2,256]{2,0,1:T(8,128)(2,1)S(1)}, bf16[72,2,256]{2,0,1:T(8,128)(2,1)S(1)}, u32[]{:S(2)}, u32[]{:S(2)}) collective-permute-start(bf16[72,2,256]{2,0,1:T(8,128)(2,1)S(1)} %pad_maximum_fusion.1), channel_id=1, source_target_pairs={{1,0},{2,1},{3,2},{4,3},{5,4},{6,5},{7,6},{8,7},{9,8},{10,9},{11,1... | collective-permute-start | bytes 221192 | tf_op jit(solution)/shard_map/ppermute | solution.py:79
  8.9 19.1 %all-to-all-start = ((bf16[8,2,18432]{2,1,0:T(2,128)(2,1)}), bf16[8,2,18432]{2,1,0:T(2,128)(2,1)S(1)}, u32[]{:S(2)}, u32[]{:S(2)}) async-start(bf16[8,2,18432]{2,1,0:T(2,128)(2,1)} %broadcast_in_dim.20), calls=%async_computation | async-start | bytes 1179648 | tf_op jit(solution)/shard_map/all_to_all | solution.py:114
  17.4 0.9 %copy-start.3 = (f32[64]{0:T(128)S(1)}, f32[64]{0:T(128)}, u32[]{:S(2)}) copy-start(f32[64]{0:T(128)} %param.9) | copy-start | bytes 772
  24.3 7.9 %copy-start.4 = (f32[64]{0:T(128)S(1)}, f32[64]{0:T(128)}, u32[]{:S(2)}) copy-start(f32[64]{0:T(128)} %param.11) | copy-start | bytes 772
  27.9 25.7 %all-to-all-start.1 = ((bf16[8,64,1536]{2,1,0:T(8,128)(2,1)}), bf16[8,64,1536]{2,1,0:T(8,128)(2,1)S(1)}, u32[]{:S(2)}, u32[]{:S(2)}) async-start(bf16[8,64,1536]{2,1,0:T(8,128)(2,1)} %reshape.70), calls=%async_computation.1 | async-start | bytes 3145728 | tf_op jit(solution)/shard_map/all_to_all | solution.py:110
